TPU v7x, 512 devices: a whole 4x8x8 slice. The times are simulated.
512 devices in a mesh: row: 32 (over y_lo, z), col: 16 (over y_hi, x, core).
Axes of the slice: x: 4, y: 8 (y_hi: 2, y_lo: 4; y = y_hi * 4 + y_lo), z: 8, core: 2. Of those that a mesh axis runs over, the one named last changes fastest.
Arguments:
- upper: float32 [8192, 8192], P('row', 'col'), may hold values from -0.125 to 0.125
- occupied: int32 [64, 64], P('row', 'col'), may hold values 0 or 1
- tile_molecules: int32 [64], replicated, may hold values from 2 to 5
Outputs:
- square_part: float32 [8192, 8192], P('row', 'col')
Inputs may be any that keep to these rules, and one draw needn't show every extreme that they name: `occupied`: only entries with row below column are read.
All inputs are finite; a program needn't handle non-finite values. No bound on the sum of `occupied` on one device may be relied on, other than what follows from the above.
Results may differ from a plain program's by a relative error of at most 0.0003.
Values sent between devices are 32-bit elements; how exact they have to be, the bound alone decides.
No kernel may reach another device: no remote copies, remote signals or barrier semaphores. Data moves between devices by JAX's collectives and lax.ppermute only.
A program may use at most 64 MiB of HBM per device.

v0:
```python
import jax
import jax.numpy as jnp
from jax import lax
from jax.sharding import PartitionSpec as P

BASIS = 23
TILE = 128
TR = 2
STEPS = 14


def from_behind(value, axis, by):
    length = lax.axis_size(axis)
    return lax.ppermute(value, axis, [(i, (i + by) % length) for i in range(length)])


def move_cols(values, offset):
    return from_behind(values, "col", offset)


def move_rows(values, offset):
    return from_behind(values, "row", offset)


def trade_cols(values):
    return lax.all_to_all(values, "col", split_axis=0, concat_axis=1, tiled=True)


def trade_rows(values):
    return lax.all_to_all(values, "row", split_axis=0, concat_axis=1, tiled=True)


def step_up(window, height):
    return jnp.concatenate([window[:, height:], move_cols(window[:, :height], -1)], axis=1)


def multiply(window, column_block, height):
    return jnp.dot(
        window[:, :height],
        column_block,
        precision=lax.Precision.HIGHEST,
        preferred_element_type=jnp.float32,
    )


def align_left(window, amount, height, col_count):
    window = jnp.where(amount & 1 == 1, step_up(window, height), window)
    for bit in range(1, col_count.bit_length()):
        window = jnp.where(amount >> bit & 1 == 1, move_cols(window, -(1 << bit - 1)), window)
    return window


def align_right(column_block, amount, row_count):
    for bit in range(row_count.bit_length() - 1):
        column_block = jnp.where(
            amount >> bit & 1 == 1, move_rows(column_block, -(1 << bit)), column_block
        )
    return column_block


def body(upper, occupied, tile_molecules):
    row_id = lax.axis_index("row")
    col_id = lax.axis_index("col")
    row_count = lax.axis_size("row")
    col_count = lax.axis_size("col")
    height = upper.shape[0]
    width = upper.shape[1]
    piece = height // col_count
    row_tiles = row_id * TR + jnp.arange(TR, dtype=jnp.int32)
    col_tiles = col_id * (2 * TR) + jnp.arange(2 * TR, dtype=jnp.int32)
    factor = jnp.where(
        row_tiles[:, None] < col_tiles[None, :],
        occupied.astype(jnp.float32),
        jnp.where(row_tiles[:, None] == col_tiles[None, :], 0.5, 0.0),
    )
    half_tri = (upper.reshape(TR, TILE, 2 * TR, TILE) * factor[:, None, :, None]).reshape(
        height, width
    )
    sectioned = jnp.transpose(half_tri.reshape(height, 2, col_count, piece), (2, 1, 3, 0))[:, None]
    first = trade_cols(sectioned)
    second = trade_rows(first.reshape(row_count, 1, piece, height))
    third = trade_cols(second.reshape(col_count, 1, 2, piece, height))
    mirrored = jnp.transpose(third.reshape(col_count, 2, piece, height), (0, 2, 1, 3)).reshape(
        height, width
    )
    mol_rows = lax.dynamic_slice_in_dim(tile_molecules, row_id * TR, TR)
    mol_cols = lax.dynamic_slice_in_dim(tile_molecules, col_id * (2 * TR), 2 * TR)
    offsets = jnp.arange(TILE, dtype=jnp.int32)
    live_rows = (offsets[None, :] < BASIS * mol_rows[:, None]).astype(jnp.float32).reshape(height)
    live_cols = (offsets[None, :] < BASIS * mol_cols[:, None]).astype(jnp.float32).reshape(width)
    density = (half_tri + mirrored) * live_rows[:, None] * live_cols[None, :]
    left_state = align_left(density, row_id, height, col_count)
    right_state = align_right(density, 2 * col_id % row_count, row_count)
    start = multiply(left_state, right_state, height)

    def advance(index, carry):
        window, column_block, total = carry
        window = step_up(window, height)
        column_block = move_rows(column_block, -1)
        return (window, column_block, total + multiply(window, column_block, height))

    result = lax.fori_loop(0, STEPS - 1, advance, (left_state, right_state, start))
    return result[2]


def solution(mesh):
    placed = (P("row", "col"), P("row", "col"), P())
    return jax.shard_map(
        body, mesh=mesh, in_specs=placed, out_specs=P("row", "col"), check_vma=False
    )
```

profile of v0, /device:TPU:23, one launch (start us, length us, event | category | flops | bytes accessed | tf_op | source)
XLA Modules:
  0.0 529.2 jit_solution(13855718673739967946)
XLA Ops:
  2.3 26.7 %all_to_all.12 = f32[16,1,2,16,256]{4,3,2,1,0:T(8,128)S(1)} all-to-all(f32[16,1,2,16,256]{4,3,2,1,0:T(8,128)S(1)} %copy.13), channel_id=1, replica_groups=mesh['row'=32,'col'=16] {'col'}, dimensions={0} | all-to-all | bytes 1048576 | tf_op jit(solution)/shard_map/all_to_all | solution.py:26
  29.1 29.0 %all_to_all.13 = f32[32,1,16,256]{3,2,1,0:T(8,128)} all-to-all(f32[32,1,16,256]{3,2,1,0:T(8,128)S(1)} %bitcast.41), channel_id=1, replica_groups=mesh['row'=32,'col'=16] {'row'}, dimensions={0} | all-to-all | bytes 1048576 | tf_op jit(solution)/shard_map/all_to_all | solution.py:30
  64.5 17.5 %all-to-all-done.2 = f32[16,1,2,16,256]{4,3,2,1,0:T(8,128)S(1)} async-done(((f32[16,1,2,16,256]{4,3,2,1,0:T(8,128)}), f32[16,1,2,16,256]{4,3,2,1,0:T(8,128)S(1)}, u32[]{:S(2)}, u32[]{:S(2)}) %all-to-all-start.2) | async-done | bytes 524320 | tf_op jit(solution)/shard_map/all_to_all | solution.py:26
  88.7 22.9 %collective-permute-done.2 = f32[256,256]{1,0:T(8,128)S(1)} collective-permute-done((f32[256,256]{1,0:T(8,128)S(1)}, f32[256,256]{1,0:T(8,128)S(1)}, u32[]{:S(2)}, u32[]{:S(2)}) %collective-permute-start.2) | collective-permute-done | bytes 262176 | tf_op jit(solution)/shard_map/ppermute | solution.py:14
  115.6 13.2 %collective-permute-done.8 = f32[256,512]{1,0:T(8,128)S(1)} collective-permute-done((f32[256,512]{1,0:T(8,128)S(1)}, f32[256,512]{1,0:T(8,128)S(1)}, u32[]{:S(2)}, u32[]{:S(2)}) %collective-permute-start.8) | collective-permute-done | bytes 524320 | tf_op jit(solution)/shard_map/ppermute | solution.py:14
  132.1 9.8 %collective-permute-done.3 = f32[256,512]{1,0:T(8,128)S(1)} collective-permute-done((f32[256,512]{1,0:T(8,128)S(1)}, f32[256,512]{1,0:T(8,128)S(1)}, u32[]{:S(2)}, u32[]{:S(2)}) %collective-permute-start.3) | collective-permute-done | bytes 524320 | tf_op jit(solution)/shard_map/ppermute | solution.py:14
  143.9 9.1 %collective-permute-done.9 = f32[256,512]{1,0:T(8,128)S(1)} collective-permute-done((f32[256,512]{1,0:T(8,128)S(1)}, f32[256,512]{1,0:T(8,128)S(1)}, u32[]{:S(2)}, u32[]{:S(2)}) %collective-permute-start.9) | collective-permute-done | bytes 524320 | tf_op jit(solution)/shard_map/ppermute | solution.py:14
  153.1 9.0 %collective-permute-start.10 = (f32[256,512]{1,0:T(8,128)S(1)}, f32[256,512]{1,0:T(8,128)S(1)}, u32[]{:S(2)}, u32[]{:S(2)}) collective-permute-start(f32[256,512]{1,0:T(8,128)S(1)} %broadcast_select_fusion.2), channel_id=1, source_target_pairs={{0,384},{16,400},{32,416},{48,432},{64,448},{80,464},{96,480},{112... | collective-permute-start | bytes 1572872 | tf_op jit(solution)/shard_map/ppermute | solution.py:14
  164.1 8.7 %collective-permute-done.10 = f32[256,512]{1,0:T(8,128)S(1)} collective-permute-done((f32[256,512]{1,0:T(8,128)S(1)}, f32[256,512]{1,0:T(8,128)S(1)}, u32[]{:S(2)}, u32[]{:S(2)}) %collective-permute-start.10) | collective-permute-done | bytes 524320 | tf_op jit(solution)/shard_map/ppermute | solution.py:14
  177.1 19.0 %collective-permute-done.5 = f32[256,512]{1,0:T(8,128)S(1)} collective-permute-done((f32[256,512]{1,0:T(8,128)S(1)}, f32[256,512]{1,0:T(8,128)S(1)}, u32[]{:S(2)}, u32[]{:S(2)}) %collective-permute-start.5) | collective-permute-done | bytes 524320 | tf_op jit(solution)/shard_map/ppermute | solution.py:14
  196.2 6.5 %collective-permute-start.6 = (f32[256,512]{1,0:T(8,128)S(1)}, f32[256,512]{1,0:T(8,128)S(1)}, u32[]{:S(2)}, u32[]{:S(2)}) collective-permute-start(f32[256,512]{1,0:T(8,128)S(1)} %broadcast_select_fusion.7), channel_id=1, source_target_pairs={{0,8},{1,9},{2,10},{3,11},{4,12},{5,13},{6,14},{7,15},{8,0},{9,1},... | collective-permute-start | bytes 1572872 | tf_op jit(solution)/shard_map/ppermute | solution.py:14
  204.1 22.3 %collective-permute-done.6 = f32[256,512]{1,0:T(8,128)S(1)} collective-permute-done((f32[256,512]{1,0:T(8,128)S(1)}, f32[256,512]{1,0:T(8,128)S(1)}, u32[]{:S(2)}, u32[]{:S(2)}) %collective-permute-start.6) | collective-permute-done | bytes 524320 | tf_op jit(solution)/shard_map/ppermute | solution.py:14
  227.2 301.2 %while.14 = (s32[]{:T(128)}, f32[256,512]{1,0:T(8,128)S(1)}, f32[256,512]{1,0:T(8,128)S(1)}, f32[256,512]{1,0:T(8,128)S(1)}, s32[]{:T(128)}) while((s32[]{:T(128)}, f32[256,512]{1,0:T(8,128)S(1)}, f32[256,512]{1,0:T(8,128)S(1)}, f32[256,512]{1,0:T(8,128)S(1)}, s32[]{:T(128)}) %tuple.23), condition=%wide.region_1.2_spmd, body=%wide.region_0.1_spmd.sunk | while | flops 402915328 | bytes 8126605 | solution.py:102
  231.8 9.8 %collective-permute-done.1 = f32[256,512]{1,0:T(8,128)S(1)} collective-permute-done((f32[256,512]{1,0:T(8,128)S(1)}, f32[256,512]{1,0:T(8,128)S(1)}, u32[]{:S(2)}, u32[]{:S(2)}) %collective-permute-start.1) | collective-permute-done | bytes 524320 | tf_op jit(solution)/shard_map/while/body/eval_jaxpr/ppermute | solution.py:14
  242.3 49.3 %collective-permute-done = f32[256,256]{1,0:T(8,128)S(1)} collective-permute-done((f32[256,256]{1,0:T(8,128)S(1)}, f32[256,256]{1,0:T(8,128)S(1)}, u32[]{:S(2)}, u32[]{:S(2)}) %collective-permute-start) | collective-permute-done | bytes 262176 | tf_op jit(solution)/shard_map/while/body/eval_jaxpr/ppermute | solution.py:14
  295.6 6.0 %collective-permute-done.1 = f32[256,512]{1,0:T(8,128)S(1)} collective-permute-done((f32[256,512]{1,0:T(8,128)S(1)}, f32[256,512]{1,0:T(8,128)S(1)}, u32[]{:S(2)}, u32[]{:S(2)}) %collective-permute-start.1) | collective-permute-done | bytes 524320 | tf_op jit(solution)/shard_map/while/body/eval_jaxpr/ppermute | solution.py:14
  311.9 6.0 %collective-permute-done.1 = f32[256,512]{1,0:T(8,128)S(1)} collective-permute-done((f32[256,512]{1,0:T(8,128)S(1)}, f32[256,512]{1,0:T(8,128)S(1)}, u32[]{:S(2)}, u32[]{:S(2)}) %collective-permute-start.1) | collective-permute-done | bytes 524320 | tf_op jit(solution)/shard_map/while/body/eval_jaxpr/ppermute | solution.py:14
  318.7 8.5 %collective-permute-done = f32[256,256]{1,0:T(8,128)S(1)} collective-permute-done((f32[256,256]{1,0:T(8,128)S(1)}, f32[256,256]{1,0:T(8,128)S(1)}, u32[]{:S(2)}, u32[]{:S(2)}) %collective-permute-start) | collective-permute-done | bytes 262176 | tf_op jit(solution)/shard_map/while/body/eval_jaxpr/ppermute | solution.py:14
  331.2 6.0 %collective-permute-done.1 = f32[256,512]{1,0:T(8,128)S(1)} collective-permute-done((f32[256,512]{1,0:T(8,128)S(1)}, f32[256,512]{1,0:T(8,128)S(1)}, u32[]{:S(2)}, u32[]{:S(2)}) %collective-permute-start.1) | collective-permute-done | bytes 524320 | tf_op jit(solution)/shard_map/while/body/eval_jaxpr/ppermute | solution.py:14
  337.9 9.6 %collective-permute-done = f32[256,256]{1,0:T(8,128)S(1)} collective-permute-done((f32[256,256]{1,0:T(8,128)S(1)}, f32[256,256]{1,0:T(8,128)S(1)}, u32[]{:S(2)}, u32[]{:S(2)}) %collective-permute-start) | collective-permute-done | bytes 262176 | tf_op jit(solution)/shard_map/while/body/eval_jaxpr/ppermute | solution.py:14
  358.3 10.3 %collective-permute-done = f32[256,256]{1,0:T(8,128)S(1)} collective-permute-done((f32[256,256]{1,0:T(8,128)S(1)}, f32[256,256]{1,0:T(8,128)S(1)}, u32[]{:S(2)}, u32[]{:S(2)}) %collective-permute-start) | collective-permute-done | bytes 262176 | tf_op jit(solution)/shard_map/while/body/eval_jaxpr/ppermute | solution.py:14
  372.6 6.0 %collective-permute-done.1 = f32[256,512]{1,0:T(8,128)S(1)} collective-permute-done((f32[256,512]{1,0:T(8,128)S(1)}, f32[256,512]{1,0:T(8,128)S(1)}, u32[]{:S(2)}, u32[]{:S(2)}) %collective-permute-start.1) | collective-permute-done | bytes 524320 | tf_op jit(solution)/shard_map/while/body/eval_jaxpr/ppermute | solution.py:14
  379.4 18.0 %collective-permute-done = f32[256,256]{1,0:T(8,128)S(1)} collective-permute-done((f32[256,256]{1,0:T(8,128)S(1)}, f32[256,256]{1,0:T(8,128)S(1)}, u32[]{:S(2)}, u32[]{:S(2)}) %collective-permute-start) | collective-permute-done | bytes 262176 | tf_op jit(solution)/shard_map/while/body/eval_jaxpr/ppermute | solution.py:14
  408.1 10.2 %collective-permute-done = f32[256,256]{1,0:T(8,128)S(1)} collective-permute-done((f32[256,256]{1,0:T(8,128)S(1)}, f32[256,256]{1,0:T(8,128)S(1)}, u32[]{:S(2)}, u32[]{:S(2)}) %collective-permute-start) | collective-permute-done | bytes 262176 | tf_op jit(solution)/shard_map/while/body/eval_jaxpr/ppermute | solution.py:14
  422.3 6.0 %collective-permute-done.1 = f32[256,512]{1,0:T(8,128)S(1)} collective-permute-done((f32[256,512]{1,0:T(8,128)S(1)}, f32[256,512]{1,0:T(8,128)S(1)}, u32[]{:S(2)}, u32[]{:S(2)}) %collective-permute-start.1) | collective-permute-done | bytes 524320 | tf_op jit(solution)/shard_map/while/body/eval_jaxpr/ppermute | solution.py:14
  429.1 10.4 %collective-permute-done = f32[256,256]{1,0:T(8,128)S(1)} collective-permute-done((f32[256,256]{1,0:T(8,128)S(1)}, f32[256,256]{1,0:T(8,128)S(1)}, u32[]{:S(2)}, u32[]{:S(2)}) %collective-permute-start) | collective-permute-done | bytes 262176 | tf_op jit(solution)/shard_map/while/body/eval_jaxpr/ppermute | solution.py:14
  443.5 6.0 %collective-permute-done.1 = f32[256,512]{1,0:T(8,128)S(1)} collective-permute-done((f32[256,512]{1,0:T(8,128)S(1)}, f32[256,512]{1,0:T(8,128)S(1)}, u32[]{:S(2)}, u32[]{:S(2)}) %collective-permute-start.1) | collective-permute-done | bytes 524320 | tf_op jit(solution)/shard_map/while/body/eval_jaxpr/ppermute | solution.py:14
  450.3 8.4 %collective-permute-done = f32[256,256]{1,0:T(8,128)S(1)} collective-permute-done((f32[256,256]{1,0:T(8,128)S(1)}, f32[256,256]{1,0:T(8,128)S(1)}, u32[]{:S(2)}, u32[]{:S(2)}) %collective-permute-start) | collective-permute-done | bytes 262176 | tf_op jit(solution)/shard_map/while/body/eval_jaxpr/ppermute | solution.py:14
  469.4 7.4 %collective-permute-done = f32[256,256]{1,0:T(8,128)S(1)} collective-permute-done((f32[256,256]{1,0:T(8,128)S(1)}, f32[256,256]{1,0:T(8,128)S(1)}, u32[]{:S(2)}, u32[]{:S(2)}) %collective-permute-start) | collective-permute-done | bytes 262176 | tf_op jit(solution)/shard_map/while/body/eval_jaxpr/ppermute | solution.py:14
  480.8 6.0 %collective-permute-done.1 = f32[256,512]{1,0:T(8,128)S(1)} collective-permute-done((f32[256,512]{1,0:T(8,128)S(1)}, f32[256,512]{1,0:T(8,128)S(1)}, u32[]{:S(2)}, u32[]{:S(2)}) %collective-permute-start.1) | collective-permute-done | bytes 524320 | tf_op jit(solution)/shard_map/while/body/eval_jaxpr/ppermute | solution.py:14
  487.6 9.2 %collective-permute-done = f32[256,256]{1,0:T(8,128)S(1)} collective-permute-done((f32[256,256]{1,0:T(8,128)S(1)}, f32[256,256]{1,0:T(8,128)S(1)}, u32[]{:S(2)}, u32[]{:S(2)}) %collective-permute-start) | collective-permute-done | bytes 262176 | tf_op jit(solution)/shard_map/while/body/eval_jaxpr/ppermute | solution.py:14
  500.8 6.0 %collective-permute-done.1 = f32[256,512]{1,0:T(8,128)S(1)} collective-permute-done((f32[256,512]{1,0:T(8,128)S(1)}, f32[256,512]{1,0:T(8,128)S(1)}, u32[]{:S(2)}, u32[]{:S(2)}) %collective-permute-start.1) | collective-permute-done | bytes 524320 | tf_op jit(solution)/shard_map/while/body/eval_jaxpr/ppermute | solution.py:14
  (133 shorter events, 134.8 us)
Async XLA Ops:
  58.1 23.9 %all-to-all-start.2 = ((f32[16,1,2,16,256]{4,3,2,1,0:T(8,128)}), f32[16,1,2,16,256]{4,3,2,1,0:T(8,128)S(1)}, u32[]{:S(2)}, u32[]{:S(2)}) async-start(f32[16,1,2,16,256]{4,3,2,1,0:T(8,128)} %bitcast.6), calls=%async_computation.2 | async-start | bytes 1048576 | tf_op jit(solution)/shard_map/all_to_all | solution.py:26
  83.6 27.9 %collective-permute-start.7 = (f32[256,512]{1,0:T(8,128)S(1)}, f32[256,512]{1,0:T(8,128)S(1)}, u32[]{:S(2)}, u32[]{:S(2)}) collective-permute-start(f32[256,512]{1,0:T(8,128)S(1)} %fusion.3), channel_id=1, source_target_pairs={{0,496},{16,0},{32,16},{48,32},{64,48},{80,64},{96,80},{112,96},{1... | collective-permute-start | bytes 1572872 | tf_op jit(solution)/shard_map/ppermute | solution.py:14
  86.2 25.3 %collective-permute-start.2 = (f32[256,256]{1,0:T(8,128)S(1)}, f32[256,256]{1,0:T(8,128)S(1)}, u32[]{:S(2)}, u32[]{:S(2)}) collective-permute-start(f32[256,256]{1,0:T(8,128)S(1)} %get-tuple-element.41), channel_id=1, source_target_pairs={{0,15},{1,0},{2,1},{3,2},{4,3},{5,4},{6,5},{7,6},{8,7},{9,8},{10,9... | collective-permute-start | bytes 786440 | tf_op jit(solution)/shard_map/ppermute | solution.py:14
  111.7 17.1 %collective-permute-start.8 = (f32[256,512]{1,0:T(8,128)S(1)}, f32[256,512]{1,0:T(8,128)S(1)}, u32[]{:S(2)}, u32[]{:S(2)}) collective-permute-start(f32[256,512]{1,0:T(8,128)S(1)} %get-tuple-element.38), channel_id=1, source_target_pairs={{0,480},{16,496},{32,0},{48,16},{64,32},{80,48},{96,64},{112,80},{... | collective-permute-start | bytes 1572872 | tf_op jit(solution)/shard_map/ppermute | solution.py:14
  113.6 28.3 %collective-permute-start.3 = (f32[256,512]{1,0:T(8,128)S(1)}, f32[256,512]{1,0:T(8,128)S(1)}, u32[]{:S(2)}, u32[]{:S(2)}) collective-permute-start(f32[256,512]{1,0:T(8,128)S(1)} %get-tuple-element.39), channel_id=1, source_target_pairs={{0,15},{1,0},{2,1},{3,2},{4,3},{5,4},{6,5},{7,6},{8,7},{9,8},{10,9... | collective-permute-start | bytes 1572872 | tf_op jit(solution)/shard_map/ppermute | solution.py:14
  128.9 24.1 %collective-permute-start.9 = (f32[256,512]{1,0:T(8,128)S(1)}, f32[256,512]{1,0:T(8,128)S(1)}, u32[]{:S(2)}, u32[]{:S(2)}) collective-permute-start(f32[256,512]{1,0:T(8,128)S(1)} %broadcast_select_fusion.1), channel_id=1, source_target_pairs={{0,448},{16,464},{32,480},{48,496},{64,0},{80,16},{96,32},{112,48}... | collective-permute-start | bytes 1572872 | tf_op jit(solution)/shard_map/ppermute | solution.py:14
  142.0 20.1 %collective-permute-start.4 = (f32[256,512]{1,0:T(8,128)S(1)}, f32[256,512]{1,0:T(8,128)S(1)}, u32[]{:S(2)}, u32[]{:S(2)}) collective-permute-start(f32[256,512]{1,0:T(8,128)S(1)} %broadcast_select_fusion.5), channel_id=1, source_target_pairs={{0,14},{1,15},{2,0},{3,1},{4,2},{5,3},{6,4},{7,5},{8,6},{9,7},{10,... | collective-permute-start | bytes 1572872 | tf_op jit(solution)/shard_map/ppermute | solution.py:14
  153.1 19.8 %collective-permute-start.10 = (f32[256,512]{1,0:T(8,128)S(1)}, f32[256,512]{1,0:T(8,128)S(1)}, u32[]{:S(2)}, u32[]{:S(2)}) collective-permute-start(f32[256,512]{1,0:T(8,128)S(1)} %broadcast_select_fusion.2), channel_id=1, source_target_pairs={{0,384},{16,400},{32,416},{48,432},{64,448},{80,464},{96,480},{112... | collective-permute-start | bytes 1572872 | tf_op jit(solution)/shard_map/ppermute | solution.py:14
  162.2 33.9 %collective-permute-start.5 = (f32[256,512]{1,0:T(8,128)S(1)}, f32[256,512]{1,0:T(8,128)S(1)}, u32[]{:S(2)}, u32[]{:S(2)}) collective-permute-start(f32[256,512]{1,0:T(8,128)S(1)} %broadcast_select_fusion.6), channel_id=1, source_target_pairs={{0,12},{1,13},{2,14},{3,15},{4,0},{5,1},{6,2},{7,3},{8,4},{9,5},{1... | collective-permute-start | bytes 1572872 | tf_op jit(solution)/shard_map/ppermute | solution.py:14
  172.9 31.1 %collective-permute-start.11 = (f32[256,512]{1,0:T(8,128)S(1)}, f32[256,512]{1,0:T(8,128)S(1)}, u32[]{:S(2)}, u32[]{:S(2)}) collective-permute-start(f32[256,512]{1,0:T(8,128)S(1)} %broadcast_select_fusion.3), channel_id=1, source_target_pairs={{0,256},{16,272},{32,288},{48,304},{64,320},{80,336},{96,352},{112... | collective-permute-start | bytes 1572872 | tf_op jit(solution)/shard_map/ppermute | solution.py:14
  196.2 30.3 %collective-permute-start.6 = (f32[256,512]{1,0:T(8,128)S(1)}, f32[256,512]{1,0:T(8,128)S(1)}, u32[]{:S(2)}, u32[]{:S(2)}) collective-permute-start(f32[256,512]{1,0:T(8,128)S(1)} %broadcast_select_fusion.7), channel_id=1, source_target_pairs={{0,8},{1,9},{2,10},{3,11},{4,12},{5,13},{6,14},{7,15},{8,0},{9,1},... | collective-permute-start | bytes 1572872 | tf_op jit(solution)/shard_map/ppermute | solution.py:14
  227.2 14.4 %collective-permute-start.1 = (f32[256,512]{1,0:T(8,128)S(1)}, f32[256,512]{1,0:T(8,128)S(1)}, u32[]{:S(2)}, u32[]{:S(2)}) collective-permute-start(f32[256,512]{1,0:T(8,128)S(1)} %get-tuple-element.78), channel_id=1, source_target_pairs={{0,496},{16,0},{32,16},{48,32},{64,48},{80,64},{96,80},{112,96},{1... | collective-permute-start | bytes 1572872 | tf_op jit(solution)/shard_map/while/body/eval_jaxpr/ppermute | solution.py:14
  229.2 62.5 %collective-permute-start = (f32[256,256]{1,0:T(8,128)S(1)}, f32[256,256]{1,0:T(8,128)S(1)}, u32[]{:S(2)}, u32[]{:S(2)}) collective-permute-start(f32[256,256]{1,0:T(8,128)S(1)} %get-tuple-element.69), channel_id=1, source_target_pairs={{0,15},{1,0},{2,1},{3,2},{4,3},{5,4},{6,5},{7,6},{8,7},{9,8},{10,9... | collective-permute-start | bytes 786440 | tf_op jit(solution)/shard_map/while/body/eval_jaxpr/ppermute | solution.py:14
  291.7 9.9 %collective-permute-start.1 = (f32[256,512]{1,0:T(8,128)S(1)}, f32[256,512]{1,0:T(8,128)S(1)}, u32[]{:S(2)}, u32[]{:S(2)}) collective-permute-start(f32[256,512]{1,0:T(8,128)S(1)} %get-tuple-element.78), channel_id=1, source_target_pairs={{0,496},{16,0},{32,16},{48,32},{64,48},{80,64},{96,80},{112,96},{1... | collective-permute-start | bytes 1572872 | tf_op jit(solution)/shard_map/while/body/eval_jaxpr/ppermute | solution.py:14
  293.7 14.2 %collective-permute-start = (f32[256,256]{1,0:T(8,128)S(1)}, f32[256,256]{1,0:T(8,128)S(1)}, u32[]{:S(2)}, u32[]{:S(2)}) collective-permute-start(f32[256,256]{1,0:T(8,128)S(1)} %get-tuple-element.69), channel_id=1, source_target_pairs={{0,15},{1,0},{2,1},{3,2},{4,3},{5,4},{6,5},{7,6},{8,7},{9,8},{10,9... | collective-permute-start | bytes 786440 | tf_op jit(solution)/shard_map/while/body/eval_jaxpr/ppermute | solution.py:14
  308.0 9.9 %collective-permute-start.1 = (f32[256,512]{1,0:T(8,128)S(1)}, f32[256,512]{1,0:T(8,128)S(1)}, u32[]{:S(2)}, u32[]{:S(2)}) collective-permute-start(f32[256,512]{1,0:T(8,128)S(1)} %get-tuple-element.78), channel_id=1, source_target_pairs={{0,496},{16,0},{32,16},{48,32},{64,48},{80,64},{96,80},{112,96},{1... | collective-permute-start | bytes 1572872 | tf_op jit(solution)/shard_map/while/body/eval_jaxpr/ppermute | solution.py:14
  310.0 17.2 %collective-permute-start = (f32[256,256]{1,0:T(8,128)S(1)}, f32[256,256]{1,0:T(8,128)S(1)}, u32[]{:S(2)}, u32[]{:S(2)}) collective-permute-start(f32[256,256]{1,0:T(8,128)S(1)} %get-tuple-element.69), channel_id=1, source_target_pairs={{0,15},{1,0},{2,1},{3,2},{4,3},{5,4},{6,5},{7,6},{8,7},{9,8},{10,9... | collective-permute-start | bytes 786440 | tf_op jit(solution)/shard_map/while/body/eval_jaxpr/ppermute | solution.py:14
  327.3 9.9 %collective-permute-start.1 = (f32[256,512]{1,0:T(8,128)S(1)}, f32[256,512]{1,0:T(8,128)S(1)}, u32[]{:S(2)}, u32[]{:S(2)}) collective-permute-start(f32[256,512]{1,0:T(8,128)S(1)} %get-tuple-element.78), channel_id=1, source_target_pairs={{0,496},{16,0},{32,16},{48,32},{64,48},{80,64},{96,80},{112,96},{1... | collective-permute-start | bytes 1572872 | tf_op jit(solution)/shard_map/while/body/eval_jaxpr/ppermute | solution.py:14
  329.2 18.3 %collective-permute-start = (f32[256,256]{1,0:T(8,128)S(1)}, f32[256,256]{1,0:T(8,128)S(1)}, u32[]{:S(2)}, u32[]{:S(2)}) collective-permute-start(f32[256,256]{1,0:T(8,128)S(1)} %get-tuple-element.69), channel_id=1, source_target_pairs={{0,15},{1,0},{2,1},{3,2},{4,3},{5,4},{6,5},{7,6},{8,7},{9,8},{10,9... | collective-permute-start | bytes 786440 | tf_op jit(solution)/shard_map/while/body/eval_jaxpr/ppermute | solution.py:14
  347.6 9.9 %collective-permute-start.1 = (f32[256,512]{1,0:T(8,128)S(1)}, f32[256,512]{1,0:T(8,128)S(1)}, u32[]{:S(2)}, u32[]{:S(2)}) collective-permute-start(f32[256,512]{1,0:T(8,128)S(1)} %get-tuple-element.78), channel_id=1, source_target_pairs={{0,496},{16,0},{32,16},{48,32},{64,48},{80,64},{96,80},{112,96},{1... | collective-permute-start | bytes 1572872 | tf_op jit(solution)/shard_map/while/body/eval_jaxpr/ppermute | solution.py:14
  349.6 19.0 %collective-permute-start = (f32[256,256]{1,0:T(8,128)S(1)}, f32[256,256]{1,0:T(8,128)S(1)}, u32[]{:S(2)}, u32[]{:S(2)}) collective-permute-start(f32[256,256]{1,0:T(8,128)S(1)} %get-tuple-element.69), channel_id=1, source_target_pairs={{0,15},{1,0},{2,1},{3,2},{4,3},{5,4},{6,5},{7,6},{8,7},{9,8},{10,9... | collective-permute-start | bytes 786440 | tf_op jit(solution)/shard_map/while/body/eval_jaxpr/ppermute | solution.py:14
  368.7 9.9 %collective-permute-start.1 = (f32[256,512]{1,0:T(8,128)S(1)}, f32[256,512]{1,0:T(8,128)S(1)}, u32[]{:S(2)}, u32[]{:S(2)}) collective-permute-start(f32[256,512]{1,0:T(8,128)S(1)} %get-tuple-element.78), channel_id=1, source_target_pairs={{0,496},{16,0},{32,16},{48,32},{64,48},{80,64},{96,80},{112,96},{1... | collective-permute-start | bytes 1572872 | tf_op jit(solution)/shard_map/while/body/eval_jaxpr/ppermute | solution.py:14
  370.7 26.7 %collective-permute-start = (f32[256,256]{1,0:T(8,128)S(1)}, f32[256,256]{1,0:T(8,128)S(1)}, u32[]{:S(2)}, u32[]{:S(2)}) collective-permute-start(f32[256,256]{1,0:T(8,128)S(1)} %get-tuple-element.69), channel_id=1, source_target_pairs={{0,15},{1,0},{2,1},{3,2},{4,3},{5,4},{6,5},{7,6},{8,7},{9,8},{10,9... | collective-permute-start | bytes 786440 | tf_op jit(solution)/shard_map/while/body/eval_jaxpr/ppermute | solution.py:14
  399.4 18.9 %collective-permute-start = (f32[256,256]{1,0:T(8,128)S(1)}, f32[256,256]{1,0:T(8,128)S(1)}, u32[]{:S(2)}, u32[]{:S(2)}) collective-permute-start(f32[256,256]{1,0:T(8,128)S(1)} %get-tuple-element.69), channel_id=1, source_target_pairs={{0,15},{1,0},{2,1},{3,2},{4,3},{5,4},{6,5},{7,6},{8,7},{9,8},{10,9... | collective-permute-start | bytes 786440 | tf_op jit(solution)/shard_map/while/body/eval_jaxpr/ppermute | solution.py:14
  418.4 9.9 %collective-permute-start.1 = (f32[256,512]{1,0:T(8,128)S(1)}, f32[256,512]{1,0:T(8,128)S(1)}, u32[]{:S(2)}, u32[]{:S(2)}) collective-permute-start(f32[256,512]{1,0:T(8,128)S(1)} %get-tuple-element.78), channel_id=1, source_target_pairs={{0,496},{16,0},{32,16},{48,32},{64,48},{80,64},{96,80},{112,96},{1... | collective-permute-start | bytes 1572872 | tf_op jit(solution)/shard_map/while/body/eval_jaxpr/ppermute | solution.py:14
  420.4 19.1 %collective-permute-start = (f32[256,256]{1,0:T(8,128)S(1)}, f32[256,256]{1,0:T(8,128)S(1)}, u32[]{:S(2)}, u32[]{:S(2)}) collective-permute-start(f32[256,256]{1,0:T(8,128)S(1)} %get-tuple-element.69), channel_id=1, source_target_pairs={{0,15},{1,0},{2,1},{3,2},{4,3},{5,4},{6,5},{7,6},{8,7},{9,8},{10,9... | collective-permute-start | bytes 786440 | tf_op jit(solution)/shard_map/while/body/eval_jaxpr/ppermute | solution.py:14
  439.6 9.9 %collective-permute-start.1 = (f32[256,512]{1,0:T(8,128)S(1)}, f32[256,512]{1,0:T(8,128)S(1)}, u32[]{:S(2)}, u32[]{:S(2)}) collective-permute-start(f32[256,512]{1,0:T(8,128)S(1)} %get-tuple-element.78), channel_id=1, source_target_pairs={{0,496},{16,0},{32,16},{48,32},{64,48},{80,64},{96,80},{112,96},{1... | collective-permute-start | bytes 1572872 | tf_op jit(solution)/shard_map/while/body/eval_jaxpr/ppermute | solution.py:14
  441.6 17.1 %collective-permute-start = (f32[256,256]{1,0:T(8,128)S(1)}, f32[256,256]{1,0:T(8,128)S(1)}, u32[]{:S(2)}, u32[]{:S(2)}) collective-permute-start(f32[256,256]{1,0:T(8,128)S(1)} %get-tuple-element.69), channel_id=1, source_target_pairs={{0,15},{1,0},{2,1},{3,2},{4,3},{5,4},{6,5},{7,6},{8,7},{9,8},{10,9... | collective-permute-start | bytes 786440 | tf_op jit(solution)/shard_map/while/body/eval_jaxpr/ppermute | solution.py:14
  460.7 16.1 %collective-permute-start = (f32[256,256]{1,0:T(8,128)S(1)}, f32[256,256]{1,0:T(8,128)S(1)}, u32[]{:S(2)}, u32[]{:S(2)}) collective-permute-start(f32[256,256]{1,0:T(8,128)S(1)} %get-tuple-element.69), channel_id=1, source_target_pairs={{0,15},{1,0},{2,1},{3,2},{4,3},{5,4},{6,5},{7,6},{8,7},{9,8},{10,9... | collective-permute-start | bytes 786440 | tf_op jit(solution)/shard_map/while/body/eval_jaxpr/ppermute | solution.py:14
  478.9 17.9 %collective-permute-start = (f32[256,256]{1,0:T(8,128)S(1)}, f32[256,256]{1,0:T(8,128)S(1)}, u32[]{:S(2)}, u32[]{:S(2)}) collective-permute-start(f32[256,256]{1,0:T(8,128)S(1)} %get-tuple-element.69), channel_id=1, source_target_pairs={{0,15},{1,0},{2,1},{3,2},{4,3},{5,4},{6,5},{7,6},{8,7},{9,8},{10,9... | collective-permute-start | bytes 786440 | tf_op jit(solution)/shard_map/while/body/eval_jaxpr/ppermute | solution.py:14
  498.9 13.7 %collective-permute-start = (f32[256,256]{1,0:T(8,128)S(1)}, f32[256,256]{1,0:T(8,128)S(1)}, u32[]{:S(2)}, u32[]{:S(2)}) collective-permute-start(f32[256,256]{1,0:T(8,128)S(1)} %get-tuple-element.69), channel_id=1, source_target_pairs={{0,15},{1,0},{2,1},{3,2},{4,3},{5,4},{6,5},{7,6},{8,7},{9,8},{10,9... | collective-permute-start | bytes 786440 | tf_op jit(solution)/shard_map/while/body/eval_jaxpr/ppermute | solution.py:14
  514.6 13.7 %collective-permute-start = (f32[256,256]{1,0:T(8,128)S(1)}, f32[256,256]{1,0:T(8,128)S(1)}, u32[]{:S(2)}, u32[]{:S(2)}) collective-permute-start(f32[256,256]{1,0:T(8,128)S(1)} %get-tuple-element.69), channel_id=1, source_target_pairs={{0,15},{1,0},{2,1},{3,2},{4,3},{5,4},{6,5},{7,6},{8,7},{9,8},{10,9... | collective-permute-start | bytes 786440 | tf_op jit(solution)/shard_map/while/body/eval_jaxpr/ppermute | solution.py:14
  (9 other events, 52.8 us)
where the time goes:
time: 531 us; the launch traced here: 529 us
  waiting for transfers between devices  363 us (68%)
  starting transfers between devices  91.7 us (17%)
  blocking collectives  55.7 us (10%)
  matrix products  9.49 us (2%)
  local copies, waits for them, and re-layouts  6.02 us (1%)
    ppermute x36, waiting for transfers between devices, from_behind(): lax.ppermute(value, axis, [(i, (i + by) % length) for i in range(length)])  346 us
    ppermute x36, starting transfers between devices, from_behind(): lax.ppermute(value, axis, [(i, (i + by) % length) for i in range(length)])  86.2 us
    all_to_all x1, blocking collectives, trade_rows(): lax.all_to_all(values, 'row', split_axis=0, concat_axis=1, tiled=True)  29 us
    all_to_all x1, blocking collectives, trade_cols(): lax.all_to_all(values, 'col', split_axis=0, concat_axis=1, tiled=True)  26.7 us
    all_to_all x1, waiting for transfers between devices, trade_cols(): lax.all_to_all(values, 'col', split_axis=0, concat_axis=1, tiled=True)  17.5 us
  transfers between devices with their start and end apart: 37, of which 35 were waited for; matrix products, arithmetic and copies ran while one was open for 2% of the time, Pallas kernels for 0%

commit v1 on v0

v1 whole, which is shorter than its diff:
```python
import jax
import jax.numpy as jnp
from jax import lax
from jax.sharding import PartitionSpec as P

BASIS = 23
TILE = 128
TR = 2
STEPS = 14

AXES = ("row", "col")


def send(value, pairs):
    return lax.ppermute(value, AXES, pairs)


def mirror_pairs(row_count, col_count, flip):
    pairs = []
    for r in range(row_count):
        for c in range(col_count):
            half = (r % 2) ^ flip
            target = (2 * c + half, r // 2)
            pairs.append((r * col_count + c, target[0] * col_count + target[1]))
    return pairs


def left_pairs(row_count, col_count, step):
    pairs = []
    for r in range(row_count):
        half = (r + step) % 2
        for c in range(col_count):
            target = ((2 * c + half - r - step) % row_count) // 2
            pairs.append((r * col_count + c, r * col_count + target))
    return pairs


def right_pairs(row_count, col_count, step):
    pairs = []
    for r in range(row_count):
        for c in range(col_count):
            target = (r - 2 * c - step) % row_count
            pairs.append((r * col_count + c, target * col_count + c))
    return pairs


def body(upper, occupied, tile_molecules):
    row_id = lax.axis_index("row")
    col_id = lax.axis_index("col")
    row_count = lax.axis_size("row")
    col_count = lax.axis_size("col")
    height = upper.shape[0]
    width = upper.shape[1]
    half_width = width // 2
    row_tiles = row_id * TR + jnp.arange(TR, dtype=jnp.int32)
    col_tiles = col_id * (2 * TR) + jnp.arange(2 * TR, dtype=jnp.int32)
    factor = jnp.where(
        row_tiles[:, None] < col_tiles[None, :],
        occupied.astype(jnp.float32),
        jnp.where(row_tiles[:, None] == col_tiles[None, :], 0.5, 0.0),
    )
    half_tri = (upper.reshape(TR, TILE, 2 * TR, TILE) * factor[:, None, :, None]).reshape(
        height, width
    )
    parity = row_id % 2
    halves = half_tri.reshape(height, 2, half_width)
    own_half = jnp.where(parity == 0, halves[:, 0], halves[:, 1]).T
    other_half = jnp.where(parity == 0, halves[:, 1], halves[:, 0]).T
    got_same = send(own_half, mirror_pairs(row_count, col_count, 0))
    got_other = send(other_half, mirror_pairs(row_count, col_count, 1))
    mirrored = jnp.where(
        parity == 0,
        jnp.concatenate([got_same, got_other], axis=1),
        jnp.concatenate([got_other, got_same], axis=1),
    )
    mol_rows = lax.dynamic_slice_in_dim(tile_molecules, row_id * TR, TR)
    mol_cols = lax.dynamic_slice_in_dim(tile_molecules, col_id * (2 * TR), 2 * TR)
    offsets = jnp.arange(TILE, dtype=jnp.int32)
    live_rows = (offsets[None, :] < BASIS * mol_rows[:, None]).astype(jnp.float32).reshape(height)
    live_cols = (offsets[None, :] < BASIS * mol_cols[:, None]).astype(jnp.float32).reshape(width)
    density = (half_tri + mirrored) * live_rows[:, None] * live_cols[None, :]
    dense_halves = density.reshape(height, 2, half_width)
    even_half = dense_halves[:, 0]
    odd_half = dense_halves[:, 1]
    total = None
    for step in range(STEPS):
        piece = jnp.where((row_id + step) % 2 == 0, even_half, odd_half)
        left = send(piece, left_pairs(row_count, col_count, step))
        right = send(density, right_pairs(row_count, col_count, step))
        term = jnp.dot(left, right, precision=lax.Precision.HIGHEST, preferred_element_type=jnp.float32)
        total = term if total is None else total + term
    return total


def solution(mesh):
    placed = (P("row", "col"), P("row", "col"), P())
    return jax.shard_map(
        body, mesh=mesh, in_specs=placed, out_specs=P("row", "col"), check_vma=False
    )
```

time: 531 us -> 477 us (0.90)
  the two profiles are of different devices: /device:TPU:23 before, /device:TPU:57 now
where the time goes in v1:
time: 477 us; the launch traced here: 476 us
  starting transfers between devices  286 us (60%)
  waiting for transfers between devices  176 us (37%)
  matrix products  10.1 us (2%)
    ppermute x30, starting transfers between devices, send(): return lax.ppermute(value, AXES, pairs)  286 us
    ppermute x30, waiting for transfers between devices, send(): return lax.ppermute(value, AXES, pairs)  176 us
    dot_general x14, matrix products, body(): jnp.dot(left, right, precision=lax.Precision.HIGHEST, preferred_element_t...  10.1 us
  transfers between devices with their start and end apart: 30, of which 6 were waited for; matrix products, arithmetic and copies ran while one was open for 2% of the time, Pallas kernels for 0%

profile of v1, /device:TPU:57, one launch (start us, length us, event | category | flops | bytes accessed | tf_op | source)
XLA Modules:
  0.0 476.3 jit_solution(9111586470979668323)
XLA Ops:
  2.4 9.6 %collective-permute-start = (f32[256,256]{1,0:T(8,128)S(1)}, f32[256,256]{1,0:T(8,128)S(1)}, u32[]{:S(2)}, u32[]{:S(2)}) collective-permute-start(f32[256,256]{1,0:T(8,128)S(1)} %get-tuple-element.19), channel_id=1, source_target_pairs={{0,0},{1,32},{2,64},{3,96},{4,128},{5,160},{6,192},{7,224},{8,256}... | collective-permute-start | bytes 786440 | tf_op jit(solution)/shard_map/ppermute | solution.py:15
  12.1 3.7 collective-permute-start.1
  17.1 4.1 collective-permute-done
  21.2 8.9 %collective-permute-done.1 = f32[256,256]{1,0:T(8,128)S(1)} collective-permute-done((f32[256,256]{1,0:T(8,128)S(1)}, f32[256,256]{1,0:T(8,128)S(1)}, u32[]{:S(2)}, u32[]{:S(2)}) %collective-permute-start.1) | collective-permute-done | bytes 262176 | tf_op jit(solution)/shard_map/ppermute | solution.py:15
  30.4 28.5 %collective-permute-start.5 = (f32[256,512]{1,0:T(8,128)S(1)}, f32[256,512]{1,0:T(8,128)S(1)}, u32[]{:S(2)}, u32[]{:S(2)}) collective-permute-start(f32[256,512]{1,0:T(8,128)S(1)} %fusion.14), channel_id=1, source_target_pairs={{0,496},{1,465},{2,434},{3,403},{4,372},{5,341},{6,310},{7,279},{8... | collective-permute-start | bytes 1572872 | tf_op jit(solution)/shard_map/ppermute | solution.py:15
  58.9 1.9 collective-permute-start.17
  60.8 2.2 collective-permute-start.19
  63.1 29.9 %collective-permute-start.4 = (f32[256,256]{0,1:T(8,128)S(1)}, f32[256,256]{0,1:T(8,128)S(1)}, u32[]{:S(2)}, u32[]{:S(2)}) collective-permute-start(f32[256,256]{0,1:T(8,128)S(1)} %get-tuple-element.11), channel_id=1, source_target_pairs={{0,0},{1,1},{2,2},{3,3},{4,4},{5,5},{6,6},{7,7},{8,8},{9,9},{10,10... | collective-permute-start | bytes 786440 | tf_op jit(solution)/shard_map/ppermute | solution.py:15
  93.1 3.2 collective-permute-start.16
  96.5 91.7 %collective-permute-done.4 = f32[256,256]{0,1:T(8,128)S(1)} collective-permute-done((f32[256,256]{0,1:T(8,128)S(1)}, f32[256,256]{0,1:T(8,128)S(1)}, u32[]{:S(2)}, u32[]{:S(2)}) %collective-permute-start.4) | collective-permute-done | bytes 262176 | tf_op jit(solution)/shard_map/ppermute | solution.py:15
  191.5 1.9 collective-permute-start.7
  194.8 1.9 collective-permute-start.9
  196.7 1.9 collective-permute-start.6
  199.3 13.4 %collective-permute-start.11 = (f32[256,512]{1,0:T(8,128)S(1)}, f32[256,512]{1,0:T(8,128)S(1)}, u32[]{:S(2)}, u32[]{:S(2)}) collective-permute-start(f32[256,512]{1,0:T(8,128)S(1)} %fusion.14), channel_id=1, source_target_pairs={{0,448},{1,417},{2,386},{3,355},{4,324},{5,293},{6,262},{7,231},{8... | collective-permute-start | bytes 1572872 | tf_op jit(solution)/shard_map/ppermute | solution.py:15
  212.7 1.9 collective-permute-done.21
  217.2 26.5 %collective-permute-start.13 = (f32[256,512]{1,0:T(8,128)S(1)}, f32[256,512]{1,0:T(8,128)S(1)}, u32[]{:S(2)}, u32[]{:S(2)}) collective-permute-start(f32[256,512]{1,0:T(8,128)S(1)} %fusion.14), channel_id=1, source_target_pairs={{0,432},{1,401},{2,370},{3,339},{4,308},{5,277},{6,246},{7,215},{8... | collective-permute-start | bytes 1572872 | tf_op jit(solution)/shard_map/ppermute | solution.py:15
  243.7 3.9 collective-permute-start.10
  248.3 17.6 %collective-permute-start.15 = (f32[256,512]{1,0:T(8,128)S(1)}, f32[256,512]{1,0:T(8,128)S(1)}, u32[]{:S(2)}, u32[]{:S(2)}) collective-permute-start(f32[256,512]{1,0:T(8,128)S(1)} %fusion.14), channel_id=1, source_target_pairs={{0,416},{1,385},{2,354},{3,323},{4,292},{5,261},{6,230},{7,199},{8... | collective-permute-start | bytes 1572872 | tf_op jit(solution)/shard_map/ppermute | solution.py:15
  265.9 1.9 collective-permute-start.12
  268.5 11.7 %collective-permute-start.23 = (f32[256,512]{1,0:T(8,128)S(1)}, f32[256,512]{1,0:T(8,128)S(1)}, u32[]{:S(2)}, u32[]{:S(2)}) collective-permute-start(f32[256,512]{1,0:T(8,128)S(1)} %fusion.14), channel_id=1, source_target_pairs={{0,352},{1,321},{2,290},{3,259},{4,228},{5,197},{6,166},{7,135},{8... | collective-permute-start | bytes 1572872 | tf_op jit(solution)/shard_map/ppermute | solution.py:15
  280.1 22.0 %collective-permute-start.14 = (f32[256,256]{0,1:T(8,128)S(1)}, f32[256,256]{0,1:T(8,128)S(1)}, u32[]{:S(2)}, u32[]{:S(2)}) collective-permute-start(f32[256,256]{0,1:T(8,128)S(1)} %get-tuple-element.10), channel_id=1, source_target_pairs={{0,13},{1,14},{2,15},{3,0},{4,1},{5,2},{6,3},{7,4},{8,5},{9,6},{10... | collective-permute-start | bytes 786440 | tf_op jit(solution)/shard_map/ppermute | solution.py:15
  302.9 1.9 collective-permute-start.25
  304.8 39.3 %collective-permute-done.13 = f32[256,512]{1,0:T(8,128)S(1)} collective-permute-done((f32[256,512]{1,0:T(8,128)S(1)}, f32[256,512]{1,0:T(8,128)S(1)}, u32[]{:S(2)}, u32[]{:S(2)}) %collective-permute-start.13) | collective-permute-done | bytes 524320 | tf_op jit(solution)/shard_map/ppermute | solution.py:15
  344.1 1.9 collective-permute-start.22
  346.7 1.9 collective-permute-start.27
  348.6 23.3 %collective-permute-start.24 = (f32[256,256]{0,1:T(8,128)S(1)}, f32[256,256]{0,1:T(8,128)S(1)}, u32[]{:S(2)}, u32[]{:S(2)}) collective-permute-start(f32[256,256]{0,1:T(8,128)S(1)} %get-tuple-element.16), channel_id=1, source_target_pairs={{0,11},{1,12},{2,13},{3,14},{4,15},{5,0},{6,1},{7,2},{8,3},{9,4},{... | collective-permute-start | bytes 786440 | tf_op jit(solution)/shard_map/ppermute | solution.py:15
  372.6 1.9 collective-permute-start.29
  374.5 1.9 collective-permute-start.26
  377.1 18.9 %collective-permute-start.3 = (f32[256,512]{1,0:T(8,128)S(1)}, f32[256,512]{1,0:T(8,128)S(1)}, u32[]{:S(2)}, u32[]{:S(2)}) collective-permute-start(f32[256,512]{1,0:T(8,128)S(1)} %fusion.14), channel_id=1, source_target_pairs={{0,0},{1,481},{2,450},{3,419},{4,388},{5,357},{6,326},{7,295},{8,2... | collective-permute-start | bytes 1572872 | tf_op jit(solution)/shard_map/ppermute | solution.py:15
  396.0 40.2 %collective-permute-start.28 = (f32[256,256]{0,1:T(8,128)S(1)}, f32[256,256]{0,1:T(8,128)S(1)}, u32[]{:S(2)}, u32[]{:S(2)}) collective-permute-start(f32[256,256]{0,1:T(8,128)S(1)} %get-tuple-element.18), channel_id=1, source_target_pairs={{0,10},{1,11},{2,12},{3,13},{4,14},{5,15},{6,0},{7,1},{8,2},{9,3},... | collective-permute-start | bytes 786440 | tf_op jit(solution)/shard_map/ppermute | solution.py:15
  436.9 6.7 %collective-permute-start.2 = (f32[256,256]{0,1:T(8,128)S(1)}, f32[256,256]{0,1:T(8,128)S(1)}, u32[]{:S(2)}, u32[]{:S(2)}) collective-permute-start(f32[256,256]{0,1:T(8,128)S(1)} %get-tuple-element.5), channel_id=1, source_target_pairs={{0,0},{1,1},{2,2},{3,3},{4,4},{5,5},{6,6},{7,7},{8,8},{9,9},{10,10... | collective-permute-start | bytes 786440 | tf_op jit(solution)/shard_map/ppermute | solution.py:15
  444.9 29.6 %collective-permute-done.2 = f32[256,256]{0,1:T(8,128)S(1)} collective-permute-done((f32[256,256]{0,1:T(8,128)S(1)}, f32[256,256]{0,1:T(8,128)S(1)}, u32[]{:S(2)}, u32[]{:S(2)}) %collective-permute-start.2) | collective-permute-done | bytes 262176 | tf_op jit(solution)/shard_map/ppermute | solution.py:15
  (68 shorter events, 19.5 us)
Async XLA Ops:
  0.0 0.7 copy-start.1
  1.1 1.0 copy-start
  2.4 18.8 %collective-permute-start = (f32[256,256]{1,0:T(8,128)S(1)}, f32[256,256]{1,0:T(8,128)S(1)}, u32[]{:S(2)}, u32[]{:S(2)}) collective-permute-start(f32[256,256]{1,0:T(8,128)S(1)} %get-tuple-element.19), channel_id=1, source_target_pairs={{0,0},{1,32},{2,64},{3,96},{4,128},{5,160},{6,192},{7,224},{8,256}... | collective-permute-start | bytes 786440 | tf_op jit(solution)/shard_map/ppermute | solution.py:15
  12.1 18.0 %collective-permute-start.1 = (f32[256,256]{1,0:T(8,128)S(1)}, f32[256,256]{1,0:T(8,128)S(1)}, u32[]{:S(2)}, u32[]{:S(2)}) collective-permute-start(f32[256,256]{1,0:T(8,128)S(1)} %get-tuple-element.20), channel_id=1, source_target_pairs={{0,16},{1,48},{2,80},{3,112},{4,144},{5,176},{6,208},{7,240},{8,27... | collective-permute-start | bytes 786440 | tf_op jit(solution)/shard_map/ppermute | solution.py:15
  30.4 159.7 %collective-permute-start.5 = (f32[256,512]{1,0:T(8,128)S(1)}, f32[256,512]{1,0:T(8,128)S(1)}, u32[]{:S(2)}, u32[]{:S(2)}) collective-permute-start(f32[256,512]{1,0:T(8,128)S(1)} %fusion.14), channel_id=1, source_target_pairs={{0,496},{1,465},{2,434},{3,403},{4,372},{5,341},{6,310},{7,279},{8... | collective-permute-start | bytes 1572872 | tf_op jit(solution)/shard_map/ppermute | solution.py:15
  58.9 134.5 %collective-permute-start.17 = (f32[256,512]{1,0:T(8,128)S(1)}, f32[256,512]{1,0:T(8,128)S(1)}, u32[]{:S(2)}, u32[]{:S(2)}) collective-permute-start(f32[256,512]{1,0:T(8,128)S(1)} %fusion.14), channel_id=1, source_target_pairs={{0,400},{1,369},{2,338},{3,307},{4,276},{5,245},{6,214},{7,183},{8... | collective-permute-start | bytes 1572872 | tf_op jit(solution)/shard_map/ppermute | solution.py:15
  60.8 135.9 %collective-permute-start.19 = (f32[256,512]{1,0:T(8,128)S(1)}, f32[256,512]{1,0:T(8,128)S(1)}, u32[]{:S(2)}, u32[]{:S(2)}) collective-permute-start(f32[256,512]{1,0:T(8,128)S(1)} %fusion.14), channel_id=1, source_target_pairs={{0,384},{1,353},{2,322},{3,291},{4,260},{5,229},{6,198},{7,167},{8... | collective-permute-start | bytes 1572872 | tf_op jit(solution)/shard_map/ppermute | solution.py:15
  63.1 125.1 %collective-permute-start.4 = (f32[256,256]{0,1:T(8,128)S(1)}, f32[256,256]{0,1:T(8,128)S(1)}, u32[]{:S(2)}, u32[]{:S(2)}) collective-permute-start(f32[256,256]{0,1:T(8,128)S(1)} %get-tuple-element.11), channel_id=1, source_target_pairs={{0,0},{1,1},{2,2},{3,3},{4,4},{5,5},{6,6},{7,7},{8,8},{9,9},{10,10... | collective-permute-start | bytes 786440 | tf_op jit(solution)/shard_map/ppermute | solution.py:15
  93.1 98.4 %collective-permute-start.16 = (f32[256,256]{0,1:T(8,128)S(1)}, f32[256,256]{0,1:T(8,128)S(1)}, u32[]{:S(2)}, u32[]{:S(2)}) collective-permute-start(f32[256,256]{0,1:T(8,128)S(1)} %get-tuple-element.12), channel_id=1, source_target_pairs={{0,13},{1,14},{2,15},{3,0},{4,1},{5,2},{6,3},{7,4},{8,5},{9,6},{10... | collective-permute-start | bytes 786440 | tf_op jit(solution)/shard_map/ppermute | solution.py:15
  188.2 26.4 %collective-permute-start.21 = (f32[256,512]{1,0:T(8,128)S(1)}, f32[256,512]{1,0:T(8,128)S(1)}, u32[]{:S(2)}, u32[]{:S(2)}) collective-permute-start(f32[256,512]{1,0:T(8,128)S(1)} %fusion.14), channel_id=1, source_target_pairs={{0,368},{1,337},{2,306},{3,275},{4,244},{5,213},{6,182},{7,151},{8... | collective-permute-start | bytes 1572872 | tf_op jit(solution)/shard_map/ppermute | solution.py:15
  190.1 4.6 collective-permute-start.18
  191.5 52.2 %collective-permute-start.7 = (f32[256,512]{1,0:T(8,128)S(1)}, f32[256,512]{1,0:T(8,128)S(1)}, u32[]{:S(2)}, u32[]{:S(2)}) collective-permute-start(f32[256,512]{1,0:T(8,128)S(1)} %fusion.14), channel_id=1, source_target_pairs={{0,480},{1,449},{2,418},{3,387},{4,356},{5,325},{6,294},{7,263},{8... | collective-permute-start | bytes 1572872 | tf_op jit(solution)/shard_map/ppermute | solution.py:15
  193.4 5.9 %collective-permute-start.20 = (f32[256,256]{0,1:T(8,128)S(1)}, f32[256,256]{0,1:T(8,128)S(1)}, u32[]{:S(2)}, u32[]{:S(2)}) collective-permute-start(f32[256,256]{0,1:T(8,128)S(1)} %get-tuple-element.14), channel_id=1, source_target_pairs={{0,12},{1,13},{2,14},{3,15},{4,0},{5,1},{6,2},{7,3},{8,4},{9,5},{1... | collective-permute-start | bytes 786440 | tf_op jit(solution)/shard_map/ppermute | solution.py:15
  194.8 71.1 %collective-permute-start.9 = (f32[256,512]{1,0:T(8,128)S(1)}, f32[256,512]{1,0:T(8,128)S(1)}, u32[]{:S(2)}, u32[]{:S(2)}) collective-permute-start(f32[256,512]{1,0:T(8,128)S(1)} %fusion.14), channel_id=1, source_target_pairs={{0,464},{1,433},{2,402},{3,371},{4,340},{5,309},{6,278},{7,247},{8... | collective-permute-start | bytes 1572872 | tf_op jit(solution)/shard_map/ppermute | solution.py:15
  196.7 20.5 %collective-permute-start.6 = (f32[256,256]{0,1:T(8,128)S(1)}, f32[256,256]{0,1:T(8,128)S(1)}, u32[]{:S(2)}, u32[]{:S(2)}) collective-permute-start(f32[256,256]{0,1:T(8,128)S(1)} %get-tuple-element.6), channel_id=1, source_target_pairs={{0,15},{1,0},{2,1},{3,2},{4,3},{5,4},{6,5},{7,6},{8,7},{9,8},{10,9... | collective-permute-start | bytes 786440 | tf_op jit(solution)/shard_map/ppermute | solution.py:15
  199.3 80.8 %collective-permute-start.11 = (f32[256,512]{1,0:T(8,128)S(1)}, f32[256,512]{1,0:T(8,128)S(1)}, u32[]{:S(2)}, u32[]{:S(2)}) collective-permute-start(f32[256,512]{1,0:T(8,128)S(1)} %fusion.14), channel_id=1, source_target_pairs={{0,448},{1,417},{2,386},{3,355},{4,324},{5,293},{6,262},{7,231},{8... | collective-permute-start | bytes 1572872 | tf_op jit(solution)/shard_map/ppermute | solution.py:15
  214.6 33.7 %collective-permute-start.8 = (f32[256,256]{0,1:T(8,128)S(1)}, f32[256,256]{0,1:T(8,128)S(1)}, u32[]{:S(2)}, u32[]{:S(2)}) collective-permute-start(f32[256,256]{0,1:T(8,128)S(1)} %get-tuple-element.7), channel_id=1, source_target_pairs={{0,15},{1,0},{2,1},{3,2},{4,3},{5,4},{6,5},{7,6},{8,7},{9,8},{10,9... | collective-permute-start | bytes 786440 | tf_op jit(solution)/shard_map/ppermute | solution.py:15
  217.2 126.9 %collective-permute-start.13 = (f32[256,512]{1,0:T(8,128)S(1)}, f32[256,512]{1,0:T(8,128)S(1)}, u32[]{:S(2)}, u32[]{:S(2)}) collective-permute-start(f32[256,512]{1,0:T(8,128)S(1)} %fusion.14), channel_id=1, source_target_pairs={{0,432},{1,401},{2,370},{3,339},{4,308},{5,277},{6,246},{7,215},{8... | collective-permute-start | bytes 1572872 | tf_op jit(solution)/shard_map/ppermute | solution.py:15
  243.7 24.8 %collective-permute-start.10 = (f32[256,256]{0,1:T(8,128)S(1)}, f32[256,256]{0,1:T(8,128)S(1)}, u32[]{:S(2)}, u32[]{:S(2)}) collective-permute-start(f32[256,256]{0,1:T(8,128)S(1)} %get-tuple-element.8), channel_id=1, source_target_pairs={{0,14},{1,15},{2,0},{3,1},{4,2},{5,3},{6,4},{7,5},{8,6},{9,7},{10,... | collective-permute-start | bytes 786440 | tf_op jit(solution)/shard_map/ppermute | solution.py:15
  248.3 100.3 %collective-permute-start.15 = (f32[256,512]{1,0:T(8,128)S(1)}, f32[256,512]{1,0:T(8,128)S(1)}, u32[]{:S(2)}, u32[]{:S(2)}) collective-permute-start(f32[256,512]{1,0:T(8,128)S(1)} %fusion.14), channel_id=1, source_target_pairs={{0,416},{1,385},{2,354},{3,323},{4,292},{5,261},{6,230},{7,199},{8... | collective-permute-start | bytes 1572872 | tf_op jit(solution)/shard_map/ppermute | solution.py:15
  265.9 37.0 %collective-permute-start.12 = (f32[256,256]{0,1:T(8,128)S(1)}, f32[256,256]{0,1:T(8,128)S(1)}, u32[]{:S(2)}, u32[]{:S(2)}) collective-permute-start(f32[256,256]{0,1:T(8,128)S(1)} %get-tuple-element.9), channel_id=1, source_target_pairs={{0,14},{1,15},{2,0},{3,1},{4,2},{5,3},{6,4},{7,5},{8,6},{9,7},{10,... | collective-permute-start | bytes 786440 | tf_op jit(solution)/shard_map/ppermute | solution.py:15
  268.5 106.0 %collective-permute-start.23 = (f32[256,512]{1,0:T(8,128)S(1)}, f32[256,512]{1,0:T(8,128)S(1)}, u32[]{:S(2)}, u32[]{:S(2)}) collective-permute-start(f32[256,512]{1,0:T(8,128)S(1)} %fusion.14), channel_id=1, source_target_pairs={{0,352},{1,321},{2,290},{3,259},{4,228},{5,197},{6,166},{7,135},{8... | collective-permute-start | bytes 1572872 | tf_op jit(solution)/shard_map/ppermute | solution.py:15
  280.1 66.5 %collective-permute-start.14 = (f32[256,256]{0,1:T(8,128)S(1)}, f32[256,256]{0,1:T(8,128)S(1)}, u32[]{:S(2)}, u32[]{:S(2)}) collective-permute-start(f32[256,256]{0,1:T(8,128)S(1)} %get-tuple-element.10), channel_id=1, source_target_pairs={{0,13},{1,14},{2,15},{3,0},{4,1},{5,2},{6,3},{7,4},{8,5},{9,6},{10... | collective-permute-start | bytes 786440 | tf_op jit(solution)/shard_map/ppermute | solution.py:15
  302.9 93.1 %collective-permute-start.25 = (f32[256,512]{1,0:T(8,128)S(1)}, f32[256,512]{1,0:T(8,128)S(1)}, u32[]{:S(2)}, u32[]{:S(2)}) collective-permute-start(f32[256,512]{1,0:T(8,128)S(1)} %fusion.14), channel_id=1, source_target_pairs={{0,336},{1,305},{2,274},{3,243},{4,212},{5,181},{6,150},{7,119},{8... | collective-permute-start | bytes 1572872 | tf_op jit(solution)/shard_map/ppermute | solution.py:15
  344.1 28.4 %collective-permute-start.22 = (f32[256,256]{0,1:T(8,128)S(1)}, f32[256,256]{0,1:T(8,128)S(1)}, u32[]{:S(2)}, u32[]{:S(2)}) collective-permute-start(f32[256,256]{0,1:T(8,128)S(1)} %get-tuple-element.15), channel_id=1, source_target_pairs={{0,11},{1,12},{2,13},{3,14},{4,15},{5,0},{6,1},{7,2},{8,3},{9,4},{... | collective-permute-start | bytes 786440 | tf_op jit(solution)/shard_map/ppermute | solution.py:15
  346.7 96.9 %collective-permute-start.27 = (f32[256,512]{1,0:T(8,128)S(1)}, f32[256,512]{1,0:T(8,128)S(1)}, u32[]{:S(2)}, u32[]{:S(2)}) collective-permute-start(f32[256,512]{1,0:T(8,128)S(1)} %fusion.14), channel_id=1, source_target_pairs={{0,320},{1,289},{2,258},{3,227},{4,196},{5,165},{6,134},{7,103},{8... | collective-permute-start | bytes 1572872 | tf_op jit(solution)/shard_map/ppermute | solution.py:15
  348.6 28.5 %collective-permute-start.24 = (f32[256,256]{0,1:T(8,128)S(1)}, f32[256,256]{0,1:T(8,128)S(1)}, u32[]{:S(2)}, u32[]{:S(2)}) collective-permute-start(f32[256,256]{0,1:T(8,128)S(1)} %get-tuple-element.16), channel_id=1, source_target_pairs={{0,11},{1,12},{2,13},{3,14},{4,15},{5,0},{6,1},{7,2},{8,3},{9,4},{... | collective-permute-start | bytes 786440 | tf_op jit(solution)/shard_map/ppermute | solution.py:15
  372.6 71.7 %collective-permute-start.29 = (f32[256,512]{1,0:T(8,128)S(1)}, f32[256,512]{1,0:T(8,128)S(1)}, u32[]{:S(2)}, u32[]{:S(2)}) collective-permute-start(f32[256,512]{1,0:T(8,128)S(1)} %fusion.14), channel_id=1, source_target_pairs={{0,304},{1,273},{2,242},{3,211},{4,180},{5,149},{6,118},{7,87},{8,... | collective-permute-start | bytes 1572872 | tf_op jit(solution)/shard_map/ppermute | solution.py:15
  374.5 62.3 %collective-permute-start.26 = (f32[256,256]{0,1:T(8,128)S(1)}, f32[256,256]{0,1:T(8,128)S(1)}, u32[]{:S(2)}, u32[]{:S(2)}) collective-permute-start(f32[256,256]{0,1:T(8,128)S(1)} %get-tuple-element.17), channel_id=1, source_target_pairs={{0,10},{1,11},{2,12},{3,13},{4,14},{5,15},{6,0},{7,1},{8,2},{9,3},... | collective-permute-start | bytes 786440 | tf_op jit(solution)/shard_map/ppermute | solution.py:15
  377.1 97.5 %collective-permute-start.3 = (f32[256,512]{1,0:T(8,128)S(1)}, f32[256,512]{1,0:T(8,128)S(1)}, u32[]{:S(2)}, u32[]{:S(2)}) collective-permute-start(f32[256,512]{1,0:T(8,128)S(1)} %fusion.14), channel_id=1, source_target_pairs={{0,0},{1,481},{2,450},{3,419},{4,388},{5,357},{6,326},{7,295},{8,2... | collective-permute-start | bytes 1572872 | tf_op jit(solution)/shard_map/ppermute | solution.py:15
  396.0 48.3 %collective-permute-start.28 = (f32[256,256]{0,1:T(8,128)S(1)}, f32[256,256]{0,1:T(8,128)S(1)}, u32[]{:S(2)}, u32[]{:S(2)}) collective-permute-start(f32[256,256]{0,1:T(8,128)S(1)} %get-tuple-element.18), channel_id=1, source_target_pairs={{0,10},{1,11},{2,12},{3,13},{4,14},{5,15},{6,0},{7,1},{8,2},{9,3},... | collective-permute-start | bytes 786440 | tf_op jit(solution)/shard_map/ppermute | solution.py:15
  436.9 37.7 %collective-permute-start.2 = (f32[256,256]{0,1:T(8,128)S(1)}, f32[256,256]{0,1:T(8,128)S(1)}, u32[]{:S(2)}, u32[]{:S(2)}) collective-permute-start(f32[256,256]{0,1:T(8,128)S(1)} %get-tuple-element.5), channel_id=1, source_target_pairs={{0,0},{1,1},{2,2},{3,3},{4,4},{5,5},{6,6},{7,7},{8,8},{9,9},{10,10... | collective-permute-start | bytes 786440 | tf_op jit(solution)/shard_map/ppermute | solution.py:15
  (1 other events, 0.7 us)

commit v2 on v1

--- a/solution.py
+++ b/solution.py
@@ -22,25 +22,6 @@
             half = (r % 2) ^ flip
             target = (2 * c + half, r // 2)
             pairs.append((r * col_count + c, target[0] * col_count + target[1]))
-    return pairs
-
-
-def left_pairs(row_count, col_count, step):
-    pairs = []
-    for r in range(row_count):
-        half = (r + step) % 2
-        for c in range(col_count):
-            target = ((2 * c + half - r - step) % row_count) // 2
-            pairs.append((r * col_count + c, r * col_count + target))
-    return pairs
-
-
-def right_pairs(row_count, col_count, step):
-    pairs = []
-    for r in range(row_count):
-        for c in range(col_count):
-            target = (r - 2 * c - step) % row_count
-            pairs.append((r * col_count + c, target * col_count + c))
     return pairs
 
 
@@ -79,14 +60,14 @@
     live_rows = (offsets[None, :] < BASIS * mol_rows[:, None]).astype(jnp.float32).reshape(height)
     live_cols = (offsets[None, :] < BASIS * mol_cols[:, None]).astype(jnp.float32).reshape(width)
     density = (half_tri + mirrored) * live_rows[:, None] * live_cols[None, :]
-    dense_halves = density.reshape(height, 2, half_width)
-    even_half = dense_halves[:, 0]
-    odd_half = dense_halves[:, 1]
+    row_panel = lax.all_gather(density, "col", axis=1, tiled=True)
+    col_panel = lax.all_gather(density, "row", axis=0, tiled=True)
+    group = upper.shape[0]
     total = None
     for step in range(STEPS):
-        piece = jnp.where((row_id + step) % 2 == 0, even_half, odd_half)
-        left = send(piece, left_pairs(row_count, col_count, step))
-        right = send(density, right_pairs(row_count, col_count, step))
+        start = (row_id + 2 * col_id + step) % row_count
+        left = lax.dynamic_slice_in_dim(row_panel, start * group, group, axis=1)
+        right = lax.dynamic_slice_in_dim(col_panel, start * group, group, axis=0)
         term = jnp.dot(left, right, precision=lax.Precision.HIGHEST, preferred_element_type=jnp.float32)
         total = term if total is None else total + term
     return total

time: 477 us -> 414 us (0.87)
  starting transfers between devices: 286 us -> 13.4 us
  waiting for transfers between devices: 176 us -> 351 us
  matrix products: 10.1 us -> 25.2 us
  between operations: 0.75 us -> 13.8 us
    all_gather x0 -> x2, waiting for transfers between devices: none -> 338 us  [the longest x1 202 us: body(): col_panel = lax.all_gather(density, 'row', axis=0, tiled=True)]
    ppermute x30 -> x2, starting transfers between devices: 286 us -> 13.3 us  [send(): return lax.ppermute(value, AXES, pairs)]
    ppermute x30 -> x2, waiting for transfers between devices: 176 us -> 12.4 us  [send(): return lax.ppermute(value, AXES, pairs)]
    dot_general x14, matrix products: 10.1 us -> 25.2 us  [body(): jnp.dot(left, right, precision=lax.Precision.HIGHEST, preferred_element_t...]
  transfers between devices with their start and end apart: 30 -> 4, of which waited for: 6 -> 4; matrix products, arithmetic and copies ran while one was open for 2% -> 0% of each run, Pallas kernels for 0% -> 0%
where the time goes in v2:
time: 414 us; the launch traced here: 410 us
  waiting for transfers between devices  351 us (85%)
  matrix products  25.2 us (6%)
  between operations  13.8 us (3%)
  starting transfers between devices  13.4 us (3%)
  other arithmetic  4.43 us (1%)
    all_gather x1, waiting for transfers between devices, body(): col_panel = lax.all_gather(density, 'row', axis=0, tiled=True)  202 us
    all_gather x1, waiting for transfers between devices, body(): row_panel = lax.all_gather(density, 'col', axis=1, tiled=True)  137 us
    dot_general x14, matrix products, body(): jnp.dot(left, right, precision=lax.Precision.HIGHEST, preferred_element_t...  25.2 us
    ppermute x2, starting transfers between devices, send(): return lax.ppermute(value, AXES, pairs)  13.3 us
    ppermute x2, waiting for transfers between devices, send(): return lax.ppermute(value, AXES, pairs)  12.4 us
  transfers between devices with their start and end apart: 4, of which 4 were waited for; matrix products, arithmetic and copies ran while one was open for 0% of the time, Pallas kernels for 0%

profile of v2, /device:TPU:57, one launch (start us, length us, event | category | flops | bytes accessed | tf_op | source)
XLA Modules:
  0.0 410.2 jit_solution(16222520946653682628)
XLA Ops:
  6.5 0.7 compare_select_fusion.1
  7.3 0.1 copy.4
  7.4 0.2 mul.122
  7.6 0.4 mul.125
  8.0 1.2 copy.8
  9.4 9.6 %collective-permute-start = (f32[256,256]{1,0:T(8,128)S(1)}, f32[256,256]{1,0:T(8,128)S(1)}, u32[]{:S(2)}, u32[]{:S(2)}) collective-permute-start(f32[256,256]{1,0:T(8,128)S(1)} %get-tuple-element.5), channel_id=1, source_target_pairs={{0,0},{1,32},{2,64},{3,96},{4,128},{5,160},{6,192},{7,224},{8,256}... | collective-permute-start | bytes 786440 | tf_op jit(solution)/shard_map/ppermute | solution.py:15
  19.0 3.7 collective-permute-start.1
  22.8 0.7 dynamic-slice_multiply_fusion.1
  23.5 0.1 fusion.46
  23.6 0.7 dynamic-slice_multiply_fusion
  24.3 0.2 copy.7
  24.5 0.1 convert_bitcast_fusion
  24.6 3.6 collective-permute-done
  28.2 8.9 %collective-permute-done.1 = f32[256,256]{1,0:T(8,128)S(1)} collective-permute-done((f32[256,256]{1,0:T(8,128)S(1)}, f32[256,256]{1,0:T(8,128)S(1)}, u32[]{:S(2)}, u32[]{:S(2)}) %collective-permute-start.1) | collective-permute-done | bytes 262176 | tf_op jit(solution)/shard_map/ppermute | solution.py:15
  37.0 2.0 fusion.2
  39.1 0.7 all-gather.5.cloned.1.call-update
  40.0 136.6 %all-gather.3.cloned.1.call-done = f32[256,8192]{1,0:T(8,128)} async-done(((f32[256,512]{1,0:T(8,128)}), f32[256,8192]{1,0:T(8,128)}) %all-gather.3.cloned.1.call-update) | async-done | bytes 8388624 | tf_op jit(solution)/shard_map/all_gather | solution.py:63
  176.6 201.5 %all-gather.5.cloned.1.call-done = f32[8192,512]{1,0:T(8,128)} async-done(((f32[256,512]{1,0:T(8,128)}), f32[8192,512]{1,0:T(8,128)}) %all-gather.5.cloned.1.call-update) | async-done | bytes 16777232 | tf_op jit(solution)/shard_map/all_gather | solution.py:64
  378.1 1.7 fusion.16
  379.8 1.7 convolution_add_fusion.12
  381.6 1.7 convolution_add_fusion.11
  383.3 1.7 convolution_add_fusion.10
  385.1 1.7 convolution_add_fusion.9
  386.8 1.7 convolution_add_fusion.8
  388.6 1.7 convolution_add_fusion.7
  390.3 1.7 convolution_add_fusion.6
  392.1 1.7 convolution_add_fusion.5
  393.8 1.7 convolution_add_fusion.4
  395.6 1.7 convolution_add_fusion.3
  397.3 1.7 convolution_add_fusion.2
  399.1 1.7 convolution_add_fusion.1
  400.8 2.6 convolution_add_fusion
  (8 shorter events, 0.2 us)
Async XLA Ops:
  6.5 170.1 %all-gather.3.cloned.1.call-start = ((), (), s32[]{:S(2)}) async-start(), calls=%async_computation | async-start | bytes 8912896 | tf_op jit(solution)/shard_map/all_gather | solution.py:63
  9.4 18.8 %collective-permute-start = (f32[256,256]{1,0:T(8,128)S(1)}, f32[256,256]{1,0:T(8,128)S(1)}, u32[]{:S(2)}, u32[]{:S(2)}) collective-permute-start(f32[256,256]{1,0:T(8,128)S(1)} %get-tuple-element.5), channel_id=1, source_target_pairs={{0,0},{1,32},{2,64},{3,96},{4,128},{5,160},{6,192},{7,224},{8,256}... | collective-permute-start | bytes 786440 | tf_op jit(solution)/shard_map/ppermute | solution.py:15
  19.0 18.0 %collective-permute-start.1 = (f32[256,256]{1,0:T(8,128)S(1)}, f32[256,256]{1,0:T(8,128)S(1)}, u32[]{:S(2)}, u32[]{:S(2)}) collective-permute-start(f32[256,256]{1,0:T(8,128)S(1)} %get-tuple-element.6), channel_id=1, source_target_pairs={{0,16},{1,48},{2,80},{3,112},{4,144},{5,176},{6,208},{7,240},{8,27... | collective-permute-start | bytes 786440 | tf_op jit(solution)/shard_map/ppermute | solution.py:15
  39.0 339.1 %all-gather.5.cloned.1.call-start = ((), (), s32[]{:S(2)}) async-start(), calls=%async_computation.1 | async-start | bytes 17301504 | tf_op jit(solution)/shard_map/all_gather | solution.py:64
Sparse Core Ops, SparseCore 0:
  39.1 137.3 all-gather.2
  178.7 199.3 all-gather.4

commit v3 on v1

--- a/solution.py
+++ b/solution.py
@@ -23,6 +23,11 @@
             target = (2 * c + half, r // 2)
             pairs.append((r * col_count + c, target[0] * col_count + target[1]))
     return pairs
+
+
+def shift(value, axis, by):
+    length = lax.axis_size(axis)
+    return lax.ppermute(value, axis, [(i, (i - by) % length) for i in range(length)])
 
 
 def left_pairs(row_count, col_count, step):
@@ -79,16 +84,25 @@
     live_rows = (offsets[None, :] < BASIS * mol_rows[:, None]).astype(jnp.float32).reshape(height)
     live_cols = (offsets[None, :] < BASIS * mol_cols[:, None]).astype(jnp.float32).reshape(width)
     density = (half_tri + mirrored) * live_rows[:, None] * live_cols[None, :]
+    group = upper.shape[0]
+    right = send(density, right_pairs(row_count, col_count, 0))
+    have = 1
+    while have < STEPS:
+        take = min(have, STEPS - have)
+        right = jnp.concatenate([right, shift(right[: take * group], "row", have)], axis=0)
+        have += take
     dense_halves = density.reshape(height, 2, half_width)
-    even_half = dense_halves[:, 0]
-    odd_half = dense_halves[:, 1]
-    total = None
-    for step in range(STEPS):
-        piece = jnp.where((row_id + step) % 2 == 0, even_half, odd_half)
-        left = send(piece, left_pairs(row_count, col_count, step))
-        right = send(density, right_pairs(row_count, col_count, step))
-        term = jnp.dot(left, right, precision=lax.Precision.HIGHEST, preferred_element_type=jnp.float32)
-        total = term if total is None else total + term
+    pieces = []
+    for step in range(2):
+        piece = jnp.where((row_id + step) % 2 == 0, dense_halves[:, 0], dense_halves[:, 1])
+        pieces.append(send(piece, left_pairs(row_count, col_count, step)))
+    left = jnp.concatenate(pieces, axis=1)
+    have = 2
+    while have < STEPS:
+        take = min(have, STEPS - have)
+        left = jnp.concatenate([left, shift(left[:, : take * group], "col", have // 2)], axis=1)
+        have += take
+    total = jnp.dot(left, right, precision=lax.Precision.HIGHEST, preferred_element_type=jnp.float32)
     return total
 
 

time: 477 us -> 546 us (1.14); the launches traced: 476 us -> 540 us
  waiting for transfers between devices: 176 us -> 360 us
  starting transfers between devices: 286 us -> 162 us
    ppermute x0 -> x7, waiting for transfers between devices: none -> 221 us  [shift(): lax.ppermute(value, axis, [(i, (i - by) % length) for i in range(length)])]
    ppermute x30 -> x5, starting transfers between devices: 286 us -> 81.6 us  [send(): return lax.ppermute(value, AXES, pairs)]
    ppermute x0 -> x7, starting transfers between devices: none -> 80.6 us  [shift(): lax.ppermute(value, axis, [(i, (i - by) % length) for i in range(length)])]
    ppermute x30 -> x5, waiting for transfers between devices: 176 us -> 139 us  [send(): return lax.ppermute(value, AXES, pairs)]
  transfers between devices with their start and end apart: 30 -> 12, of which waited for: 6 -> 10; matrix products, arithmetic and copies ran while one was open for 2% -> 1% of each run, Pallas kernels for 0% -> 0%
where the time goes in v3:
time: 546 us; the launch traced here: 540 us
  waiting for transfers between devices  360 us (66%)
  starting transfers between devices  162 us (30%)
  matrix products  7.35 us (1%)
    ppermute x7, waiting for transfers between devices, shift(): lax.ppermute(value, axis, [(i, (i - by) % length) for i in range(length)])  221 us
    ppermute x5, waiting for transfers between devices, send(): return lax.ppermute(value, AXES, pairs)  139 us
    ppermute x5, starting transfers between devices, send(): return lax.ppermute(value, AXES, pairs)  81.6 us
    ppermute x7, starting transfers between devices, shift(): lax.ppermute(value, axis, [(i, (i - by) % length) for i in range(length)])  80.6 us
  transfers between devices with their start and end apart: 12, of which 10 were waited for; matrix products, arithmetic and copies ran while one was open for 1% of the time, Pallas kernels for 0%

profile of v3, /device:TPU:57, one launch (start us, length us, event | category | flops | bytes accessed | tf_op | source)
XLA Modules:
  0.0 539.6 jit_solution(2466311974072119519)
XLA Ops:
  0.0 0.8 compare_select_fusion.1
  0.9 0.2 mul.50
  1.1 0.4 mul.53
  1.5 1.2 copy.10
  2.9 9.6 %collective-permute-start = (f32[256,256]{1,0:T(8,128)S(1)}, f32[256,256]{1,0:T(8,128)S(1)}, u32[]{:S(2)}, u32[]{:S(2)}) collective-permute-start(f32[256,256]{1,0:T(8,128)S(1)} %get-tuple-element.7), channel_id=1, source_target_pairs={{0,0},{1,32},{2,64},{3,96},{4,128},{5,160},{6,192},{7,224},{8,256}... | collective-permute-start | bytes 786440 | tf_op jit(solution)/shard_map/ppermute | solution.py:15
  12.5 3.7 collective-permute-start.1
  16.8 4.9 collective-permute-done
  21.6 8.9 %collective-permute-done.1 = f32[256,256]{1,0:T(8,128)S(1)} collective-permute-done((f32[256,256]{1,0:T(8,128)S(1)}, f32[256,256]{1,0:T(8,128)S(1)}, u32[]{:S(2)}, u32[]{:S(2)}) %collective-permute-start.1) | collective-permute-done | bytes 262176 | tf_op jit(solution)/shard_map/ppermute | solution.py:15
  30.7 24.7 %collective-permute-start.7 = (f32[256,512]{1,0:T(8,128)S(1)}, f32[256,512]{1,0:T(8,128)S(1)}, u32[]{:S(2)}, u32[]{:S(2)}) collective-permute-start(f32[256,512]{1,0:T(8,128)S(1)} %fusion.2), channel_id=1, source_target_pairs={{0,0},{1,481},{2,450},{3,419},{4,388},{5,357},{6,326},{7,295},{8,2... | collective-permute-start | bytes 1572872 | tf_op jit(solution)/shard_map/ppermute | solution.py:15
  55.3 6.1 %collective-permute-done.7 = f32[256,512]{1,0:T(8,128)S(1)} collective-permute-done((f32[256,512]{1,0:T(8,128)S(1)}, f32[256,512]{1,0:T(8,128)S(1)}, u32[]{:S(2)}, u32[]{:S(2)}) %collective-permute-start.7) | collective-permute-done | bytes 524320 | tf_op jit(solution)/shard_map/ppermute | solution.py:15
  61.4 13.9 %collective-permute-start.8 = (f32[256,512]{1,0:T(8,128)S(1)}, f32[256,512]{1,0:T(8,128)S(1)}, u32[]{:S(2)}, u32[]{:S(2)}) collective-permute-start(f32[256,512]{1,0:T(8,128)S(1)} %collective-permute-done.7), channel_id=1, source_target_pairs={{0,496},{16,0},{32,16},{48,32},{64,48},{80,64},{96,80},{112,96},{1... | collective-permute-start | bytes 1572872 | tf_op jit(solution)/shard_map/ppermute | solution.py:30
  75.4 11.3 %collective-permute-done.8 = f32[256,512]{1,0:T(8,128)S(1)} collective-permute-done((f32[256,512]{1,0:T(8,128)S(1)}, f32[256,512]{1,0:T(8,128)S(1)}, u32[]{:S(2)}, u32[]{:S(2)}) %collective-permute-start.8) | collective-permute-done | bytes 524320 | tf_op jit(solution)/shard_map/ppermute | solution.py:30
  86.8 41.3 %collective-permute-start.9 = (f32[512,512]{1,0:T(8,128)S(1)}, f32[512,512]{1,0:T(8,128)S(1)}, u32[]{:S(2)}, u32[]{:S(2)}) collective-permute-start(f32[512,512]{1,0:T(8,128)S(1)} %pad_maximum_fusion.8), channel_id=1, source_target_pairs={{0,480},{16,496},{32,0},{48,16},{64,32},{80,48},{96,64},{112,80},{... | collective-permute-start | bytes 3145736 | tf_op jit(solution)/shard_map/ppermute | solution.py:30
  128.0 29.9 %collective-permute-done.9 = f32[512,512]{1,0:T(8,128)S(1)} collective-permute-done((f32[512,512]{1,0:T(8,128)S(1)}, f32[512,512]{1,0:T(8,128)S(1)}, u32[]{:S(2)}, u32[]{:S(2)}) %collective-permute-start.9) | collective-permute-done | bytes 1048608 | tf_op jit(solution)/shard_map/ppermute | solution.py:30
  157.9 1.5 pad_maximum_fusion.3
  159.4 7.3 %collective-permute-start.10 = (f32[1024,512]{1,0:T(8,128)}, f32[1024,512]{1,0:T(8,128)S(1)}, u32[]{:S(2)}, u32[]{:S(2)}) collective-permute-start(f32[1024,512]{1,0:T(8,128)} %pad_maximum_fusion.3), channel_id=1, source_target_pairs={{0,448},{16,464},{32,480},{48,496},{64,0},{80,16},{96,32},{112,48}... | collective-permute-start | bytes 6291464 | tf_op jit(solution)/shard_map/ppermute | solution.py:30
  166.7 2.0 copy.11
  168.8 1.2 select_bitcast_fusion
  169.9 1.9 collective-permute-start.2
  171.9 41.7 %collective-permute-start.3 = (f32[256,256]{0,1:T(8,128)S(1)}, f32[256,256]{0,1:T(8,128)S(1)}, u32[]{:S(2)}, u32[]{:S(2)}) collective-permute-start(f32[256,256]{0,1:T(8,128)S(1)} %get-tuple-element.5), channel_id=1, source_target_pairs={{0,0},{1,1},{2,2},{3,3},{4,4},{5,5},{6,6},{7,7},{8,8},{9,9},{10,10... | collective-permute-start | bytes 786440 | tf_op jit(solution)/shard_map/ppermute | solution.py:15
  213.6 113.4 %collective-permute-done.2 = f32[256,256]{0,1:T(8,128)S(1)} collective-permute-done((f32[256,256]{0,1:T(8,128)S(1)}, f32[256,256]{0,1:T(8,128)S(1)}, u32[]{:S(2)}, u32[]{:S(2)}) %collective-permute-start.2) | collective-permute-done | bytes 262176 | tf_op jit(solution)/shard_map/ppermute | solution.py:15
  326.9 5.6 %collective-permute-done.3 = f32[256,256]{0,1:T(8,128)S(1)} collective-permute-done((f32[256,256]{0,1:T(8,128)S(1)}, f32[256,256]{0,1:T(8,128)S(1)}, u32[]{:S(2)}, u32[]{:S(2)}) %collective-permute-start.3) | collective-permute-done | bytes 262176 | tf_op jit(solution)/shard_map/ppermute | solution.py:15
  332.6 4.2 collective-permute-start.4
  336.8 6.3 %collective-permute-done.4 = f32[256,512]{0,1:T(8,128)S(1)} collective-permute-done((f32[256,512]{0,1:T(8,128)S(1)}, f32[256,512]{0,1:T(8,128)S(1)}, u32[]{:S(2)}, u32[]{:S(2)}) %collective-permute-start.4) | collective-permute-done | bytes 524320 | tf_op jit(solution)/shard_map/ppermute | solution.py:30
  343.2 9.9 %collective-permute-start.5 = (f32[256,1024]{0,1:T(8,128)S(1)}, f32[256,1024]{0,1:T(8,128)S(1)}, u32[]{:S(2)}, u32[]{:S(2)}) collective-permute-start(f32[256,1024]{0,1:T(8,128)S(1)} %pad_maximum_fusion.7), channel_id=1, source_target_pairs={{0,14},{1,15},{2,0},{3,1},{4,2},{5,3},{6,4},{7,5},{8,6},{9,7},{10,... | collective-permute-start | bytes 3145736 | tf_op jit(solution)/shard_map/ppermute | solution.py:30
  353.1 0.4 pad_maximum_fusion
  353.5 1.9 collective-permute-start.11
  355.5 48.7 %collective-permute-done.5 = f32[256,1024]{0,1:T(8,128)S(1)} collective-permute-done((f32[256,1024]{0,1:T(8,128)S(1)}, f32[256,1024]{0,1:T(8,128)S(1)}, u32[]{:S(2)}, u32[]{:S(2)}) %collective-permute-start.5) | collective-permute-done | bytes 1048608 | tf_op jit(solution)/shard_map/ppermute | solution.py:30
  404.3 2.1 collective-permute-start.6
  406.8 124.8 %collective-permute-done.6 = f32[256,1536]{0,1:T(8,128)S(1)} collective-permute-done((f32[256,1536]{0,1:T(8,128)S(1)}, f32[256,1536]{0,1:T(8,128)S(1)}, u32[]{:S(2)}, u32[]{:S(2)}) %collective-permute-start.6) | collective-permute-done | bytes 1572896 | tf_op jit(solution)/shard_map/ppermute | solution.py:30
  531.9 0.3 constant_dynamic-update-slice_fusion.5
  532.2 7.4 %fusion.4 = f32[256,512]{1,0:T(8,128)} fusion(f32[256,3584]{0,1:T(8,128)S(1)} %constant_dynamic-update-slice_fusion, f32[3584,512]{1,0:T(8,128)S(1)} %constant_dynamic-update-slice_fusion.5), kind=kOutput, calls=%fused_computation.39 | convolution fusion | flops 5637144576 | bytes 11534336 | tf_op jit(solution)/shard_map/dot_general | solution.py:105
  (41 shorter events, 1.8 us)
Async XLA Ops:
  0.0 16.2 %copy-start.6 = (s32[64]{0:T(128)S(1)}, s32[64]{0:T(128)}, u32[]{:S(2)}) copy-start(s32[64]{0:T(128)} %param.5) | copy-start | bytes 772
  0.9 29.7 %copy-start.4 = (f32[256,512]{1,0:T(8,128)S(1)}, f32[256,512]{1,0:T(8,128)}, u32[]{:S(2)}) copy-start(f32[256,512]{1,0:T(8,128)} %param.3) | copy-start | bytes 1572868
  2.9 18.8 %collective-permute-start = (f32[256,256]{1,0:T(8,128)S(1)}, f32[256,256]{1,0:T(8,128)S(1)}, u32[]{:S(2)}, u32[]{:S(2)}) collective-permute-start(f32[256,256]{1,0:T(8,128)S(1)} %get-tuple-element.7), channel_id=1, source_target_pairs={{0,0},{1,32},{2,64},{3,96},{4,128},{5,160},{6,192},{7,224},{8,256}... | collective-permute-start | bytes 786440 | tf_op jit(solution)/shard_map/ppermute | solution.py:15
  12.5 18.0 %collective-permute-start.1 = (f32[256,256]{1,0:T(8,128)S(1)}, f32[256,256]{1,0:T(8,128)S(1)}, u32[]{:S(2)}, u32[]{:S(2)}) collective-permute-start(f32[256,256]{1,0:T(8,128)S(1)} %get-tuple-element.8), channel_id=1, source_target_pairs={{0,16},{1,48},{2,80},{3,112},{4,144},{5,176},{6,208},{7,240},{8,27... | collective-permute-start | bytes 786440 | tf_op jit(solution)/shard_map/ppermute | solution.py:15
  30.7 56.1 %copy-start.5 = (f32[256,512]{1,0:T(8,128)}, f32[256,512]{1,0:T(8,128)S(1)}, u32[]{:S(2)}) copy-start(f32[256,512]{1,0:T(8,128)S(1)} %fusion.2) | copy-start | bytes 1572868
  30.7 30.8 %collective-permute-start.7 = (f32[256,512]{1,0:T(8,128)S(1)}, f32[256,512]{1,0:T(8,128)S(1)}, u32[]{:S(2)}, u32[]{:S(2)}) collective-permute-start(f32[256,512]{1,0:T(8,128)S(1)} %fusion.2), channel_id=1, source_target_pairs={{0,0},{1,481},{2,450},{3,419},{4,388},{5,357},{6,326},{7,295},{8,2... | collective-permute-start | bytes 1572872 | tf_op jit(solution)/shard_map/ppermute | solution.py:15
  61.4 96.4 %copy-start = (f32[256,512]{1,0:T(8,128)}, f32[256,512]{1,0:T(8,128)S(1)}, u32[]{:S(2)}) copy-start(f32[256,512]{1,0:T(8,128)S(1)} %collective-permute-done.7) | copy-start | bytes 1572868
  61.4 25.2 %collective-permute-start.8 = (f32[256,512]{1,0:T(8,128)S(1)}, f32[256,512]{1,0:T(8,128)S(1)}, u32[]{:S(2)}, u32[]{:S(2)}) collective-permute-start(f32[256,512]{1,0:T(8,128)S(1)} %collective-permute-done.7), channel_id=1, source_target_pairs={{0,496},{16,0},{32,16},{48,32},{64,48},{80,64},{96,80},{112,96},{1... | collective-permute-start | bytes 1572872 | tf_op jit(solution)/shard_map/ppermute | solution.py:30
  86.7 72.7 %copy-start.2 = (f32[256,512]{1,0:T(8,128)}, f32[256,512]{1,0:T(8,128)S(1)}, u32[]{:S(2)}) copy-start(f32[256,512]{1,0:T(8,128)S(1)} %collective-permute-done.8) | copy-start | bytes 1572868
  86.8 71.1 %collective-permute-start.9 = (f32[512,512]{1,0:T(8,128)S(1)}, f32[512,512]{1,0:T(8,128)S(1)}, u32[]{:S(2)}, u32[]{:S(2)}) collective-permute-start(f32[512,512]{1,0:T(8,128)S(1)} %pad_maximum_fusion.8), channel_id=1, source_target_pairs={{0,480},{16,496},{32,0},{48,16},{64,32},{80,48},{96,64},{112,80},{... | collective-permute-start | bytes 3145736 | tf_op jit(solution)/shard_map/ppermute | solution.py:30
  159.4 193.7 %collective-permute-start.10 = (f32[1024,512]{1,0:T(8,128)}, f32[1024,512]{1,0:T(8,128)S(1)}, u32[]{:S(2)}, u32[]{:S(2)}) collective-permute-start(f32[1024,512]{1,0:T(8,128)} %pad_maximum_fusion.3), channel_id=1, source_target_pairs={{0,448},{16,464},{32,480},{48,496},{64,0},{80,16},{96,32},{112,48}... | collective-permute-start | bytes 6291464 | tf_op jit(solution)/shard_map/ppermute | solution.py:30
  168.8 184.3 %copy-start.1 = (f32[256,512]{1,0:T(8,128)S(1)}, f32[256,512]{1,0:T(8,128)}, u32[]{:S(2)}) copy-start(f32[256,512]{1,0:T(8,128)} %copy-done) | copy-start | bytes 1572868
  168.8 184.3 %copy-start.3 = (f32[256,512]{1,0:T(8,128)S(1)}, f32[256,512]{1,0:T(8,128)}, u32[]{:S(2)}) copy-start(f32[256,512]{1,0:T(8,128)} %copy-done.2) | copy-start | bytes 1572868
  169.9 157.0 %collective-permute-start.2 = (f32[256,256]{0,1:T(8,128)S(1)}, f32[256,256]{0,1:T(8,128)S(1)}, u32[]{:S(2)}, u32[]{:S(2)}) collective-permute-start(f32[256,256]{0,1:T(8,128)S(1)} %get-tuple-element.6), channel_id=1, source_target_pairs={{0,0},{1,1},{2,2},{3,3},{4,4},{5,5},{6,6},{7,7},{8,8},{9,9},{10,10... | collective-permute-start | bytes 786440 | tf_op jit(solution)/shard_map/ppermute | solution.py:15
  171.9 160.7 %collective-permute-start.3 = (f32[256,256]{0,1:T(8,128)S(1)}, f32[256,256]{0,1:T(8,128)S(1)}, u32[]{:S(2)}, u32[]{:S(2)}) collective-permute-start(f32[256,256]{0,1:T(8,128)S(1)} %get-tuple-element.5), channel_id=1, source_target_pairs={{0,0},{1,1},{2,2},{3,3},{4,4},{5,5},{6,6},{7,7},{8,8},{9,9},{10,10... | collective-permute-start | bytes 786440 | tf_op jit(solution)/shard_map/ppermute | solution.py:15
  332.6 10.5 %collective-permute-start.4 = (f32[256,512]{0,1:T(8,128)S(1)}, f32[256,512]{0,1:T(8,128)S(1)}, u32[]{:S(2)}, u32[]{:S(2)}) collective-permute-start(f32[256,512]{0,1:T(8,128)S(1)} %pad_maximum_fusion.9), channel_id=1, source_target_pairs={{0,15},{1,0},{2,1},{3,2},{4,3},{5,4},{6,5},{7,6},{8,7},{9,8},{10,9... | collective-permute-start | bytes 1572872 | tf_op jit(solution)/shard_map/ppermute | solution.py:30
  343.2 61.0 %collective-permute-start.5 = (f32[256,1024]{0,1:T(8,128)S(1)}, f32[256,1024]{0,1:T(8,128)S(1)}, u32[]{:S(2)}, u32[]{:S(2)}) collective-permute-start(f32[256,1024]{0,1:T(8,128)S(1)} %pad_maximum_fusion.7), channel_id=1, source_target_pairs={{0,14},{1,15},{2,0},{3,1},{4,2},{5,3},{6,4},{7,5},{8,6},{9,7},{10,... | collective-permute-start | bytes 3145736 | tf_op jit(solution)/shard_map/ppermute | solution.py:30
  353.5 178.4 %collective-permute-start.11 = (f32[1536,512]{1,0:T(8,128)S(1)}, f32[1536,512]{1,0:T(8,128)S(1)}, u32[]{:S(2)}, u32[]{:S(2)}) collective-permute-start(f32[1536,512]{1,0:T(8,128)S(1)} %pad_maximum_fusion), channel_id=1, source_target_pairs={{0,384},{16,400},{32,416},{48,432},{64,448},{80,464},{96,480},{112... | collective-permute-start | bytes 9437192 | tf_op jit(solution)/shard_map/ppermute | solution.py:30
  404.3 127.3 %collective-permute-start.6 = (f32[256,1536]{0,1:T(8,128)S(1)}, f32[256,1536]{0,1:T(8,128)S(1)}, u32[]{:S(2)}, u32[]{:S(2)}) collective-permute-start(f32[256,1536]{0,1:T(8,128)S(1)} %pad_maximum_fusion.4), channel_id=1, source_target_pairs={{0,12},{1,13},{2,14},{3,15},{4,0},{5,1},{6,2},{7,3},{8,4},{9,5},{1... | collective-permute-start | bytes 4718600 | tf_op jit(solution)/shard_map/ppermute | solution.py:30

commit v4 on v3

--- a/solution.py
+++ b/solution.py
@@ -85,12 +85,7 @@
     live_cols = (offsets[None, :] < BASIS * mol_cols[:, None]).astype(jnp.float32).reshape(width)
     density = (half_tri + mirrored) * live_rows[:, None] * live_cols[None, :]
     group = upper.shape[0]
-    right = send(density, right_pairs(row_count, col_count, 0))
-    have = 1
-    while have < STEPS:
-        take = min(have, STEPS - have)
-        right = jnp.concatenate([right, shift(right[: take * group], "row", have)], axis=0)
-        have += take
+    col_panel = lax.all_gather(density, "row", axis=0, tiled=True)
     dense_halves = density.reshape(height, 2, half_width)
     pieces = []
     for step in range(2):
@@ -102,6 +97,9 @@
         take = min(have, STEPS - have)
         left = jnp.concatenate([left, shift(left[:, : take * group], "col", have // 2)], axis=1)
         have += take
+    start = (row_id + 2 * col_id) % row_count
+    doubled = jnp.concatenate([col_panel, col_panel[: STEPS * group]], axis=0)
+    right = lax.dynamic_slice_in_dim(doubled, start * group, STEPS * group, axis=0)
     total = jnp.dot(left, right, precision=lax.Precision.HIGHEST, preferred_element_type=jnp.float32)
     return total
 

time: 546 us -> 434 us (0.79)
  the two profiles are of different devices: /device:TPU:57 before, /device:TPU:1 now
where the time goes in v4:
time: 434 us; the launch traced here: 433 us
  waiting for transfers between devices  348 us (80%)
  starting transfers between devices  44.5 us (10%)
  between operations  13.6 us (3%)
  local copies, waits for them, and re-layouts  12.5 us (3%)
  matrix products  10.7 us (2%)
    all_gather x1, waiting for transfers between devices, body(): col_panel = lax.all_gather(density, 'row', axis=0, tiled=True)  167 us
    ppermute x3, waiting for transfers between devices, shift(): lax.ppermute(value, axis, [(i, (i - by) % length) for i in range(length)])  154 us
    ppermute x3, starting transfers between devices, shift(): lax.ppermute(value, axis, [(i, (i - by) % length) for i in range(length)])  32.2 us
    ppermute x4, waiting for transfers between devices, send(): return lax.ppermute(value, AXES, pairs)  27.6 us
    ppermute x4, starting transfers between devices, send(): return lax.ppermute(value, AXES, pairs)  12.3 us
    dot_general x1, matrix products, body(): jnp.dot(left, right, precision=lax.Precision.HIGHEST, preferred_element_t...  10.7 us
  transfers between devices with their start and end apart: 8, of which 6 were waited for; matrix products, arithmetic and copies ran while one was open for 2% of the time, Pallas kernels for 0%

profile of v4, /device:TPU:1, one launch (start us, length us, event | category | flops | bytes accessed | tf_op | source)
XLA Modules:
  0.0 433.1 jit_solution(18252036856069387465)
XLA Ops:
  6.5 0.8 compare_select_fusion.1
  7.3 0.1 copy.4
  7.4 0.2 mul.56
  7.6 0.4 mul.59
  8.0 1.2 copy.10
  9.4 7.2 %collective-permute-start = (f32[256,256]{1,0:T(8,128)S(1)}, f32[256,256]{1,0:T(8,128)S(1)}, u32[]{:S(2)}, u32[]{:S(2)}) collective-permute-start(f32[256,256]{1,0:T(8,128)S(1)} %get-tuple-element.7), channel_id=1, source_target_pairs={{0,0},{1,32},{2,64},{3,96},{4,128},{5,160},{6,192},{7,224},{8,256}... | collective-permute-start | bytes 786440 | tf_op jit(solution)/shard_map/ppermute | solution.py:15
  16.6 3.7 collective-permute-start.1
  20.4 0.1 dynamic-slice_multiply_fusion.1
  20.4 0.1 fusion.6
  20.5 0.1 dynamic-slice_multiply_fusion
  20.6 0.2 copy.9
  20.9 8.7 %collective-permute-done = f32[256,256]{1,0:T(8,128)S(1)} collective-permute-done((f32[256,256]{1,0:T(8,128)S(1)}, f32[256,256]{1,0:T(8,128)S(1)}, u32[]{:S(2)}, u32[]{:S(2)}) %collective-permute-start) | collective-permute-done | bytes 262176 | tf_op jit(solution)/shard_map/ppermute | solution.py:15
  29.6 19.0 %collective-permute-done.1 = f32[256,256]{1,0:T(8,128)S(1)} collective-permute-done((f32[256,256]{1,0:T(8,128)S(1)}, f32[256,256]{1,0:T(8,128)S(1)}, u32[]{:S(2)}, u32[]{:S(2)}) %collective-permute-start.1) | collective-permute-done | bytes 262176 | tf_op jit(solution)/shard_map/ppermute | solution.py:15
  48.5 0.9 fusion.5
  49.5 1.2 copy.11
  50.8 0.7 collective-permute-start.3
  51.5 0.7 collective-permute-start.2
  52.2 1.9 collective-permute-start.4
  54.1 26.6 %collective-permute-done.4 = f32[256,512]{0,1:T(8,128)S(1)} collective-permute-done((f32[256,512]{0,1:T(8,128)S(1)}, f32[256,512]{0,1:T(8,128)S(1)}, u32[]{:S(2)}, u32[]{:S(2)}) %collective-permute-start.4) | collective-permute-done | bytes 524320 | tf_op jit(solution)/shard_map/ppermute | solution.py:30
  80.8 28.4 %collective-permute-start.5 = (f32[256,1024]{0,1:T(8,128)S(1)}, f32[256,1024]{0,1:T(8,128)S(1)}, u32[]{:S(2)}, u32[]{:S(2)}) collective-permute-start(f32[256,1024]{0,1:T(8,128)S(1)} %pad_maximum_fusion.3), channel_id=1, source_target_pairs={{0,14},{1,15},{2,0},{3,1},{4,2},{5,3},{6,4},{7,5},{8,6},{9,7},{10,... | collective-permute-start | bytes 3145736 | tf_op jit(solution)/shard_map/ppermute | solution.py:30
  109.2 44.3 %collective-permute-done.5 = f32[256,1024]{0,1:T(8,128)S(1)} collective-permute-done((f32[256,1024]{0,1:T(8,128)S(1)}, f32[256,1024]{0,1:T(8,128)S(1)}, u32[]{:S(2)}, u32[]{:S(2)}) %collective-permute-start.5) | collective-permute-done | bytes 1048608 | tf_op jit(solution)/shard_map/ppermute | solution.py:30
  153.5 1.3 pad_maximum_fusion
  154.8 1.9 collective-permute-start.6
  156.7 0.7 constant_dynamic-update-slice_fusion.4
  157.4 0.7 constant_dynamic-update-slice_fusion.3
  158.1 0.8 constant_dynamic-update-slice_fusion.2
  159.0 1.1 constant_dynamic-update-slice_fusion.1
  160.0 82.8 %collective-permute-done.6 = f32[256,1536]{0,1:T(8,128)} collective-permute-done((f32[256,1536]{0,1:T(8,128)}, f32[256,1536]{0,1:T(8,128)}, u32[]{:S(2)}, u32[]{:S(2)}) %collective-permute-start.6) | collective-permute-done | bytes 1572896 | tf_op jit(solution)/shard_map/ppermute | solution.py:30
  242.9 2.7 constant_dynamic-update-slice_fusion
  245.5 166.9 %all-gather.2.cloned.1.call-done = f32[8192,512]{1,0:T(8,128)} async-done(((f32[256,512]{1,0:T(8,128)}), f32[8192,512]{1,0:T(8,128)}) %all-gather.2.cloned.1.call-update) | async-done | bytes 16777232 | tf_op jit(solution)/shard_map/all_gather | solution.py:88
  412.5 3.1 slice-done
  415.5 10.7 %fusion.1 = f32[256,512]{1,0:T(8,128)} fusion(f32[256,3584]{0,1:T(8,128)} %constant_dynamic-update-slice_fusion, s32[]{:T(128)S(6)} %select_n.95, f32[8192,512]{1,0:T(8,128)} %all-gather.2.cloned.1.call-done, f32[3584,512]{1,0:T(8,128)S(1)} %slice-done), kind=kOutput, calls=%fused_computation.3 | convolution fusion | flops 5638979584 | bytes 28311556 | tf_op jit(solution)/shard_map/dot_general | solution.py:103
  (18 shorter events, 0.4 us)
Async XLA Ops:
  6.5 13.8 %copy-start.1 = (s32[64]{0:T(128)S(1)}, s32[64]{0:T(128)}, u32[]{:S(2)}) copy-start(s32[64]{0:T(128)} %param.5) | copy-start | bytes 772
  6.5 405.9 %all-gather.2.cloned.1.call-start = ((), (), s32[]{:S(2)}) async-start(), calls=%async_computation | async-start | bytes 17301504 | tf_op jit(solution)/shard_map/all_gather | solution.py:88
  7.4 41.1 %copy-start = (f32[256,512]{1,0:T(8,128)S(1)}, f32[256,512]{1,0:T(8,128)}, u32[]{:S(2)}) copy-start(f32[256,512]{1,0:T(8,128)} %param.3) | copy-start | bytes 1572868
  9.4 20.2 %collective-permute-start = (f32[256,256]{1,0:T(8,128)S(1)}, f32[256,256]{1,0:T(8,128)S(1)}, u32[]{:S(2)}, u32[]{:S(2)}) collective-permute-start(f32[256,256]{1,0:T(8,128)S(1)} %get-tuple-element.7), channel_id=1, source_target_pairs={{0,0},{1,32},{2,64},{3,96},{4,128},{5,160},{6,192},{7,224},{8,256}... | collective-permute-start | bytes 786440 | tf_op jit(solution)/shard_map/ppermute | solution.py:15
  16.6 31.9 %collective-permute-start.1 = (f32[256,256]{1,0:T(8,128)S(1)}, f32[256,256]{1,0:T(8,128)S(1)}, u32[]{:S(2)}, u32[]{:S(2)}) collective-permute-start(f32[256,256]{1,0:T(8,128)S(1)} %get-tuple-element.8), channel_id=1, source_target_pairs={{0,16},{1,48},{2,80},{3,112},{4,144},{5,176},{6,208},{7,240},{8,27... | collective-permute-start | bytes 786440 | tf_op jit(solution)/shard_map/ppermute | solution.py:15
  50.8 1.4 collective-permute-start.3
  51.5 0.7 collective-permute-start.2
  52.2 28.5 %collective-permute-start.4 = (f32[256,512]{0,1:T(8,128)S(1)}, f32[256,512]{0,1:T(8,128)S(1)}, u32[]{:S(2)}, u32[]{:S(2)}) collective-permute-start(f32[256,512]{0,1:T(8,128)S(1)} %pad_maximum_fusion.4), channel_id=1, source_target_pairs={{0,15},{1,0},{2,1},{3,2},{4,3},{5,4},{6,5},{7,6},{8,7},{9,8},{10,9... | collective-permute-start | bytes 1572872 | tf_op jit(solution)/shard_map/ppermute | solution.py:30
  80.8 72.7 %collective-permute-start.5 = (f32[256,1024]{0,1:T(8,128)S(1)}, f32[256,1024]{0,1:T(8,128)S(1)}, u32[]{:S(2)}, u32[]{:S(2)}) collective-permute-start(f32[256,1024]{0,1:T(8,128)S(1)} %pad_maximum_fusion.3), channel_id=1, source_target_pairs={{0,14},{1,15},{2,0},{3,1},{4,2},{5,3},{6,4},{7,5},{8,6},{9,7},{10,... | collective-permute-start | bytes 3145736 | tf_op jit(solution)/shard_map/ppermute | solution.py:30
  154.8 88.1 %collective-permute-start.6 = (f32[256,1536]{0,1:T(8,128)}, f32[256,1536]{0,1:T(8,128)}, u32[]{:S(2)}, u32[]{:S(2)}) collective-permute-start(f32[256,1536]{0,1:T(8,128)} %pad_maximum_fusion), channel_id=1, source_target_pairs={{0,12},{1,13},{2,14},{3,15},{4,0},{5,1},{6,2},{7,3},{8,4},{9,5},{1... | collective-permute-start | bytes 4718600 | tf_op jit(solution)/shard_map/ppermute | solution.py:30
  412.5 3.1 slice-start
Sparse Core Ops, SparseCore 0:
  49.6 362.8 all-gather.1

commit v5 on v2

--- a/solution.py
+++ b/solution.py
@@ -60,16 +60,20 @@
     live_rows = (offsets[None, :] < BASIS * mol_rows[:, None]).astype(jnp.float32).reshape(height)
     live_cols = (offsets[None, :] < BASIS * mol_cols[:, None]).astype(jnp.float32).reshape(width)
     density = (half_tri + mirrored) * live_rows[:, None] * live_cols[None, :]
-    row_panel = lax.all_gather(density, "col", axis=1, tiled=True)
+    group = upper.shape[0]
     col_panel = lax.all_gather(density, "row", axis=0, tiled=True)
-    group = upper.shape[0]
-    total = None
-    for step in range(STEPS):
-        start = (row_id + 2 * col_id + step) % row_count
-        left = lax.dynamic_slice_in_dim(row_panel, start * group, group, axis=1)
-        right = lax.dynamic_slice_in_dim(col_panel, start * group, group, axis=0)
-        term = jnp.dot(left, right, precision=lax.Precision.HIGHEST, preferred_element_type=jnp.float32)
-        total = term if total is None else total + term
+    start = (row_id + 2 * col_id) % row_count
+    picks = (start + jnp.arange(STEPS, dtype=jnp.int32)) % row_count
+    right = col_panel.reshape(row_count, group, width)[picks].reshape(STEPS * group, width)
+    window = jnp.where(parity == 0, right[:, :half_width], right[:, half_width:])
+    left_t = send(window, mirror_pairs(row_count, col_count, 0))
+    total = lax.dot_general(
+        left_t,
+        right,
+        (((0,), (0,)), ((), ())),
+        precision=lax.Precision.HIGHEST,
+        preferred_element_type=jnp.float32,
+    )
     return total
 
 

time: 414 us -> 655 us (1.58)
  the two profiles are of different devices: /device:TPU:57 before, /device:TPU:27 now
where the time goes in v5:
time: 655 us
  waiting for transfers between devices  591 us (90%)
  starting transfers between devices  23.7 us (4%)
  between operations  13.5 us (2%)
  local copies, waits for them, and re-layouts  11.9 us (2%)
  matrix products  7.35 us (1%)
  other arithmetic  7.25 us (1%)
    ppermute x3, waiting for transfers between devices, send(): return lax.ppermute(value, AXES, pairs)  395 us
    all_gather x1, waiting for transfers between devices, body(): col_panel = lax.all_gather(density, 'row', axis=0, tiled=True)  197 us
    ppermute x3, starting transfers between devices, send(): return lax.ppermute(value, AXES, pairs)  23.7 us
  transfers between devices with their start and end apart: 4, of which 4 were waited for; matrix products, arithmetic and copies ran while one was open for 0% of the time, Pallas kernels for 0%

profile of v5, /device:TPU:27, one launch (start us, length us, event | category | flops | bytes accessed | tf_op | source)
XLA Modules:
  0.0 655.0 jit_solution(16754100921097549021)
XLA Ops:
  6.5 0.0 copy-start.1
  6.5 0.0 all-gather.2.cloned.1.call-start
  6.5 0.8 compare_select_fusion.4
  7.4 0.1 copy.4
  7.5 0.2 mul.53
  7.7 0.4 mul.56
  8.1 1.2 copy.8
  9.3 0.1 mul.57
  9.5 14.4 %collective-permute-start = (f32[256,256]{1,0:T(8,128)S(1)}, f32[256,256]{1,0:T(8,128)S(1)}, u32[]{:S(2)}, u32[]{:S(2)}) collective-permute-start(f32[256,256]{1,0:T(8,128)S(1)} %get-tuple-element.5), channel_id=1, source_target_pairs={{0,0},{1,32},{2,64},{3,96},{4,128},{5,160},{6,192},{7,224},{8,256}... | collective-permute-start | bytes 786440 | tf_op jit(solution)/shard_map/ppermute | solution.py:15
  23.8 1.9 collective-permute-start.1
  25.8 0.7 dynamic-slice_multiply_fusion.1
  26.5 0.1 fusion.3
  26.6 0.7 dynamic-slice_multiply_fusion
  27.4 0.2 copy.7
  27.6 0.1 convert_bitcast_fusion
  27.6 38.6 %collective-permute-done = f32[256,256]{1,0:T(8,128)S(1)} collective-permute-done((f32[256,256]{1,0:T(8,128)S(1)}, f32[256,256]{1,0:T(8,128)S(1)}, u32[]{:S(2)}, u32[]{:S(2)}) %collective-permute-start) | collective-permute-done | bytes 262176 | tf_op jit(solution)/shard_map/ppermute | solution.py:15
  66.2 2.1 collective-permute-done.1
  68.3 0.0 copy-done.1
  68.3 0.9 fusion.2
  69.2 0.0 all-gather.2.cloned.1.call-update
  69.2 196.7 %all-gather.2.cloned.1.call-done = f32[8192,512]{1,0:T(8,128)} async-done(((f32[256,512]{1,0:T(8,128)}), f32[8192,512]{1,0:T(8,128)}) %all-gather.2.cloned.1.call-update) | async-done | bytes 16777232 | tf_op jit(solution)/shard_map/all_gather | solution.py:64
  265.9 9.7 %gather_fusion = f32[14,256,512]{2,1,0:T(8,128)} fusion(f32[32,256,512]{2,1,0:T(8,128)} %bitcast.31, s32[1024]{0:T(1024)S(1)} %pad_clamp_fusion), kind=kCustom, calls=%fused_computation | custom fusion | bytes 14680120 | tf_op jit(solution)/shard_map/gather | solution.py:67
  275.7 0.0 copy-start
  275.7 3.8 slice_select_fusion
  279.4 7.4 %collective-permute-start.2 = (f32[3584,256]{1,0:T(8,128)S(1)}, f32[3584,256]{1,0:T(8,128)S(1)}, u32[]{:S(2)}, u32[]{:S(2)}) collective-permute-start(f32[3584,256]{1,0:T(8,128)S(1)} %slice_select_fusion), channel_id=1, source_target_pairs={{0,0},{1,32},{2,64},{3,96},{4,128},{5,160},{6,192},{7,224},{8,256}... | collective-permute-start | bytes 11010056 | tf_op jit(solution)/shard_map/ppermute | solution.py:15
  286.8 354.0 %collective-permute-done.2 = f32[3584,256]{1,0:T(8,128)S(1)} collective-permute-done((f32[3584,256]{1,0:T(8,128)S(1)}, f32[3584,256]{1,0:T(8,128)S(1)}, u32[]{:S(2)}, u32[]{:S(2)}) %collective-permute-start.2) | collective-permute-done | bytes 3670048 | tf_op jit(solution)/shard_map/ppermute | solution.py:15
  640.8 0.0 copy-done
  640.8 7.4 %fusion.6 = f32[256,512]{1,0:T(8,128)} fusion(f32[3584,256]{1,0:T(8,128)S(1)} %collective-permute-done.2, f32[3584,512]{1,0:T(8,128)S(1)} %bitcast.29), kind=kOutput, calls=%fused_computation.26 | convolution fusion | flops 5637144576 | bytes 11534336 | tf_op jit(solution)/shard_map/dot_general | solution.py:70
  (6 shorter events, 0.1 us)
Async XLA Ops:
  6.5 61.7 %copy-start.1 = (f32[256,512]{1,0:T(8,128)S(1)}, f32[256,512]{1,0:T(8,128)}, u32[]{:S(2)}) copy-start(f32[256,512]{1,0:T(8,128)} %param.3) | copy-start | bytes 1572868
  6.5 259.4 %all-gather.2.cloned.1.call-start = ((), (), s32[]{:S(2)}) async-start(), calls=%async_computation | async-start | bytes 17301504 | tf_op jit(solution)/shard_map/all_gather | solution.py:64
  9.5 56.7 %collective-permute-start = (f32[256,256]{1,0:T(8,128)S(1)}, f32[256,256]{1,0:T(8,128)S(1)}, u32[]{:S(2)}, u32[]{:S(2)}) collective-permute-start(f32[256,256]{1,0:T(8,128)S(1)} %get-tuple-element.5), channel_id=1, source_target_pairs={{0,0},{1,32},{2,64},{3,96},{4,128},{5,160},{6,192},{7,224},{8,256}... | collective-permute-start | bytes 786440 | tf_op jit(solution)/shard_map/ppermute | solution.py:15
  23.8 44.4 %collective-permute-start.1 = (f32[256,256]{1,0:T(8,128)S(1)}, f32[256,256]{1,0:T(8,128)S(1)}, u32[]{:S(2)}, u32[]{:S(2)}) collective-permute-start(f32[256,256]{1,0:T(8,128)S(1)} %get-tuple-element.6), channel_id=1, source_target_pairs={{0,16},{1,48},{2,80},{3,112},{4,144},{5,176},{6,208},{7,240},{8,27... | collective-permute-start | bytes 786440 | tf_op jit(solution)/shard_map/ppermute | solution.py:15
  275.7 365.1 %copy-start = (f32[14,256,512]{2,1,0:T(8,128)S(1)}, f32[14,256,512]{2,1,0:T(8,128)}, u32[]{:S(2)}) copy-start(f32[14,256,512]{2,1,0:T(8,128)} %gather_fusion) | copy-start | bytes 22020100
  279.4 361.3 %collective-permute-start.2 = (f32[3584,256]{1,0:T(8,128)S(1)}, f32[3584,256]{1,0:T(8,128)S(1)}, u32[]{:S(2)}, u32[]{:S(2)}) collective-permute-start(f32[3584,256]{1,0:T(8,128)S(1)} %slice_select_fusion), channel_id=1, source_target_pairs={{0,0},{1,32},{2,64},{3,96},{4,128},{5,160},{6,192},{7,224},{8,256}... | collective-permute-start | bytes 11010056 | tf_op jit(solution)/shard_map/ppermute | solution.py:15
Sparse Core Ops, SparseCore 0:
  69.3 196.5 all-gather.1

commit v6 on v2

--- a/solution.py
+++ b/solution.py
@@ -60,7 +60,11 @@
     live_rows = (offsets[None, :] < BASIS * mol_rows[:, None]).astype(jnp.float32).reshape(height)
     live_cols = (offsets[None, :] < BASIS * mol_cols[:, None]).astype(jnp.float32).reshape(width)
     density = (half_tri + mirrored) * live_rows[:, None] * live_cols[None, :]
-    row_panel = lax.all_gather(density, "col", axis=1, tiled=True)
+    groups = [list(range(k, col_count, 2)) for k in range(2)]
+    own_cols = lax.all_gather(density, "col", axis=0, axis_index_groups=groups)
+    mate_cols = lax.ppermute(own_cols, "col", [(i, i ^ 1) for i in range(col_count)])
+    pair = jnp.where(col_id % 2 == 0, jnp.stack([own_cols, mate_cols], 1), jnp.stack([mate_cols, own_cols], 1))
+    row_panel = jnp.transpose(pair, (2, 0, 1, 3)).reshape(height, col_count * width)
     col_panel = lax.all_gather(density, "row", axis=0, tiled=True)
     group = upper.shape[0]
     total = None

time: 414 us -> 413 us (level)
  waiting for transfers between devices: 351 us -> 328 us
  other arithmetic: 4.43 us -> 14.3 us
  local copies, waits for them, and re-layouts: 2.19 us -> 11.3 us
    all_gather x1, waiting for transfers between devices: 202 us -> 173 us  [body(): col_panel = lax.all_gather(density, 'row', axis=0, tiled=True)]
    transpose x0 -> x1, other arithmetic: none -> 9.84 us  [body(): jnp.transpose(pair, (2, 0, 1, 3)).reshape(height, col_count * width)]
    transpose x0 -> x1, local copies, waits for them, and re-layouts: none -> 9.12 us  [body(): jnp.transpose(pair, (2, 0, 1, 3)).reshape(height, col_count * width)]
    ppermute x0 -> x1, waiting for transfers between devices: none -> 6.89 us  [body(): lax.ppermute(own_cols, 'col', [(i, i ^ 1) for i in range(col_count)])]
  transfers between devices with their start and end apart: 4 -> 5, of which waited for: 4 -> 5; matrix products, arithmetic and copies ran while one was open for 0% -> 5% of each run, Pallas kernels for 0% -> 0%
where the time goes in v6:
time: 413 us; the launch traced here: 409 us
  waiting for transfers between devices  328 us (79%)
  matrix products  25.4 us (6%)
  starting transfers between devices  16.5 us (4%)
  other arithmetic  14.3 us (3%)
  between operations  13.8 us (3%)
  local copies, waits for them, and re-layouts  11.3 us (3%)
    all_gather x1, waiting for transfers between devices, body(): col_panel = lax.all_gather(density, 'row', axis=0, tiled=True)  173 us
    all_gather x1, waiting for transfers between devices, body(): own_cols = lax.all_gather(density, 'col', axis=0, axis_index_groups=groups)  135 us
    dot_general x14, matrix products, body(): jnp.dot(left, right, precision=lax.Precision.HIGHEST, preferred_element_t...  25.4 us
    ppermute x2, starting transfers between devices, send(): return lax.ppermute(value, AXES, pairs)  13.3 us
    ppermute x2, waiting for transfers between devices, send(): return lax.ppermute(value, AXES, pairs)  12.4 us
    transpose x1, other arithmetic, body(): jnp.transpose(pair, (2, 0, 1, 3)).reshape(height, col_count * width)  9.84 us
    transpose x1, local copies, waits for them, and re-layouts, body(): jnp.transpose(pair, (2, 0, 1, 3)).reshape(height, col_count * width)  9.12 us
  transfers between devices with their start and end apart: 5, of which 5 were waited for; matrix products, arithmetic and copies ran while one was open for 5% of the time, Pallas kernels for 0%

profile of v6, /device:TPU:57, one launch (start us, length us, event | category | flops | bytes accessed | tf_op | source)
XLA Modules:
  0.0 409.3 jit_solution(1970077258149618220)
XLA Ops:
  6.5 0.7 compare_select_fusion.1
  7.4 0.2 mul.122
  7.6 0.4 mul.125
  8.0 1.2 copy.12
  9.4 9.6 %collective-permute-start = (f32[256,256]{1,0:T(8,128)S(1)}, f32[256,256]{1,0:T(8,128)S(1)}, u32[]{:S(2)}, u32[]{:S(2)}) collective-permute-start(f32[256,256]{1,0:T(8,128)S(1)} %get-tuple-element.5), channel_id=1, source_target_pairs={{0,0},{1,32},{2,64},{3,96},{4,128},{5,160},{6,192},{7,224},{8,256}... | collective-permute-start | bytes 786440 | tf_op jit(solution)/shard_map/ppermute | solution.py:15
  19.0 3.7 collective-permute-start.1
  22.8 0.7 dynamic-slice_multiply_fusion.1
  23.6 0.7 dynamic-slice_multiply_fusion
  24.6 3.6 collective-permute-done
  28.2 8.9 %collective-permute-done.1 = f32[256,256]{1,0:T(8,128)S(1)} collective-permute-done((f32[256,256]{1,0:T(8,128)S(1)}, f32[256,256]{1,0:T(8,128)S(1)}, u32[]{:S(2)}, u32[]{:S(2)}) %collective-permute-start.1) | collective-permute-done | bytes 262176 | tf_op jit(solution)/shard_map/ppermute | solution.py:15
  37.0 2.0 fusion.3
  39.1 0.7 all-gather.4.cloned.1.call-update
  39.8 134.6 %all-gather.6.cloned.1.call-done = f32[2048,512]{1,0:T(8,128)} async-done(((f32[256,512]{1,0:T(8,128)}), f32[2048,512]{1,0:T(8,128)}) %all-gather.6.cloned.1.call-update) | async-done | bytes 4194320 | tf_op jit(solution)/shard_map/all_gather | solution.py:64
  174.4 3.2 collective-permute-start.2
  177.8 6.9 %collective-permute-done.2 = f32[8,256,512]{2,1,0:T(8,128)} collective-permute-done((f32[8,256,512]{2,1,0:T(8,128)}, f32[8,256,512]{2,1,0:T(8,128)}, u32[]{:S(2)}, u32[]{:S(2)}) %collective-permute-start.2) | collective-permute-done | bytes 4194336 | tf_op jit(solution)/shard_map/ppermute | solution.py:65
  184.7 9.8 %fusion = f32[256,8,2,512]{3,0,1,2:T(8,128)} fusion(f32[8,1,256,512]{3,2,0,1:T(8,128)} %bitcast.9, f32[8,1,256,512]{3,2,0,1:T(8,128)} %bitcast.44, pred[]{:T(512)S(6)} %eq.34), kind=kLoop, calls=%fused_computation.1 | loop fusion | flops 6291456 | bytes 16777216 | tf_op jit(solution)/shard_map/transpose | solution.py:67
  194.5 9.1 %copy.13 = f32[256,8,2,512]{0,3,2,1:T(8,128)} copy(f32[256,8,2,512]{3,0,1,2:T(8,128)} %fusion) | data formatting | bytes 16777216 | tf_op jit(solution)/shard_map/transpose | solution.py:67
  203.6 173.3 %all-gather.4.cloned.1.call-done = f32[8192,512]{1,0:T(8,128)} async-done(((f32[256,512]{1,0:T(8,128)}), f32[8192,512]{1,0:T(8,128)}) %all-gather.4.cloned.1.call-update) | async-done | bytes 16777232 | tf_op jit(solution)/shard_map/all_gather | solution.py:68
  377.0 1.7 fusion.17
  378.7 1.8 convolution_add_fusion.12
  380.5 1.8 convolution_add_fusion.11
  382.3 1.8 convolution_add_fusion.10
  384.0 1.8 convolution_add_fusion.9
  385.8 1.8 convolution_add_fusion.8
  387.6 1.8 convolution_add_fusion.7
  389.3 1.8 convolution_add_fusion.6
  391.1 1.8 convolution_add_fusion.5
  392.9 1.8 convolution_add_fusion.4
  394.6 1.8 convolution_add_fusion.3
  396.4 1.8 convolution_add_fusion.2
  398.2 1.8 convolution_add_fusion.1
  399.9 2.6 convolution_add_fusion
  (12 shorter events, 0.6 us)
Async XLA Ops:
  6.5 167.9 %all-gather.6.cloned.1.call-start = ((), (), s32[]{:S(2)}) async-start(), calls=%async_computation.1 | async-start | bytes 4718592 | tf_op jit(solution)/shard_map/all_gather | solution.py:64
  9.4 18.8 %collective-permute-start = (f32[256,256]{1,0:T(8,128)S(1)}, f32[256,256]{1,0:T(8,128)S(1)}, u32[]{:S(2)}, u32[]{:S(2)}) collective-permute-start(f32[256,256]{1,0:T(8,128)S(1)} %get-tuple-element.5), channel_id=1, source_target_pairs={{0,0},{1,32},{2,64},{3,96},{4,128},{5,160},{6,192},{7,224},{8,256}... | collective-permute-start | bytes 786440 | tf_op jit(solution)/shard_map/ppermute | solution.py:15
  19.0 18.0 %collective-permute-start.1 = (f32[256,256]{1,0:T(8,128)S(1)}, f32[256,256]{1,0:T(8,128)S(1)}, u32[]{:S(2)}, u32[]{:S(2)}) collective-permute-start(f32[256,256]{1,0:T(8,128)S(1)} %get-tuple-element.6), channel_id=1, source_target_pairs={{0,16},{1,48},{2,80},{3,112},{4,144},{5,176},{6,208},{7,240},{8,27... | collective-permute-start | bytes 786440 | tf_op jit(solution)/shard_map/ppermute | solution.py:15
  39.0 338.0 %all-gather.4.cloned.1.call-start = ((), (), s32[]{:S(2)}) async-start(), calls=%async_computation | async-start | bytes 17301504 | tf_op jit(solution)/shard_map/all_gather | solution.py:68
  174.4 10.3 %collective-permute-start.2 = (f32[8,256,512]{2,1,0:T(8,128)}, f32[8,256,512]{2,1,0:T(8,128)}, u32[]{:S(2)}, u32[]{:S(2)}) collective-permute-start(f32[8,256,512]{2,1,0:T(8,128)} %bitcast.43), channel_id=1, source_target_pairs={{0,1},{1,0},{2,3},{3,2},{4,5},{5,4},{6,7},{7,6},{8,9},{9,8},{10,11... | collective-permute-start | bytes 12582920 | tf_op jit(solution)/shard_map/ppermute | solution.py:65
Sparse Core Ops, SparseCore 0:
  39.1 135.2 all-gather.5
  176.5 200.4 all-gather.3

commit v7 on v6

--- a/solution.py
+++ b/solution.py
@@ -67,13 +67,11 @@
     row_panel = jnp.transpose(pair, (2, 0, 1, 3)).reshape(height, col_count * width)
     col_panel = lax.all_gather(density, "row", axis=0, tiled=True)
     group = upper.shape[0]
-    total = None
-    for step in range(STEPS):
-        start = (row_id + 2 * col_id + step) % row_count
-        left = lax.dynamic_slice_in_dim(row_panel, start * group, group, axis=1)
-        right = lax.dynamic_slice_in_dim(col_panel, start * group, group, axis=0)
-        term = jnp.dot(left, right, precision=lax.Precision.HIGHEST, preferred_element_type=jnp.float32)
-        total = term if total is None else total + term
+    start = (row_id + 2 * col_id) % row_count
+    picks = (start + jnp.arange(STEPS, dtype=jnp.int32)) % row_count
+    left = row_panel.reshape(height, row_count, group)[:, picks].reshape(height, STEPS * group)
+    right = col_panel.reshape(row_count, group, width)[picks].reshape(STEPS * group, width)
+    total = jnp.dot(left, right, precision=lax.Precision.HIGHEST, preferred_element_type=jnp.float32)
     return total
 
 

time: 413 us -> 408 us (0.988)
  local copies, waits for them, and re-layouts: 11.3 us -> 36.2 us
  matrix products: 25.4 us -> 10.2 us
  waiting for transfers between devices: 328 us -> 314 us
    gather x0 -> x2, local copies, waits for them, and re-layouts: none -> 15.8 us  [the longest x1 9.71 us: body(): col_panel.reshape(row_count, group, width)[picks]]
    dot_general x14 -> x1, matrix products: 25.4 us -> 10.2 us  [body(): jnp.dot(left, right, precision=lax.Precision.HIGHEST, preferred_element_t...]
    all_gather x1, waiting for transfers between devices: 173 us -> 158 us  [body(): col_panel = lax.all_gather(density, 'row', axis=0, tiled=True)]
    another operation x0 -> x1, local copies, waits for them, and re-layouts: none -> 9.06 us  [body(): row_panel.reshape(height, row_count, group)[:, picks]]
  transfers between devices with their start and end apart: 5 -> 5, of which waited for: 5 -> 5; matrix products, arithmetic and copies ran while one was open for 5% -> 9% of each run, Pallas kernels for 0% -> 0%
where the time goes in v7:
time: 408 us; the launch traced here: 404 us
  waiting for transfers between devices  314 us (77%)
  local copies, waits for them, and re-layouts  36.2 us (9%)
  starting transfers between devices  16.5 us (4%)
  between operations  13.5 us (3%)
  other arithmetic  13.2 us (3%)
  matrix products  10.2 us (2%)
    all_gather x1, waiting for transfers between devices, body(): col_panel = lax.all_gather(density, 'row', axis=0, tiled=True)  158 us
    all_gather x1, waiting for transfers between devices, body(): own_cols = lax.all_gather(density, 'col', axis=0, axis_index_groups=groups)  137 us
    ppermute x2, starting transfers between devices, send(): return lax.ppermute(value, AXES, pairs)  13.3 us
    ppermute x2, waiting for transfers between devices, send(): return lax.ppermute(value, AXES, pairs)  11.3 us
    dot_general x1, matrix products, body(): jnp.dot(left, right, precision=lax.Precision.HIGHEST, preferred_element_t...  10.2 us
    transpose x1, other arithmetic, body(): jnp.transpose(pair, (2, 0, 1, 3)).reshape(height, col_count * width)  9.83 us
    gather x1, local copies, waits for them, and re-layouts, body(): col_panel.reshape(row_count, group, width)[picks]  9.71 us
    transpose x1, local copies, waits for them, and re-layouts, body(): jnp.transpose(pair, (2, 0, 1, 3)).reshape(height, col_count * width)  9.14 us
  transfers between devices with their start and end apart: 5, of which 5 were waited for; matrix products, arithmetic and copies ran while one was open for 9% of the time, Pallas kernels for 0%

profile of v7, /device:TPU:57, one launch (start us, length us, event | category | flops | bytes accessed | tf_op | source)
XLA Modules:
  0.0 404.0 jit_solution(14366523556312761099)
XLA Ops:
  6.5 0.0 copy-start
  6.5 0.0 all-gather.6.cloned.1.call-start
  6.5 1.3 copy.13
  7.9 0.8 compare_select_fusion.4
  8.6 0.1 copy.11
  8.7 0.2 mul.53
  8.9 0.4 mul.56
  9.4 0.1 mul.57
  9.5 11.4 %collective-permute-start.1 = (f32[256,256]{1,0:T(8,128)S(1)}, f32[256,256]{1,0:T(8,128)S(1)}, u32[]{:S(2)}, u32[]{:S(2)}) collective-permute-start(f32[256,256]{1,0:T(8,128)S(1)} %get-tuple-element.6), channel_id=1, source_target_pairs={{0,16},{1,48},{2,80},{3,112},{4,144},{5,176},{6,208},{7,240},{8,27... | collective-permute-start | bytes 786440 | tf_op jit(solution)/shard_map/ppermute | solution.py:15
  20.9 1.9 collective-permute-start
  22.9 0.7 dynamic-slice_multiply_fusion.1
  23.6 0.1 fusion.9
  23.7 0.7 dynamic-slice_multiply_fusion
  24.4 0.2 copy.16
  24.6 0.1 convert_bitcast_fusion
  24.7 5.0 %collective-permute-done.1 = f32[256,256]{1,0:T(8,128)S(1)} collective-permute-done((f32[256,256]{1,0:T(8,128)S(1)}, f32[256,256]{1,0:T(8,128)S(1)}, u32[]{:S(2)}, u32[]{:S(2)}) %collective-permute-start.1) | collective-permute-done | bytes 262176 | tf_op jit(solution)/shard_map/ppermute | solution.py:15
  29.7 6.4 %collective-permute-done = f32[256,256]{1,0:T(8,128)S(1)} collective-permute-done((f32[256,256]{1,0:T(8,128)S(1)}, f32[256,256]{1,0:T(8,128)S(1)}, u32[]{:S(2)}, u32[]{:S(2)}) %collective-permute-start) | collective-permute-done | bytes 262176 | tf_op jit(solution)/shard_map/ppermute | solution.py:15
  36.0 0.0 copy-done
  36.0 0.9 fusion.8
  37.0 0.0 all-gather.6.cloned.1.call-update
  37.0 0.0 all-gather.4.cloned.1.call-start
  37.0 0.7 all-gather.4.cloned.1.call-update
  37.7 137.0 %all-gather.6.cloned.1.call-done = f32[2048,512]{1,0:T(8,128)} async-done(((f32[256,512]{1,0:T(8,128)}), f32[2048,512]{1,0:T(8,128)}) %all-gather.6.cloned.1.call-update) | async-done | bytes 4194320 | tf_op jit(solution)/shard_map/all_gather | solution.py:64
  174.7 3.2 collective-permute-start.2
  177.9 7.1 %collective-permute-done.2 = f32[8,256,512]{2,1,0:T(8,128)} collective-permute-done((f32[8,256,512]{2,1,0:T(8,128)}, f32[8,256,512]{2,1,0:T(8,128)}, u32[]{:S(2)}, u32[]{:S(2)}) %collective-permute-start.2) | collective-permute-done | bytes 4194336 | tf_op jit(solution)/shard_map/ppermute | solution.py:65
  185.0 9.8 %fusion = f32[256,8,2,512]{3,0,1,2:T(8,128)} fusion(f32[8,1,256,512]{3,2,0,1:T(8,128)} %bitcast.9, f32[8,1,256,512]{3,2,0,1:T(8,128)} %bitcast.42, pred[]{:T(512)S(6)} %eq.11), kind=kLoop, calls=%fused_computation.3 | loop fusion | flops 6291456 | bytes 16777216 | tf_op jit(solution)/shard_map/transpose | solution.py:67
  194.8 9.1 %copy.14 = f32[256,8,2,512]{0,3,2,1:T(8,128)} copy(f32[256,8,2,512]{3,0,1,2:T(8,128)} %fusion) | data formatting | bytes 16777216 | tf_op jit(solution)/shard_map/transpose | solution.py:67
  204.0 9.1 %copy.15 = f32[256,32,256]{2,0,1:T(8,128)} copy(f32[256,32,256]{0,2,1:T(8,128)} %bitcast.39) | data formatting | bytes 16777216 | tf_op jit(solution)/shard_map/reshape;reshape | solution.py:72
  213.0 6.1 %gather_fusion = f32[14,256,256]{2,1,0:T(8,128)} fusion(f32[256,32,256]{2,0,1:T(8,128)} %copy.15, s32[1024]{0:T(1024)S(1)} %pad_clamp_fusion), kind=kCustom, calls=%fused_computation | custom fusion | bytes 7340088 | tf_op jit(solution)/shard_map/gather | solution.py:72
  219.1 158.2 %all-gather.4.cloned.1.call-done = f32[8192,512]{1,0:T(8,128)} async-done(((f32[256,512]{1,0:T(8,128)}), f32[8192,512]{1,0:T(8,128)}) %all-gather.4.cloned.1.call-update) | async-done | bytes 16777232 | tf_op jit(solution)/shard_map/all_gather | solution.py:68
  377.3 9.7 %gather_fusion.1 = f32[14,256,512]{2,1,0:T(8,128)} fusion(f32[32,256,512]{2,1,0:T(8,128)} %bitcast.43, s32[1024]{0:T(1024)S(1)} %pad_clamp_fusion), kind=kCustom, calls=%fused_computation.1 | custom fusion | bytes 14680120 | tf_op jit(solution)/shard_map/gather | solution.py:73
  387.0 10.2 %fusion.3 = f32[256,512]{1,0:T(8,128)} fusion(f32[14,256,512]{2,1,0:T(8,128)} %gather_fusion.1, f32[14,256,256]{2,1,0:T(8,128)} %gather_fusion), kind=kOutput, calls=%fused_computation.6 | convolution fusion | flops 5637144576 | bytes 11534336 | tf_op jit(solution)/shard_map/dot_general | solution.py:74
  (6 shorter events, 0.1 us)
Async XLA Ops:
  6.5 29.5 %copy-start = (f32[256,512]{1,0:T(8,128)S(1)}, f32[256,512]{1,0:T(8,128)}, u32[]{:S(2)}) copy-start(f32[256,512]{1,0:T(8,128)} %param.3) | copy-start | bytes 1572868
  6.5 168.2 %all-gather.6.cloned.1.call-start = ((), (), s32[]{:S(2)}) async-start(), calls=%async_computation.1 | async-start | bytes 4718592 | tf_op jit(solution)/shard_map/all_gather | solution.py:64
  9.5 20.2 %collective-permute-start.1 = (f32[256,256]{1,0:T(8,128)S(1)}, f32[256,256]{1,0:T(8,128)S(1)}, u32[]{:S(2)}, u32[]{:S(2)}) collective-permute-start(f32[256,256]{1,0:T(8,128)S(1)} %get-tuple-element.6), channel_id=1, source_target_pairs={{0,16},{1,48},{2,80},{3,112},{4,144},{5,176},{6,208},{7,240},{8,27... | collective-permute-start | bytes 786440 | tf_op jit(solution)/shard_map/ppermute | solution.py:15
  20.9 15.1 %collective-permute-start = (f32[256,256]{1,0:T(8,128)S(1)}, f32[256,256]{1,0:T(8,128)S(1)}, u32[]{:S(2)}, u32[]{:S(2)}) collective-permute-start(f32[256,256]{1,0:T(8,128)S(1)} %get-tuple-element.5), channel_id=1, source_target_pairs={{0,0},{1,32},{2,64},{3,96},{4,128},{5,160},{6,192},{7,224},{8,256}... | collective-permute-start | bytes 786440 | tf_op jit(solution)/shard_map/ppermute | solution.py:15
  37.0 340.3 %all-gather.4.cloned.1.call-start = ((), (), s32[]{:S(2)}) async-start(), calls=%async_computation | async-start | bytes 17301504 | tf_op jit(solution)/shard_map/all_gather | solution.py:68
  174.7 10.3 %collective-permute-start.2 = (f32[8,256,512]{2,1,0:T(8,128)}, f32[8,256,512]{2,1,0:T(8,128)}, u32[]{:S(2)}, u32[]{:S(2)}) collective-permute-start(f32[8,256,512]{2,1,0:T(8,128)} %bitcast.41), channel_id=1, source_target_pairs={{0,1},{1,0},{2,3},{3,2},{4,5},{5,4},{6,7},{7,6},{8,9},{9,8},{10,11... | collective-permute-start | bytes 12582920 | tf_op jit(solution)/shard_map/ppermute | solution.py:65
Sparse Core Ops, SparseCore 0:
  37.1 137.5 all-gather.5
  176.8 200.4 all-gather.3

commit v8 on v7

--- a/solution.py
+++ b/solution.py
@@ -22,6 +22,21 @@
             half = (r % 2) ^ flip
             target = (2 * c + half, r // 2)
             pairs.append((r * col_count + c, target[0] * col_count + target[1]))
+    return pairs
+
+
+def shift(value, axis, by):
+    length = lax.axis_size(axis)
+    return lax.ppermute(value, axis, [(i, (i - by) % length) for i in range(length)])
+
+
+def left_pairs(row_count, col_count, step):
+    pairs = []
+    for r in range(row_count):
+        half = (r + step) % 2
+        for c in range(col_count):
+            target = ((2 * c + half - r - step) % row_count) // 2
+            pairs.append((r * col_count + c, r * col_count + target))
     return pairs
 
 
@@ -60,16 +75,20 @@
     live_rows = (offsets[None, :] < BASIS * mol_rows[:, None]).astype(jnp.float32).reshape(height)
     live_cols = (offsets[None, :] < BASIS * mol_cols[:, None]).astype(jnp.float32).reshape(width)
     density = (half_tri + mirrored) * live_rows[:, None] * live_cols[None, :]
-    groups = [list(range(k, col_count, 2)) for k in range(2)]
-    own_cols = lax.all_gather(density, "col", axis=0, axis_index_groups=groups)
-    mate_cols = lax.ppermute(own_cols, "col", [(i, i ^ 1) for i in range(col_count)])
-    pair = jnp.where(col_id % 2 == 0, jnp.stack([own_cols, mate_cols], 1), jnp.stack([mate_cols, own_cols], 1))
-    row_panel = jnp.transpose(pair, (2, 0, 1, 3)).reshape(height, col_count * width)
+    dense_halves = density.reshape(height, 2, half_width)
+    parts = []
+    for step in range(2):
+        piece = jnp.where((row_id + step) % 2 == 0, dense_halves[:, 0], dense_halves[:, 1])
+        parts.append(send(piece, left_pairs(row_count, col_count, step)))
+    window = jnp.concatenate(parts, axis=1)
+    for _ in range(STEPS // 2 - 1):
+        window = shift(window, "col", 1)
+        parts.append(window)
+    left = jnp.concatenate(parts, axis=1)
     col_panel = lax.all_gather(density, "row", axis=0, tiled=True)
     group = upper.shape[0]
     start = (row_id + 2 * col_id) % row_count
     picks = (start + jnp.arange(STEPS, dtype=jnp.int32)) % row_count
-    left = row_panel.reshape(height, row_count, group)[:, picks].reshape(height, STEPS * group)
     right = col_panel.reshape(row_count, group, width)[picks].reshape(STEPS * group, width)
     total = jnp.dot(left, right, precision=lax.Precision.HIGHEST, preferred_element_type=jnp.float32)
     return total

time: 408 us -> 403 us (0.988)
  the two profiles are of different devices: /device:TPU:57 before, /device:TPU:495 now
where the time goes in v8:
time: 403 us
  starting transfers between devices  220 us (55%)
  waiting for transfers between devices  132 us (33%)
  local copies, waits for them, and re-layouts  19.7 us (5%)
  matrix products  15.7 us (4%)
  between operations  13.6 us (3%)
    ppermute x6, starting transfers between devices, shift(): lax.ppermute(value, axis, [(i, (i - by) % length) for i in range(length)])  206 us
    ppermute x6, waiting for transfers between devices, shift(): lax.ppermute(value, axis, [(i, (i - by) % length) for i in range(length)])  86.3 us
    ppermute x4, waiting for transfers between devices, send(): return lax.ppermute(value, AXES, pairs)  45.4 us
    dot_general x1, matrix products, body(): jnp.dot(left, right, precision=lax.Precision.HIGHEST, preferred_element_t...  15.7 us
    ppermute x4, starting transfers between devices, send(): return lax.ppermute(value, AXES, pairs)  14.3 us
    gather x1, local copies, waits for them, and re-layouts, body(): col_panel.reshape(row_count, group, width)[picks]  9.72 us
  transfers between devices with their start and end apart: 11, of which 10 were waited for; matrix products, arithmetic and copies ran while one was open for 2% of the time, Pallas kernels for 0%

profile of v8, /device:TPU:495, one launch (start us, length us, event | category | flops | bytes accessed | tf_op | source)
XLA Modules:
  0.0 402.8 jit_solution(7302264624088701598)
XLA Ops:
  6.5 0.8 compare_select_fusion.4
  8.0 1.2 copy.10
  9.4 2.9 collective-permute-start
  12.3 4.5 %collective-permute-start.1 = (f32[256,256]{1,0:T(8,128)S(1)}, f32[256,256]{1,0:T(8,128)S(1)}, u32[]{:S(2)}, u32[]{:S(2)}) collective-permute-start(f32[256,256]{1,0:T(8,128)S(1)} %get-tuple-element.8), channel_id=1, source_target_pairs={{0,16},{1,48},{2,80},{3,112},{4,144},{5,176},{6,208},{7,240},{8,27... | collective-permute-start | bytes 786440 | tf_op jit(solution)/shard_map/ppermute | solution.py:15
  17.4 20.7 %collective-permute-done = f32[256,256]{1,0:T(8,128)S(1)} collective-permute-done((f32[256,256]{1,0:T(8,128)S(1)}, f32[256,256]{1,0:T(8,128)S(1)}, u32[]{:S(2)}, u32[]{:S(2)}) %collective-permute-start) | collective-permute-done | bytes 262176 | tf_op jit(solution)/shard_map/ppermute | solution.py:15
  38.1 5.9 %collective-permute-done.1 = f32[256,256]{1,0:T(8,128)S(1)} collective-permute-done((f32[256,256]{1,0:T(8,128)S(1)}, f32[256,256]{1,0:T(8,128)S(1)}, u32[]{:S(2)}, u32[]{:S(2)}) %collective-permute-start.1) | collective-permute-done | bytes 262176 | tf_op jit(solution)/shard_map/ppermute | solution.py:15
  44.0 0.9 fusion.2
  45.0 1.2 copy.11
  46.3 1.9 collective-permute-start.3
  48.2 5.0 %collective-permute-start.2 = (f32[256,256]{0,1:T(8,128)S(1)}, f32[256,256]{0,1:T(8,128)S(1)}, u32[]{:S(2)}, u32[]{:S(2)}) collective-permute-start(f32[256,256]{0,1:T(8,128)S(1)} %get-tuple-element.6), channel_id=1, source_target_pairs={{0,0},{1,1},{2,2},{3,3},{4,4},{5,5},{6,6},{7,7},{8,8},{9,9},{10,10... | collective-permute-start | bytes 786440 | tf_op jit(solution)/shard_map/ppermute | solution.py:15
  53.2 6.9 %collective-permute-done.3 = f32[256,256]{0,1:T(8,128)S(1)} collective-permute-done((f32[256,256]{0,1:T(8,128)S(1)}, f32[256,256]{0,1:T(8,128)S(1)}, u32[]{:S(2)}, u32[]{:S(2)}) %collective-permute-start.3) | collective-permute-done | bytes 262176 | tf_op jit(solution)/shard_map/ppermute | solution.py:15
  60.1 11.8 %collective-permute-done.2 = f32[256,256]{0,1:T(8,128)S(1)} collective-permute-done((f32[256,256]{0,1:T(8,128)S(1)}, f32[256,256]{0,1:T(8,128)S(1)}, u32[]{:S(2)}, u32[]{:S(2)}) %collective-permute-start.2) | collective-permute-done | bytes 262176 | tf_op jit(solution)/shard_map/ppermute | solution.py:15
  72.0 190.8 %collective-permute-start.4 = (f32[256,512]{0,1:T(8,128)S(1)}, f32[256,512]{0,1:T(8,128)S(1)}, u32[]{:S(2)}, u32[]{:S(2)}) collective-permute-start(f32[256,512]{0,1:T(8,128)S(1)} %pad_maximum_fusion), channel_id=1, source_target_pairs={{0,15},{1,0},{2,1},{3,2},{4,3},{5,4},{6,5},{7,6},{8,7},{9,8},{10,9... | collective-permute-start | bytes 1572872 | tf_op jit(solution)/shard_map/ppermute | solution.py:30
  262.8 1.5 collective-permute-done.4
  264.3 7.1 %collective-permute-start.5 = (f32[256,512]{0,1:T(8,128)S(1)}, f32[256,512]{0,1:T(8,128)S(1)}, u32[]{:S(2)}, u32[]{:S(2)}) collective-permute-start(f32[256,512]{0,1:T(8,128)S(1)} %collective-permute-done.4), channel_id=1, source_target_pairs={{0,15},{1,0},{2,1},{3,2},{4,3},{5,4},{6,5},{7,6},{8,7},{9,8},{10,9... | collective-permute-start | bytes 1572872 | tf_op jit(solution)/shard_map/ppermute | solution.py:30
  271.4 29.0 %collective-permute-done.5 = f32[256,512]{0,1:T(8,128)S(1)} collective-permute-done((f32[256,512]{0,1:T(8,128)S(1)}, f32[256,512]{0,1:T(8,128)S(1)}, u32[]{:S(2)}, u32[]{:S(2)}) %collective-permute-start.5) | collective-permute-done | bytes 524320 | tf_op jit(solution)/shard_map/ppermute | solution.py:30
  300.4 1.9 collective-permute-start.6
  302.3 17.8 %collective-permute-done.6 = f32[256,512]{0,1:T(8,128)S(1)} collective-permute-done((f32[256,512]{0,1:T(8,128)S(1)}, f32[256,512]{0,1:T(8,128)S(1)}, u32[]{:S(2)}, u32[]{:S(2)}) %collective-permute-start.6) | collective-permute-done | bytes 524320 | tf_op jit(solution)/shard_map/ppermute | solution.py:30
  320.1 1.9 collective-permute-start.7
  322.0 14.6 %collective-permute-done.7 = f32[256,512]{0,1:T(8,128)S(1)} collective-permute-done((f32[256,512]{0,1:T(8,128)S(1)}, f32[256,512]{0,1:T(8,128)S(1)}, u32[]{:S(2)}, u32[]{:S(2)}) %collective-permute-start.7) | collective-permute-done | bytes 524320 | tf_op jit(solution)/shard_map/ppermute | solution.py:30
  336.6 1.9 collective-permute-start.8
  340.0 13.1 %collective-permute-done.8 = f32[256,512]{0,1:T(8,128)S(1)} collective-permute-done((f32[256,512]{0,1:T(8,128)S(1)}, f32[256,512]{0,1:T(8,128)S(1)}, u32[]{:S(2)}, u32[]{:S(2)}) %collective-permute-start.8) | collective-permute-done | bytes 524320 | tf_op jit(solution)/shard_map/ppermute | solution.py:30
  353.1 1.9 collective-permute-start.9
  355.0 0.9 constant_dynamic-update-slice_fusion.5
  355.9 0.9 constant_dynamic-update-slice_fusion.4
  356.8 0.9 constant_dynamic-update-slice_fusion.3
  357.7 0.8 constant_dynamic-update-slice_fusion.2
  358.5 0.9 constant_dynamic-update-slice_fusion.1
  359.4 10.3 %collective-permute-done.9 = f32[256,512]{0,1:T(8,128)S(1)} collective-permute-done((f32[256,512]{0,1:T(8,128)S(1)}, f32[256,512]{0,1:T(8,128)S(1)}, u32[]{:S(2)}, u32[]{:S(2)}) %collective-permute-start.9) | collective-permute-done | bytes 524320 | tf_op jit(solution)/shard_map/ppermute | solution.py:30
  369.6 0.8 constant_dynamic-update-slice_fusion
  370.5 9.7 %gather_fusion = f32[14,256,512]{2,1,0:T(8,128)} fusion(f32[32,256,512]{2,1,0:T(8,128)} %bitcast.35, s32[1024]{0:T(1024)S(1)} %pad_clamp_fusion), kind=kCustom, calls=%fused_computation | custom fusion | bytes 14680120 | tf_op jit(solution)/shard_map/gather | solution.py:92
  380.2 15.7 %fusion.6 = f32[256,512]{1,0:T(8,128)} fusion(f32[256,3584]{0,1:T(8,128)} %constant_dynamic-update-slice_fusion, f32[3584,512]{1,0:T(8,128)} %bitcast.33), kind=kOutput, calls=%fused_computation.36 | convolution fusion | flops 5637144576 | bytes 11534336 | tf_op jit(solution)/shard_map/dot_general | solution.py:93
  (26 shorter events, 2.9 us)
Async XLA Ops:
  6.5 10.3 %copy-start.1 = (s32[64]{0:T(128)S(1)}, s32[64]{0:T(128)}, u32[]{:S(2)}) copy-start(s32[64]{0:T(128)} %param.5) | copy-start | bytes 772
  6.5 363.9 %all-gather.2.cloned.1.call-start = ((), (), s32[]{:S(2)}) async-start(), calls=%async_computation | async-start | bytes 17301504 | tf_op jit(solution)/shard_map/all_gather | solution.py:88
  7.4 36.7 %copy-start = (f32[256,512]{1,0:T(8,128)S(1)}, f32[256,512]{1,0:T(8,128)}, u32[]{:S(2)}) copy-start(f32[256,512]{1,0:T(8,128)} %param.3) | copy-start | bytes 1572868
  9.4 28.7 %collective-permute-start = (f32[256,256]{1,0:T(8,128)S(1)}, f32[256,256]{1,0:T(8,128)S(1)}, u32[]{:S(2)}, u32[]{:S(2)}) collective-permute-start(f32[256,256]{1,0:T(8,128)S(1)} %get-tuple-element.7), channel_id=1, source_target_pairs={{0,0},{1,32},{2,64},{3,96},{4,128},{5,160},{6,192},{7,224},{8,256}... | collective-permute-start | bytes 786440 | tf_op jit(solution)/shard_map/ppermute | solution.py:15
  12.3 31.8 %collective-permute-start.1 = (f32[256,256]{1,0:T(8,128)S(1)}, f32[256,256]{1,0:T(8,128)S(1)}, u32[]{:S(2)}, u32[]{:S(2)}) collective-permute-start(f32[256,256]{1,0:T(8,128)S(1)} %get-tuple-element.8), channel_id=1, source_target_pairs={{0,16},{1,48},{2,80},{3,112},{4,144},{5,176},{6,208},{7,240},{8,27... | collective-permute-start | bytes 786440 | tf_op jit(solution)/shard_map/ppermute | solution.py:15
  46.3 13.8 %collective-permute-start.3 = (f32[256,256]{0,1:T(8,128)S(1)}, f32[256,256]{0,1:T(8,128)S(1)}, u32[]{:S(2)}, u32[]{:S(2)}) collective-permute-start(f32[256,256]{0,1:T(8,128)S(1)} %get-tuple-element.5), channel_id=1, source_target_pairs={{0,0},{1,1},{2,2},{3,3},{4,4},{5,5},{6,6},{7,7},{8,8},{9,9},{10,10... | collective-permute-start | bytes 786440 | tf_op jit(solution)/shard_map/ppermute | solution.py:15
  48.2 23.7 %collective-permute-start.2 = (f32[256,256]{0,1:T(8,128)S(1)}, f32[256,256]{0,1:T(8,128)S(1)}, u32[]{:S(2)}, u32[]{:S(2)}) collective-permute-start(f32[256,256]{0,1:T(8,128)S(1)} %get-tuple-element.6), channel_id=1, source_target_pairs={{0,0},{1,1},{2,2},{3,3},{4,4},{5,5},{6,6},{7,7},{8,8},{9,9},{10,10... | collective-permute-start | bytes 786440 | tf_op jit(solution)/shard_map/ppermute | solution.py:15
  72.0 192.4 %collective-permute-start.4 = (f32[256,512]{0,1:T(8,128)S(1)}, f32[256,512]{0,1:T(8,128)S(1)}, u32[]{:S(2)}, u32[]{:S(2)}) collective-permute-start(f32[256,512]{0,1:T(8,128)S(1)} %pad_maximum_fusion), channel_id=1, source_target_pairs={{0,15},{1,0},{2,1},{3,2},{4,3},{5,4},{6,5},{7,6},{8,7},{9,8},{10,9... | collective-permute-start | bytes 1572872 | tf_op jit(solution)/shard_map/ppermute | solution.py:30
  264.3 36.1 %collective-permute-start.5 = (f32[256,512]{0,1:T(8,128)S(1)}, f32[256,512]{0,1:T(8,128)S(1)}, u32[]{:S(2)}, u32[]{:S(2)}) collective-permute-start(f32[256,512]{0,1:T(8,128)S(1)} %collective-permute-done.4), channel_id=1, source_target_pairs={{0,15},{1,0},{2,1},{3,2},{4,3},{5,4},{6,5},{7,6},{8,7},{9,8},{10,9... | collective-permute-start | bytes 1572872 | tf_op jit(solution)/shard_map/ppermute | solution.py:30
  300.4 19.7 %collective-permute-start.6 = (f32[256,512]{0,1:T(8,128)S(1)}, f32[256,512]{0,1:T(8,128)S(1)}, u32[]{:S(2)}, u32[]{:S(2)}) collective-permute-start(f32[256,512]{0,1:T(8,128)S(1)} %collective-permute-done.5), channel_id=1, source_target_pairs={{0,15},{1,0},{2,1},{3,2},{4,3},{5,4},{6,5},{7,6},{8,7},{9,8},{10,9... | collective-permute-start | bytes 1572872 | tf_op jit(solution)/shard_map/ppermute | solution.py:30
  320.1 16.5 %collective-permute-start.7 = (f32[256,512]{0,1:T(8,128)S(1)}, f32[256,512]{0,1:T(8,128)S(1)}, u32[]{:S(2)}, u32[]{:S(2)}) collective-permute-start(f32[256,512]{0,1:T(8,128)S(1)} %collective-permute-done.6), channel_id=1, source_target_pairs={{0,15},{1,0},{2,1},{3,2},{4,3},{5,4},{6,5},{7,6},{8,7},{9,8},{10,9... | collective-permute-start | bytes 1572872 | tf_op jit(solution)/shard_map/ppermute | solution.py:30
  336.6 16.5 %collective-permute-start.8 = (f32[256,512]{0,1:T(8,128)S(1)}, f32[256,512]{0,1:T(8,128)S(1)}, u32[]{:S(2)}, u32[]{:S(2)}) collective-permute-start(f32[256,512]{0,1:T(8,128)S(1)} %collective-permute-done.7), channel_id=1, source_target_pairs={{0,15},{1,0},{2,1},{3,2},{4,3},{5,4},{6,5},{7,6},{8,7},{9,8},{10,9... | collective-permute-start | bytes 1572872 | tf_op jit(solution)/shard_map/ppermute | solution.py:30
  353.1 16.5 %collective-permute-start.9 = (f32[256,512]{0,1:T(8,128)S(1)}, f32[256,512]{0,1:T(8,128)S(1)}, u32[]{:S(2)}, u32[]{:S(2)}) collective-permute-start(f32[256,512]{0,1:T(8,128)S(1)} %collective-permute-done.8), channel_id=1, source_target_pairs={{0,15},{1,0},{2,1},{3,2},{4,3},{5,4},{6,5},{7,6},{8,7},{9,8},{10,9... | collective-permute-start | bytes 1572872 | tf_op jit(solution)/shard_map/ppermute | solution.py:30
Sparse Core Ops, SparseCore 0:
  45.1 213.3 all-gather.1

commit v9 on v8

--- a/solution.py
+++ b/solution.py
@@ -76,14 +76,22 @@
     live_cols = (offsets[None, :] < BASIS * mol_cols[:, None]).astype(jnp.float32).reshape(width)
     density = (half_tri + mirrored) * live_rows[:, None] * live_cols[None, :]
     dense_halves = density.reshape(height, 2, half_width)
+    middle = STEPS // 2 - 1
     parts = []
-    for step in range(2):
+    for step in (middle, middle + 1):
         piece = jnp.where((row_id + step) % 2 == 0, dense_halves[:, 0], dense_halves[:, 1])
         parts.append(send(piece, left_pairs(row_count, col_count, step)))
-    window = jnp.concatenate(parts, axis=1)
-    for _ in range(STEPS // 2 - 1):
-        window = shift(window, "col", 1)
-        parts.append(window)
+    centre = jnp.concatenate(parts, axis=1)
+    ahead = centre
+    behind = centre
+    after = []
+    before = []
+    for _ in range(middle // 2):
+        ahead = shift(ahead, "col", 1)
+        behind = shift(behind, "col", -1)
+        after.append(ahead)
+        before.insert(0, behind)
+    parts = before + [centre] + after
     left = jnp.concatenate(parts, axis=1)
     col_panel = lax.all_gather(density, "row", axis=0, tiled=True)
     group = upper.shape[0]

time: 403 us -> 364 us (0.903)
  the two profiles are of different devices: /device:TPU:495 before, /device:TPU:55 now
where the time goes in v9:
time: 364 us
  starting transfers between devices  232 us (64%)
  waiting for transfers between devices  85.8 us (24%)
  local copies, waits for them, and re-layouts  20 us (5%)
  between operations  13.6 us (4%)
  matrix products  10.2 us (3%)
    ppermute x6, starting transfers between devices, shift(): lax.ppermute(value, axis, [(i, (i - by) % length) for i in range(length)])  206 us
    ppermute x6, waiting for transfers between devices, shift(): lax.ppermute(value, axis, [(i, (i - by) % length) for i in range(length)])  47.2 us
    ppermute x4, waiting for transfers between devices, send(): return lax.ppermute(value, AXES, pairs)  38.5 us
    ppermute x4, starting transfers between devices, send(): return lax.ppermute(value, AXES, pairs)  25.9 us
    dot_general x1, matrix products, body(): jnp.dot(left, right, precision=lax.Precision.HIGHEST, preferred_element_t...  10.2 us
    gather x1, local copies, waits for them, and re-layouts, body(): col_panel.reshape(row_count, group, width)[picks]  9.72 us
  transfers between devices with their start and end apart: 11, of which 8 were waited for; matrix products, arithmetic and copies ran while one was open for 3% of the time, Pallas kernels for 0%

profile of v9, /device:TPU:55, one launch (start us, length us, event | category | flops | bytes accessed | tf_op | source)
XLA Modules:
  0.0 363.9 jit_solution(15662841891111568945)
XLA Ops:
  6.5 0.8 compare_select_fusion.4
  8.0 1.2 copy.11
  9.4 11.2 %collective-permute-start = (f32[256,256]{1,0:T(8,128)S(1)}, f32[256,256]{1,0:T(8,128)S(1)}, u32[]{:S(2)}, u32[]{:S(2)}) collective-permute-start(f32[256,256]{1,0:T(8,128)S(1)} %get-tuple-element.8), channel_id=1, source_target_pairs={{0,0},{1,32},{2,64},{3,96},{4,128},{5,160},{6,192},{7,224},{8,256}... | collective-permute-start | bytes 786440 | tf_op jit(solution)/shard_map/ppermute | solution.py:15
  20.7 1.9 collective-permute-start.1
  23.2 16.9 %collective-permute-done = f32[256,256]{1,0:T(8,128)S(1)} collective-permute-done((f32[256,256]{1,0:T(8,128)S(1)}, f32[256,256]{1,0:T(8,128)S(1)}, u32[]{:S(2)}, u32[]{:S(2)}) %collective-permute-start) | collective-permute-done | bytes 262176 | tf_op jit(solution)/shard_map/ppermute | solution.py:15
  40.1 4.7 %collective-permute-done.1 = f32[256,256]{1,0:T(8,128)S(1)} collective-permute-done((f32[256,256]{1,0:T(8,128)S(1)}, f32[256,256]{1,0:T(8,128)S(1)}, u32[]{:S(2)}, u32[]{:S(2)}) %collective-permute-start.1) | collective-permute-done | bytes 262176 | tf_op jit(solution)/shard_map/ppermute | solution.py:15
  44.8 0.9 fusion.2
  45.7 1.4 reshape.121
  47.6 1.9 collective-permute-start.2
  49.6 10.8 %collective-permute-start.3 = (f32[256,256]{1,0:T(8,128)S(1)}, f32[256,256]{1,0:T(8,128)S(1)}, u32[]{:S(2)}, u32[]{:S(2)}) collective-permute-start(f32[256,256]{1,0:T(8,128)S(1)} %bitcast.38), channel_id=1, source_target_pairs={{0,13},{1,14},{2,15},{3,0},{4,1},{5,2},{6,3},{7,4},{8,5},{9,6},{10... | collective-permute-start | bytes 786440 | tf_op jit(solution)/shard_map/ppermute | solution.py:15
  60.3 14.2 %collective-permute-done.2 = f32[256,256]{1,0:T(8,128)S(1)} collective-permute-done((f32[256,256]{1,0:T(8,128)S(1)}, f32[256,256]{1,0:T(8,128)S(1)}, u32[]{:S(2)}, u32[]{:S(2)}) %collective-permute-start.2) | collective-permute-done | bytes 262176 | tf_op jit(solution)/shard_map/ppermute | solution.py:15
  74.5 2.8 collective-permute-done.3
  77.3 9.0 %collective-permute-start.4 = (f32[256,512]{1,0:T(8,128)S(1)}, f32[256,512]{1,0:T(8,128)S(1)}, u32[]{:S(2)}, u32[]{:S(2)}) collective-permute-start(f32[256,512]{1,0:T(8,128)S(1)} %constant_dynamic-update-slice_fusion), channel_id=1, source_target_pairs={{0,1},{1,2},{2,3},{3,4},{4,5},{5,6},{6,7},{7,8},{8,9},{9,10},{10,1... | collective-permute-start | bytes 1572872 | tf_op jit(solution)/shard_map/ppermute | solution.py:30
  86.4 3.5 collective-permute-start.7
  89.9 8.2 %collective-permute-done.4 = f32[256,512]{1,0:T(8,128)S(1)} collective-permute-done((f32[256,512]{1,0:T(8,128)S(1)}, f32[256,512]{1,0:T(8,128)S(1)}, u32[]{:S(2)}, u32[]{:S(2)}) %collective-permute-start.4) | collective-permute-done | bytes 524320 | tf_op jit(solution)/shard_map/ppermute | solution.py:30
  98.1 179.8 %collective-permute-start.5 = (f32[256,512]{1,0:T(8,128)S(1)}, f32[256,512]{1,0:T(8,128)S(1)}, u32[]{:S(2)}, u32[]{:S(2)}) collective-permute-start(f32[256,512]{1,0:T(8,128)S(1)} %collective-permute-done.4), channel_id=1, source_target_pairs={{0,1},{1,2},{2,3},{3,4},{4,5},{5,6},{6,7},{7,8},{8,9},{9,10},{10,1... | collective-permute-start | bytes 1572872 | tf_op jit(solution)/shard_map/ppermute | solution.py:30
  277.9 25.4 %collective-permute-done.7 = f32[256,512]{1,0:T(8,128)S(1)} collective-permute-done((f32[256,512]{1,0:T(8,128)S(1)}, f32[256,512]{1,0:T(8,128)S(1)}, u32[]{:S(2)}, u32[]{:S(2)}) %collective-permute-start.7) | collective-permute-done | bytes 524320 | tf_op jit(solution)/shard_map/ppermute | solution.py:30
  303.3 1.9 collective-permute-start.8
  305.2 9.7 %collective-permute-start.6 = (f32[256,512]{1,0:T(8,128)S(1)}, f32[256,512]{1,0:T(8,128)S(1)}, u32[]{:S(2)}, u32[]{:S(2)}) collective-permute-start(f32[256,512]{1,0:T(8,128)S(1)} %collective-permute-done.5), channel_id=1, source_target_pairs={{0,1},{1,2},{2,3},{3,4},{4,5},{5,6},{6,7},{7,8},{8,9},{9,10},{10,1... | collective-permute-start | bytes 1572872 | tf_op jit(solution)/shard_map/ppermute | solution.py:30
  314.9 4.9 %collective-permute-done.8 = f32[256,512]{1,0:T(8,128)S(1)} collective-permute-done((f32[256,512]{1,0:T(8,128)S(1)}, f32[256,512]{1,0:T(8,128)S(1)}, u32[]{:S(2)}, u32[]{:S(2)}) %collective-permute-start.8) | collective-permute-done | bytes 524320 | tf_op jit(solution)/shard_map/ppermute | solution.py:30
  319.8 1.9 collective-permute-start.9
  321.7 0.9 constant_dynamic-update-slice_fusion.9
  322.6 0.9 constant_dynamic-update-slice_fusion.8
  323.5 0.9 constant_dynamic-update-slice_fusion.7
  324.4 0.7 constant_dynamic-update-slice_fusion.6
  325.1 0.7 constant_dynamic-update-slice_fusion.5
  325.8 0.9 constant_dynamic-update-slice_fusion.4
  326.7 0.8 constant_dynamic-update-slice_fusion.3
  327.5 8.8 %collective-permute-done.9 = f32[256,512]{1,0:T(8,128)S(1)} collective-permute-done((f32[256,512]{1,0:T(8,128)S(1)}, f32[256,512]{1,0:T(8,128)S(1)}, u32[]{:S(2)}, u32[]{:S(2)}) %collective-permute-start.9) | collective-permute-done | bytes 524320 | tf_op jit(solution)/shard_map/ppermute | solution.py:30
  336.3 0.9 constant_dynamic-update-slice_fusion.2
  337.2 9.7 %gather_fusion = f32[14,256,512]{2,1,0:T(8,128)} fusion(f32[32,256,512]{2,1,0:T(8,128)} %bitcast.35, s32[1024]{0:T(1024)S(1)} %pad_clamp_fusion), kind=kCustom, calls=%fused_computation | custom fusion | bytes 14680120 | tf_op jit(solution)/shard_map/gather | solution.py:100
  346.9 10.2 %fusion.7 = f32[256,512]{1,0:T(8,128)} fusion(f32[256,3584]{1,0:T(8,128)} %constant_dynamic-update-slice_fusion.2, f32[3584,512]{1,0:T(8,128)} %bitcast.33), kind=kOutput, calls=%fused_computation.39 | convolution fusion | flops 5637144576 | bytes 11534336 | tf_op jit(solution)/shard_map/dot_general | solution.py:101
  (29 shorter events, 2.0 us)
Async XLA Ops:
  6.5 16.1 %copy-start.1 = (s32[64]{0:T(128)S(1)}, s32[64]{0:T(128)}, u32[]{:S(2)}) copy-start(s32[64]{0:T(128)} %param.5) | copy-start | bytes 772
  6.5 330.6 %all-gather.2.cloned.1.call-start = ((), (), s32[]{:S(2)}) async-start(), calls=%async_computation | async-start | bytes 17301504 | tf_op jit(solution)/shard_map/all_gather | solution.py:96
  7.4 37.4 %copy-start = (f32[256,512]{1,0:T(8,128)S(1)}, f32[256,512]{1,0:T(8,128)}, u32[]{:S(2)}) copy-start(f32[256,512]{1,0:T(8,128)} %param.3) | copy-start | bytes 1572868
  9.4 30.7 %collective-permute-start = (f32[256,256]{1,0:T(8,128)S(1)}, f32[256,256]{1,0:T(8,128)S(1)}, u32[]{:S(2)}, u32[]{:S(2)}) collective-permute-start(f32[256,256]{1,0:T(8,128)S(1)} %get-tuple-element.8), channel_id=1, source_target_pairs={{0,0},{1,32},{2,64},{3,96},{4,128},{5,160},{6,192},{7,224},{8,256}... | collective-permute-start | bytes 786440 | tf_op jit(solution)/shard_map/ppermute | solution.py:15
  20.7 24.1 %collective-permute-start.1 = (f32[256,256]{1,0:T(8,128)S(1)}, f32[256,256]{1,0:T(8,128)S(1)}, u32[]{:S(2)}, u32[]{:S(2)}) collective-permute-start(f32[256,256]{1,0:T(8,128)S(1)} %get-tuple-element.9), channel_id=1, source_target_pairs={{0,16},{1,48},{2,80},{3,112},{4,144},{5,176},{6,208},{7,240},{8,27... | collective-permute-start | bytes 786440 | tf_op jit(solution)/shard_map/ppermute | solution.py:15
  47.6 26.9 %collective-permute-start.2 = (f32[256,256]{1,0:T(8,128)S(1)}, f32[256,256]{1,0:T(8,128)S(1)}, u32[]{:S(2)}, u32[]{:S(2)}) collective-permute-start(f32[256,256]{1,0:T(8,128)S(1)} %fusion.3), channel_id=1, source_target_pairs={{0,13},{1,14},{2,15},{3,0},{4,1},{5,2},{6,3},{7,4},{8,5},{9,6},{10... | collective-permute-start | bytes 786440 | tf_op jit(solution)/shard_map/ppermute | solution.py:15
  49.6 27.7 %collective-permute-start.3 = (f32[256,256]{1,0:T(8,128)S(1)}, f32[256,256]{1,0:T(8,128)S(1)}, u32[]{:S(2)}, u32[]{:S(2)}) collective-permute-start(f32[256,256]{1,0:T(8,128)S(1)} %bitcast.38), channel_id=1, source_target_pairs={{0,13},{1,14},{2,15},{3,0},{4,1},{5,2},{6,3},{7,4},{8,5},{9,6},{10... | collective-permute-start | bytes 786440 | tf_op jit(solution)/shard_map/ppermute | solution.py:15
  77.3 20.8 %collective-permute-start.4 = (f32[256,512]{1,0:T(8,128)S(1)}, f32[256,512]{1,0:T(8,128)S(1)}, u32[]{:S(2)}, u32[]{:S(2)}) collective-permute-start(f32[256,512]{1,0:T(8,128)S(1)} %constant_dynamic-update-slice_fusion), channel_id=1, source_target_pairs={{0,1},{1,2},{2,3},{3,4},{4,5},{5,6},{6,7},{7,8},{8,9},{9,10},{10,1... | collective-permute-start | bytes 1572872 | tf_op jit(solution)/shard_map/ppermute | solution.py:30
  86.4 216.9 %collective-permute-start.7 = (f32[256,512]{1,0:T(8,128)S(1)}, f32[256,512]{1,0:T(8,128)S(1)}, u32[]{:S(2)}, u32[]{:S(2)}) collective-permute-start(f32[256,512]{1,0:T(8,128)S(1)} %constant_dynamic-update-slice_fusion), channel_id=1, source_target_pairs={{0,15},{1,0},{2,1},{3,2},{4,3},{5,4},{6,5},{7,6},{8,7},{9,8},{10,9... | collective-permute-start | bytes 1572872 | tf_op jit(solution)/shard_map/ppermute | solution.py:30
  98.1 207.1 %collective-permute-start.5 = (f32[256,512]{1,0:T(8,128)S(1)}, f32[256,512]{1,0:T(8,128)S(1)}, u32[]{:S(2)}, u32[]{:S(2)}) collective-permute-start(f32[256,512]{1,0:T(8,128)S(1)} %collective-permute-done.4), channel_id=1, source_target_pairs={{0,1},{1,2},{2,3},{3,4},{4,5},{5,6},{6,7},{7,8},{8,9},{9,10},{10,1... | collective-permute-start | bytes 1572872 | tf_op jit(solution)/shard_map/ppermute | solution.py:30
  303.3 16.5 %collective-permute-start.8 = (f32[256,512]{1,0:T(8,128)S(1)}, f32[256,512]{1,0:T(8,128)S(1)}, u32[]{:S(2)}, u32[]{:S(2)}) collective-permute-start(f32[256,512]{1,0:T(8,128)S(1)} %collective-permute-done.7), channel_id=1, source_target_pairs={{0,15},{1,0},{2,1},{3,2},{4,3},{5,4},{6,5},{7,6},{8,7},{9,8},{10,9... | collective-permute-start | bytes 1572872 | tf_op jit(solution)/shard_map/ppermute | solution.py:30
  305.2 16.5 %collective-permute-start.6 = (f32[256,512]{1,0:T(8,128)S(1)}, f32[256,512]{1,0:T(8,128)S(1)}, u32[]{:S(2)}, u32[]{:S(2)}) collective-permute-start(f32[256,512]{1,0:T(8,128)S(1)} %collective-permute-done.5), channel_id=1, source_target_pairs={{0,1},{1,2},{2,3},{3,4},{4,5},{5,6},{6,7},{7,8},{8,9},{9,10},{10,1... | collective-permute-start | bytes 1572872 | tf_op jit(solution)/shard_map/ppermute | solution.py:30
  319.8 16.5 %collective-permute-start.9 = (f32[256,512]{1,0:T(8,128)S(1)}, f32[256,512]{1,0:T(8,128)S(1)}, u32[]{:S(2)}, u32[]{:S(2)}) collective-permute-start(f32[256,512]{1,0:T(8,128)S(1)} %collective-permute-done.8), channel_id=1, source_target_pairs={{0,15},{1,0},{2,1},{3,2},{4,3},{5,4},{6,5},{7,6},{8,7},{9,8},{10,9... | collective-permute-start | bytes 1572872 | tf_op jit(solution)/shard_map/ppermute | solution.py:30
Sparse Core Ops, SparseCore 0:
  45.8 254.2 all-gather.1

commit v10 on v9

--- a/solution.py
+++ b/solution.py
@@ -40,6 +40,15 @@
     return pairs
 
 
+def right_pairs(row_count, col_count, step):
+    pairs = []
+    for r in range(row_count):
+        for c in range(col_count):
+            target = (r - 2 * c - step) % row_count
+            pairs.append((r * col_count + c, target * col_count + c))
+    return pairs
+
+
 def body(upper, occupied, tile_molecules):
     row_id = lax.axis_index("row")
     col_id = lax.axis_index("col")
@@ -75,29 +84,24 @@
     live_rows = (offsets[None, :] < BASIS * mol_rows[:, None]).astype(jnp.float32).reshape(height)
     live_cols = (offsets[None, :] < BASIS * mol_cols[:, None]).astype(jnp.float32).reshape(width)
     density = (half_tri + mirrored) * live_rows[:, None] * live_cols[None, :]
-    dense_halves = density.reshape(height, 2, half_width)
+    group = upper.shape[0]
+    row_panel = lax.all_gather(density, "col", axis=1, tiled=True)
     middle = STEPS // 2 - 1
-    parts = []
-    for step in (middle, middle + 1):
-        piece = jnp.where((row_id + step) % 2 == 0, dense_halves[:, 0], dense_halves[:, 1])
-        parts.append(send(piece, left_pairs(row_count, col_count, step)))
-    centre = jnp.concatenate(parts, axis=1)
+    centre = send(density, right_pairs(row_count, col_count, middle))
     ahead = centre
     behind = centre
     after = []
     before = []
-    for _ in range(middle // 2):
-        ahead = shift(ahead, "col", 1)
-        behind = shift(behind, "col", -1)
+    for _ in range(STEPS - 1 - middle):
+        ahead = shift(ahead, "row", 1)
         after.append(ahead)
+    for _ in range(middle):
+        behind = shift(behind, "row", -1)
         before.insert(0, behind)
-    parts = before + [centre] + after
-    left = jnp.concatenate(parts, axis=1)
-    col_panel = lax.all_gather(density, "row", axis=0, tiled=True)
-    group = upper.shape[0]
+    right = jnp.concatenate(before + [centre] + after, axis=0)
     start = (row_id + 2 * col_id) % row_count
     picks = (start + jnp.arange(STEPS, dtype=jnp.int32)) % row_count
-    right = col_panel.reshape(row_count, group, width)[picks].reshape(STEPS * group, width)
+    left = row_panel.reshape(height, row_count, group)[:, picks].reshape(height, STEPS * group)
     total = jnp.dot(left, right, precision=lax.Precision.HIGHEST, preferred_element_type=jnp.float32)
     return total
 

time: 364 us -> 352 us (0.967)
  the two profiles are of different devices: /device:TPU:55 before, /device:TPU:14 now
where the time goes in v10:
time: 352 us; the launch traced here: 351 us
  waiting for transfers between devices  200 us (57%)
  starting transfers between devices  67.7 us (19%)
  local copies, waits for them, and re-layouts  50.1 us (14%)
  matrix products  15.7 us (4%)
  between operations  13.7 us (4%)
    ppermute x3, waiting for transfers between devices, send(): return lax.ppermute(value, AXES, pairs)  109 us
    ppermute x13, waiting for transfers between devices, shift(): lax.ppermute(value, axis, [(i, (i - by) % length) for i in range(length)])  90.9 us
    ppermute x13, starting transfers between devices, shift(): lax.ppermute(value, axis, [(i, (i - by) % length) for i in range(length)])  52.6 us
    unnamed x25, local copies, waits for them, and re-layouts  19.3 us
    dot_general x1, matrix products, body(): jnp.dot(left, right, precision=lax.Precision.HIGHEST, preferred_element_t...  15.7 us
    ppermute x3, starting transfers between devices, send(): return lax.ppermute(value, AXES, pairs)  15 us
    gather x2, local copies, waits for them, and re-layouts, body(): row_panel.reshape(height, row_count, group)[:, picks]  11.1 us
    reshape x1, local copies, waits for them, and re-layouts, body(): row_panel.reshape(height, row_count, group)[:, picks]  8.99 us
  transfers between devices with their start and end apart: 17, of which 9 were waited for; matrix products, arithmetic and copies ran while one was open for 6% of the time, Pallas kernels for 0%

profile of v10, /device:TPU:14, one launch (start us, length us, event | category | flops | bytes accessed | tf_op | source)
XLA Modules:
  0.0 350.8 jit_solution(7223770770705725491)
XLA Ops:
  9.5 11.2 %collective-permute-start.1 = (f32[256,256]{1,0:T(8,128)S(1)}, f32[256,256]{1,0:T(8,128)S(1)}, u32[]{:S(2)}, u32[]{:S(2)}) collective-permute-start(f32[256,256]{1,0:T(8,128)S(1)} %get-tuple-element.6), channel_id=1, source_target_pairs={{0,16},{1,48},{2,80},{3,112},{4,144},{5,176},{6,208},{7,240},{8,27... | collective-permute-start | bytes 786440 | tf_op jit(solution)/shard_map/ppermute | solution.py:15
  20.7 1.9 collective-permute-start
  24.5 63.8 %collective-permute-done.1 = f32[256,256]{1,0:T(8,128)S(1)} collective-permute-done((f32[256,256]{1,0:T(8,128)S(1)}, f32[256,256]{1,0:T(8,128)S(1)}, u32[]{:S(2)}, u32[]{:S(2)}) %collective-permute-start.1) | collective-permute-done | bytes 262176 | tf_op jit(solution)/shard_map/ppermute | solution.py:15
  89.2 1.9 collective-permute-start.2
  91.2 45.4 %collective-permute-done.2 = f32[256,512]{1,0:T(8,128)S(1)} collective-permute-done((f32[256,512]{1,0:T(8,128)}, f32[256,512]{1,0:T(8,128)S(1)}, u32[]{:S(2)}, u32[]{:S(2)}) %collective-permute-start.2) | collective-permute-done | bytes 524320 | tf_op jit(solution)/shard_map/ppermute | solution.py:15
  136.5 1.9 collective-permute-start.9
  138.5 3.9 %collective-permute-start.3 = (f32[256,512]{1,0:T(8,128)S(1)}, f32[256,512]{1,0:T(8,128)S(1)}, u32[]{:S(2)}, u32[]{:S(2)}) collective-permute-start(f32[256,512]{1,0:T(8,128)S(1)} %collective-permute-done.2), channel_id=1, source_target_pairs={{0,16},{16,32},{32,48},{48,64},{64,80},{80,96},{96,112},{112,128},... | collective-permute-start | bytes 1572872 | tf_op jit(solution)/shard_map/ppermute | solution.py:30
  142.4 9.2 %collective-permute-done.9 = f32[256,512]{1,0:T(8,128)S(1)} collective-permute-done((f32[256,512]{1,0:T(8,128)S(1)}, f32[256,512]{1,0:T(8,128)S(1)}, u32[]{:S(2)}, u32[]{:S(2)}) %collective-permute-start.9) | collective-permute-done | bytes 524320 | tf_op jit(solution)/shard_map/ppermute | solution.py:30
  151.6 3.7 %collective-permute-start.10 = (f32[256,512]{1,0:T(8,128)S(1)}, f32[256,512]{1,0:T(8,128)S(1)}, u32[]{:S(2)}, u32[]{:S(2)}) collective-permute-start(f32[256,512]{1,0:T(8,128)S(1)} %collective-permute-done.9), channel_id=1, source_target_pairs={{0,496},{16,0},{32,16},{48,32},{64,48},{80,64},{96,80},{112,96},{1... | collective-permute-start | bytes 1572872 | tf_op jit(solution)/shard_map/ppermute | solution.py:30
  155.6 2.1 collective-permute-start.4
  157.7 37.8 %collective-permute-done.10 = f32[256,512]{1,0:T(8,128)S(1)} collective-permute-done((f32[256,512]{1,0:T(8,128)S(1)}, f32[256,512]{1,0:T(8,128)S(1)}, u32[]{:S(2)}, u32[]{:S(2)}) %collective-permute-start.10) | collective-permute-done | bytes 524320 | tf_op jit(solution)/shard_map/ppermute | solution.py:30
  195.5 7.2 %collective-permute-start.11 = (f32[256,512]{1,0:T(8,128)S(1)}, f32[256,512]{1,0:T(8,128)S(1)}, u32[]{:S(2)}, u32[]{:S(2)}) collective-permute-start(f32[256,512]{1,0:T(8,128)S(1)} %collective-permute-done.10), channel_id=1, source_target_pairs={{0,496},{16,0},{32,16},{48,32},{64,48},{80,64},{96,80},{112,96},{1... | collective-permute-start | bytes 1572872 | tf_op jit(solution)/shard_map/ppermute | solution.py:30
  202.8 1.9 collective-permute-start.5
  204.7 17.4 %collective-permute-done.11 = f32[256,512]{1,0:T(8,128)S(1)} collective-permute-done((f32[256,512]{1,0:T(8,128)S(1)}, f32[256,512]{1,0:T(8,128)S(1)}, u32[]{:S(2)}, u32[]{:S(2)}) %collective-permute-start.11) | collective-permute-done | bytes 524320 | tf_op jit(solution)/shard_map/ppermute | solution.py:30
  222.1 6.5 %collective-permute-start.12 = (f32[256,512]{1,0:T(8,128)S(1)}, f32[256,512]{1,0:T(8,128)S(1)}, u32[]{:S(2)}, u32[]{:S(2)}) collective-permute-start(f32[256,512]{1,0:T(8,128)S(1)} %collective-permute-done.11), channel_id=1, source_target_pairs={{0,496},{16,0},{32,16},{48,32},{64,48},{80,64},{96,80},{112,96},{1... | collective-permute-start | bytes 1572872 | tf_op jit(solution)/shard_map/ppermute | solution.py:30
  228.6 1.9 collective-permute-start.6
  230.5 9.5 %collective-permute-done.12 = f32[256,512]{1,0:T(8,128)S(1)} collective-permute-done((f32[256,512]{1,0:T(8,128)S(1)}, f32[256,512]{1,0:T(8,128)S(1)}, u32[]{:S(2)}, u32[]{:S(2)}) %collective-permute-start.12) | collective-permute-done | bytes 524320 | tf_op jit(solution)/shard_map/ppermute | solution.py:30
  240.8 6.5 %collective-permute-start.13 = (f32[256,512]{1,0:T(8,128)S(1)}, f32[256,512]{1,0:T(8,128)}, u32[]{:S(2)}, u32[]{:S(2)}) collective-permute-start(f32[256,512]{1,0:T(8,128)S(1)} %collective-permute-done.12), channel_id=1, source_target_pairs={{0,496},{16,0},{32,16},{48,32},{64,48},{80,64},{96,80},{112,96},{1... | collective-permute-start | bytes 1572872 | tf_op jit(solution)/shard_map/ppermute | solution.py:30
  247.3 1.9 collective-permute-start.7
  249.3 8.7 %collective-permute-done.13 = f32[256,512]{1,0:T(8,128)} collective-permute-done((f32[256,512]{1,0:T(8,128)S(1)}, f32[256,512]{1,0:T(8,128)}, u32[]{:S(2)}, u32[]{:S(2)}) %collective-permute-start.13) | collective-permute-done | bytes 524320 | tf_op jit(solution)/shard_map/ppermute | solution.py:30
  258.0 6.6 %collective-permute-start.14 = (f32[256,512]{1,0:T(8,128)}, f32[256,512]{1,0:T(8,128)}, u32[]{:S(2)}, u32[]{:S(2)}) collective-permute-start(f32[256,512]{1,0:T(8,128)} %collective-permute-done.13), channel_id=1, source_target_pairs={{0,496},{16,0},{32,16},{48,32},{64,48},{80,64},{96,80},{112,96},{1... | collective-permute-start | bytes 1572872 | tf_op jit(solution)/shard_map/ppermute | solution.py:30
  264.6 1.9 collective-permute-start.8
  266.6 8.0 %collective-permute-done.14 = f32[256,512]{1,0:T(8,128)} collective-permute-done((f32[256,512]{1,0:T(8,128)}, f32[256,512]{1,0:T(8,128)}, u32[]{:S(2)}, u32[]{:S(2)}) %collective-permute-start.14) | collective-permute-done | bytes 524320 | tf_op jit(solution)/shard_map/ppermute | solution.py:30
  274.6 6.5 %collective-permute-start.15 = (f32[256,512]{1,0:T(8,128)}, f32[256,512]{1,0:T(8,128)S(1)}, u32[]{:S(2)}, u32[]{:S(2)}) collective-permute-start(f32[256,512]{1,0:T(8,128)} %collective-permute-done.14), channel_id=1, source_target_pairs={{0,496},{16,0},{32,16},{48,32},{64,48},{80,64},{96,80},{112,96},{1... | collective-permute-start | bytes 1572872 | tf_op jit(solution)/shard_map/ppermute | solution.py:30
  281.1 1.9 constant_dynamic-update-slice_fusion.13
  283.0 1.9 constant_dynamic-update-slice_fusion.12
  294.5 1.9 constant_dynamic-update-slice_fusion.2
  299.1 9.0 %copy.18 = f32[256,8192]{0,1:T(8,128)} copy(f32[256,8192]{1,0:T(8,128)} %all-gather.2.cloned.1.call-done) | data formatting | bytes 16777216 | tf_op jit(solution)/shard_map/all_gather | solution.py:88
  308.1 9.0 %copy.19 = f32[256,32,256]{2,0,1:T(8,128)} copy(f32[256,32,256]{0,2,1:T(8,128)} %bitcast.29) | data formatting | bytes 16777216 | tf_op jit(solution)/shard_map/reshape | solution.py:104
  317.1 6.0 %gather_fusion = f32[14,256,256]{2,1,0:T(8,128)} fusion(f32[256,32,256]{2,0,1:T(8,128)} %copy.19, s32[1024]{0:T(1024)S(1)} %pad_clamp_fusion), kind=kCustom, calls=%fused_computation | custom fusion | bytes 7340088 | tf_op jit(solution)/shard_map/gather | solution.py:104
  323.0 5.1 %copy.20 = f32[256,14,256]{0,2,1:T(8,128)} copy(f32[256,14,256]{2,0,1:T(8,128)} %bitcast.30) | data formatting | bytes 7340032 | tf_op jit(solution)/shard_map/gather | solution.py:104
  328.2 15.7 %fusion.6 = f32[256,512]{1,0:T(8,128)} fusion(f32[256,3584]{0,1:T(8,128)} %bitcast.31, f32[3584,512]{1,0:T(8,128)} %constant_dynamic-update-slice_fusion), kind=kOutput, calls=%fused_computation.39 | convolution fusion | flops 5637144576 | bytes 11534336 | tf_op jit(solution)/shard_map/dot_general | solution.py:105
  (50 shorter events, 19.1 us)
Async XLA Ops:
  6.5 81.8 %copy-start = (f32[256,512]{1,0:T(8,128)S(1)}, f32[256,512]{1,0:T(8,128)}, u32[]{:S(2)}) copy-start(f32[256,512]{1,0:T(8,128)} %param.3) | copy-start | bytes 1572868
  6.5 292.6 %all-gather.2.cloned.1.call-start = ((), (), s32[]{:S(2)}) async-start(), calls=%async_computation | async-start | bytes 8912896 | tf_op jit(solution)/shard_map/all_gather | solution.py:88
  9.5 78.8 %collective-permute-start.1 = (f32[256,256]{1,0:T(8,128)S(1)}, f32[256,256]{1,0:T(8,128)S(1)}, u32[]{:S(2)}, u32[]{:S(2)}) collective-permute-start(f32[256,256]{1,0:T(8,128)S(1)} %get-tuple-element.6), channel_id=1, source_target_pairs={{0,16},{1,48},{2,80},{3,112},{4,144},{5,176},{6,208},{7,240},{8,27... | collective-permute-start | bytes 786440 | tf_op jit(solution)/shard_map/ppermute | solution.py:15
  20.7 67.6 %collective-permute-start = (f32[256,256]{1,0:T(8,128)S(1)}, f32[256,256]{1,0:T(8,128)S(1)}, u32[]{:S(2)}, u32[]{:S(2)}) collective-permute-start(f32[256,256]{1,0:T(8,128)S(1)} %get-tuple-element.5), channel_id=1, source_target_pairs={{0,0},{1,32},{2,64},{3,96},{4,128},{5,160},{6,192},{7,224},{8,256}... | collective-permute-start | bytes 786440 | tf_op jit(solution)/shard_map/ppermute | solution.py:15
  89.2 47.3 %collective-permute-start.2 = (f32[256,512]{1,0:T(8,128)}, f32[256,512]{1,0:T(8,128)S(1)}, u32[]{:S(2)}, u32[]{:S(2)}) collective-permute-start(f32[256,512]{1,0:T(8,128)} %fusion.2), channel_id=1, source_target_pairs={{0,416},{1,385},{2,354},{3,323},{4,292},{5,261},{6,230},{7,199},{8... | collective-permute-start | bytes 1572872 | tf_op jit(solution)/shard_map/ppermute | solution.py:15
  136.5 15.0 %collective-permute-start.9 = (f32[256,512]{1,0:T(8,128)S(1)}, f32[256,512]{1,0:T(8,128)S(1)}, u32[]{:S(2)}, u32[]{:S(2)}) collective-permute-start(f32[256,512]{1,0:T(8,128)S(1)} %collective-permute-done.2), channel_id=1, source_target_pairs={{0,496},{16,0},{32,16},{48,32},{64,48},{80,64},{96,80},{112,96},{1... | collective-permute-start | bytes 1572872 | tf_op jit(solution)/shard_map/ppermute | solution.py:30
  138.5 17.2 %collective-permute-start.3 = (f32[256,512]{1,0:T(8,128)S(1)}, f32[256,512]{1,0:T(8,128)S(1)}, u32[]{:S(2)}, u32[]{:S(2)}) collective-permute-start(f32[256,512]{1,0:T(8,128)S(1)} %collective-permute-done.2), channel_id=1, source_target_pairs={{0,16},{16,32},{32,48},{48,64},{64,80},{80,96},{96,112},{112,128},... | collective-permute-start | bytes 1572872 | tf_op jit(solution)/shard_map/ppermute | solution.py:30
  151.6 43.9 %collective-permute-start.10 = (f32[256,512]{1,0:T(8,128)S(1)}, f32[256,512]{1,0:T(8,128)S(1)}, u32[]{:S(2)}, u32[]{:S(2)}) collective-permute-start(f32[256,512]{1,0:T(8,128)S(1)} %collective-permute-done.9), channel_id=1, source_target_pairs={{0,496},{16,0},{32,16},{48,32},{64,48},{80,64},{96,80},{112,96},{1... | collective-permute-start | bytes 1572872 | tf_op jit(solution)/shard_map/ppermute | solution.py:30
  155.6 47.1 %collective-permute-start.4 = (f32[256,512]{1,0:T(8,128)S(1)}, f32[256,512]{1,0:T(8,128)S(1)}, u32[]{:S(2)}, u32[]{:S(2)}) collective-permute-start(f32[256,512]{1,0:T(8,128)S(1)} %collective-permute-done.3), channel_id=1, source_target_pairs={{0,16},{16,32},{32,48},{48,64},{64,80},{80,96},{96,112},{112,128},... | collective-permute-start | bytes 1572872 | tf_op jit(solution)/shard_map/ppermute | solution.py:30
  195.5 26.6 %collective-permute-start.11 = (f32[256,512]{1,0:T(8,128)S(1)}, f32[256,512]{1,0:T(8,128)S(1)}, u32[]{:S(2)}, u32[]{:S(2)}) collective-permute-start(f32[256,512]{1,0:T(8,128)S(1)} %collective-permute-done.10), channel_id=1, source_target_pairs={{0,496},{16,0},{32,16},{48,32},{64,48},{80,64},{96,80},{112,96},{1... | collective-permute-start | bytes 1572872 | tf_op jit(solution)/shard_map/ppermute | solution.py:30
  202.8 25.8 %collective-permute-start.5 = (f32[256,512]{1,0:T(8,128)S(1)}, f32[256,512]{1,0:T(8,128)S(1)}, u32[]{:S(2)}, u32[]{:S(2)}) collective-permute-start(f32[256,512]{1,0:T(8,128)S(1)} %collective-permute-done.4), channel_id=1, source_target_pairs={{0,16},{16,32},{32,48},{48,64},{64,80},{80,96},{96,112},{112,128},... | collective-permute-start | bytes 1572872 | tf_op jit(solution)/shard_map/ppermute | solution.py:30
  222.1 18.0 %collective-permute-start.12 = (f32[256,512]{1,0:T(8,128)S(1)}, f32[256,512]{1,0:T(8,128)S(1)}, u32[]{:S(2)}, u32[]{:S(2)}) collective-permute-start(f32[256,512]{1,0:T(8,128)S(1)} %collective-permute-done.11), channel_id=1, source_target_pairs={{0,496},{16,0},{32,16},{48,32},{64,48},{80,64},{96,80},{112,96},{1... | collective-permute-start | bytes 1572872 | tf_op jit(solution)/shard_map/ppermute | solution.py:30
  228.5 29.4 %copy-start.3 = (f32[256,512]{1,0:T(8,128)}, f32[256,512]{1,0:T(8,128)S(1)}, u32[]{:S(2)}) copy-start(f32[256,512]{1,0:T(8,128)S(1)} %collective-permute-done.5) | copy-start | bytes 1572868
  228.6 18.8 %collective-permute-start.6 = (f32[256,512]{1,0:T(8,128)S(1)}, f32[256,512]{1,0:T(8,128)S(1)}, u32[]{:S(2)}, u32[]{:S(2)}) collective-permute-start(f32[256,512]{1,0:T(8,128)S(1)} %collective-permute-done.5), channel_id=1, source_target_pairs={{0,16},{16,32},{32,48},{48,64},{64,80},{80,96},{96,112},{112,128},... | collective-permute-start | bytes 1572872 | tf_op jit(solution)/shard_map/ppermute | solution.py:30
  240.0 0.8 copy-start.1
  240.8 17.2 %collective-permute-start.13 = (f32[256,512]{1,0:T(8,128)S(1)}, f32[256,512]{1,0:T(8,128)}, u32[]{:S(2)}, u32[]{:S(2)}) collective-permute-start(f32[256,512]{1,0:T(8,128)S(1)} %collective-permute-done.12), channel_id=1, source_target_pairs={{0,496},{16,0},{32,16},{48,32},{64,48},{80,64},{96,80},{112,96},{1... | collective-permute-start | bytes 1572872 | tf_op jit(solution)/shard_map/ppermute | solution.py:30
  247.3 17.3 %copy-start.4 = (f32[256,512]{1,0:T(8,128)}, f32[256,512]{1,0:T(8,128)S(1)}, u32[]{:S(2)}) copy-start(f32[256,512]{1,0:T(8,128)S(1)} %collective-permute-done.6) | copy-start | bytes 1572868
  247.3 17.3 %collective-permute-start.7 = (f32[256,512]{1,0:T(8,128)S(1)}, f32[256,512]{1,0:T(8,128)}, u32[]{:S(2)}, u32[]{:S(2)}) collective-permute-start(f32[256,512]{1,0:T(8,128)S(1)} %collective-permute-done.6), channel_id=1, source_target_pairs={{0,16},{16,32},{32,48},{48,64},{64,80},{80,96},{96,112},{112,128},... | collective-permute-start | bytes 1572872 | tf_op jit(solution)/shard_map/ppermute | solution.py:30
  258.0 16.7 %collective-permute-start.14 = (f32[256,512]{1,0:T(8,128)}, f32[256,512]{1,0:T(8,128)}, u32[]{:S(2)}, u32[]{:S(2)}) collective-permute-start(f32[256,512]{1,0:T(8,128)} %collective-permute-done.13), channel_id=1, source_target_pairs={{0,496},{16,0},{32,16},{48,32},{64,48},{80,64},{96,80},{112,96},{1... | collective-permute-start | bytes 1572872 | tf_op jit(solution)/shard_map/ppermute | solution.py:30
  264.6 16.5 %collective-permute-start.8 = (f32[256,512]{1,0:T(8,128)}, f32[256,512]{1,0:T(8,128)}, u32[]{:S(2)}, u32[]{:S(2)}) collective-permute-start(f32[256,512]{1,0:T(8,128)} %collective-permute-done.7), channel_id=1, source_target_pairs={{0,16},{16,32},{32,48},{48,64},{64,80},{80,96},{96,112},{112,128},... | collective-permute-start | bytes 1572872 | tf_op jit(solution)/shard_map/ppermute | solution.py:30
  266.5 27.1 %copy-start.2 = (f32[256,512]{1,0:T(8,128)S(1)}, f32[256,512]{1,0:T(8,128)}, u32[]{:S(2)}) copy-start(f32[256,512]{1,0:T(8,128)} %copy-done.1) | copy-start | bytes 1572868
  274.6 23.6 %collective-permute-start.15 = (f32[256,512]{1,0:T(8,128)}, f32[256,512]{1,0:T(8,128)S(1)}, u32[]{:S(2)}, u32[]{:S(2)}) collective-permute-start(f32[256,512]{1,0:T(8,128)} %collective-permute-done.14), channel_id=1, source_target_pairs={{0,496},{16,0},{32,16},{48,32},{64,48},{80,64},{96,80},{112,96},{1... | collective-permute-start | bytes 1572872 | tf_op jit(solution)/shard_map/ppermute | solution.py:30
Sparse Core Ops, SparseCore 0:
  89.4 143.1 all-gather.1

commit v11 on v10

--- a/solution.py
+++ b/solution.py
@@ -98,11 +98,13 @@
     for _ in range(middle):
         behind = shift(behind, "row", -1)
         before.insert(0, behind)
-    right = jnp.concatenate(before + [centre] + after, axis=0)
-    start = (row_id + 2 * col_id) % row_count
-    picks = (start + jnp.arange(STEPS, dtype=jnp.int32)) % row_count
-    left = row_panel.reshape(height, row_count, group)[:, picks].reshape(height, STEPS * group)
-    total = jnp.dot(left, right, precision=lax.Precision.HIGHEST, preferred_element_type=jnp.float32)
+    pieces = before + [centre] + after
+    total = None
+    for step in range(STEPS):
+        start = (row_id + 2 * col_id + step) % row_count
+        left = lax.dynamic_slice_in_dim(row_panel, start * group, group, axis=1)
+        term = jnp.dot(left, pieces[step], precision=lax.Precision.HIGHEST, preferred_element_type=jnp.float32)
+        total = term if total is None else total + term
     return total
 
 

time: 352 us -> 338 us (0.960)
  the two profiles are of different devices: /device:TPU:14 before, /device:TPU:15 now
where the time goes in v11:
time: 338 us; the launch traced here: 337 us
  waiting for transfers between devices  227 us (67%)
  starting transfers between devices  64.8 us (19%)
  matrix products  23.7 us (7%)
  between operations  14 us (4%)
  other arithmetic  4.43 us (1%)
    ppermute x3, waiting for transfers between devices, send(): return lax.ppermute(value, AXES, pairs)  189 us
    ppermute x13, starting transfers between devices, shift(): lax.ppermute(value, axis, [(i, (i - by) % length) for i in range(length)])  49.4 us
    ppermute x13, waiting for transfers between devices, shift(): lax.ppermute(value, axis, [(i, (i - by) % length) for i in range(length)])  38.1 us
    dot_general x14, matrix products, body(): jnp.dot(left, pieces[step], precision=lax.Precision.HIGHEST, preferred_el...  23.7 us
    ppermute x3, starting transfers between devices, send(): return lax.ppermute(value, AXES, pairs)  15.3 us
  transfers between devices with their start and end apart: 17, of which 12 were waited for; matrix products, arithmetic and copies ran while one was open for 7% of the time, Pallas kernels for 0%

profile of v11, /device:TPU:15, one launch (start us, length us, event | category | flops | bytes accessed | tf_op | source)
XLA Modules:
  0.0 336.5 jit_solution(12647562565809483939)
XLA Ops:
  9.4 11.5 %collective-permute-start = (f32[256,256]{1,0:T(8,128)S(1)}, f32[256,256]{1,0:T(8,128)S(1)}, u32[]{:S(2)}, u32[]{:S(2)}) collective-permute-start(f32[256,256]{1,0:T(8,128)S(1)} %get-tuple-element.5), channel_id=1, source_target_pairs={{0,0},{1,32},{2,64},{3,96},{4,128},{5,160},{6,192},{7,224},{8,256}... | collective-permute-start | bytes 786440 | tf_op jit(solution)/shard_map/ppermute | solution.py:15
  20.9 1.9 collective-permute-start.1
  24.7 61.4 %collective-permute-done = f32[256,256]{1,0:T(8,128)S(1)} collective-permute-done((f32[256,256]{1,0:T(8,128)S(1)}, f32[256,256]{1,0:T(8,128)S(1)}, u32[]{:S(2)}, u32[]{:S(2)}) %collective-permute-start) | collective-permute-done | bytes 262176 | tf_op jit(solution)/shard_map/ppermute | solution.py:15
  86.1 4.3 %collective-permute-done.1 = f32[256,256]{1,0:T(8,128)S(1)} collective-permute-done((f32[256,256]{1,0:T(8,128)S(1)}, f32[256,256]{1,0:T(8,128)S(1)}, u32[]{:S(2)}, u32[]{:S(2)}) %collective-permute-start.1) | collective-permute-done | bytes 262176 | tf_op jit(solution)/shard_map/ppermute | solution.py:15
  90.4 2.0 fusion.7
  92.3 1.9 collective-permute-start.2
  94.3 123.6 %collective-permute-done.2 = f32[256,512]{1,0:T(8,128)S(1)} collective-permute-done((f32[256,512]{1,0:T(8,128)}, f32[256,512]{1,0:T(8,128)S(1)}, u32[]{:S(2)}, u32[]{:S(2)}) %collective-permute-start.2) | collective-permute-done | bytes 524320 | tf_op jit(solution)/shard_map/ppermute | solution.py:15
  217.8 1.9 collective-permute-start.9
  219.8 3.4 collective-permute-start.3
  223.1 5.2 %collective-permute-done.9 = f32[256,512]{1,0:T(8,128)S(1)} collective-permute-done((f32[256,512]{1,0:T(8,128)S(1)}, f32[256,512]{1,0:T(8,128)S(1)}, u32[]{:S(2)}, u32[]{:S(2)}) %collective-permute-start.9) | collective-permute-done | bytes 524320 | tf_op jit(solution)/shard_map/ppermute | solution.py:30
  228.3 4.5 %collective-permute-start.10 = (f32[256,512]{1,0:T(8,128)S(1)}, f32[256,512]{1,0:T(8,128)S(1)}, u32[]{:S(2)}, u32[]{:S(2)}) collective-permute-start(f32[256,512]{1,0:T(8,128)S(1)} %collective-permute-done.9), channel_id=1, source_target_pairs={{0,496},{16,0},{32,16},{48,32},{64,48},{80,64},{96,80},{112,96},{1... | collective-permute-start | bytes 1572872 | tf_op jit(solution)/shard_map/ppermute | solution.py:30
  232.9 3.6 %collective-permute-done.3 = f32[256,512]{1,0:T(8,128)S(1)} collective-permute-done((f32[256,512]{1,0:T(8,128)S(1)}, f32[256,512]{1,0:T(8,128)S(1)}, u32[]{:S(2)}, u32[]{:S(2)}) %collective-permute-start.3) | collective-permute-done | bytes 524320 | tf_op jit(solution)/shard_map/ppermute | solution.py:30
  236.5 1.9 collective-permute-start.4
  238.4 2.7 collective-permute-done.10
  241.1 5.9 %collective-permute-start.11 = (f32[256,512]{1,0:T(8,128)S(1)}, f32[256,512]{1,0:T(8,128)S(1)}, u32[]{:S(2)}, u32[]{:S(2)}) collective-permute-start(f32[256,512]{1,0:T(8,128)S(1)} %collective-permute-done.10), channel_id=1, source_target_pairs={{0,496},{16,0},{32,16},{48,32},{64,48},{80,64},{96,80},{112,96},{1... | collective-permute-start | bytes 1572872 | tf_op jit(solution)/shard_map/ppermute | solution.py:30
  247.1 5.3 %collective-permute-done.4 = f32[256,512]{1,0:T(8,128)S(1)} collective-permute-done((f32[256,512]{1,0:T(8,128)S(1)}, f32[256,512]{1,0:T(8,128)S(1)}, u32[]{:S(2)}, u32[]{:S(2)}) %collective-permute-start.4) | collective-permute-done | bytes 524320 | tf_op jit(solution)/shard_map/ppermute | solution.py:30
  252.3 1.9 collective-permute-start.5
  254.2 4.0 %collective-permute-done.11 = f32[256,512]{1,0:T(8,128)S(1)} collective-permute-done((f32[256,512]{1,0:T(8,128)S(1)}, f32[256,512]{1,0:T(8,128)S(1)}, u32[]{:S(2)}, u32[]{:S(2)}) %collective-permute-start.11) | collective-permute-done | bytes 524320 | tf_op jit(solution)/shard_map/ppermute | solution.py:30
  258.2 5.9 %collective-permute-start.12 = (f32[256,512]{1,0:T(8,128)S(1)}, f32[256,512]{1,0:T(8,128)S(1)}, u32[]{:S(2)}, u32[]{:S(2)}) collective-permute-start(f32[256,512]{1,0:T(8,128)S(1)} %collective-permute-done.11), channel_id=1, source_target_pairs={{0,496},{16,0},{32,16},{48,32},{64,48},{80,64},{96,80},{112,96},{1... | collective-permute-start | bytes 1572872 | tf_op jit(solution)/shard_map/ppermute | solution.py:30
  264.1 3.2 collective-permute-done.5
  267.3 1.9 collective-permute-start.6
  269.2 5.7 %collective-permute-done.12 = f32[256,512]{1,0:T(8,128)S(1)} collective-permute-done((f32[256,512]{1,0:T(8,128)S(1)}, f32[256,512]{1,0:T(8,128)S(1)}, u32[]{:S(2)}, u32[]{:S(2)}) %collective-permute-start.12) | collective-permute-done | bytes 524320 | tf_op jit(solution)/shard_map/ppermute | solution.py:30
  274.9 6.3 %collective-permute-start.13 = (f32[256,512]{1,0:T(8,128)S(1)}, f32[256,512]{1,0:T(8,128)}, u32[]{:S(2)}, u32[]{:S(2)}) collective-permute-start(f32[256,512]{1,0:T(8,128)S(1)} %collective-permute-done.12), channel_id=1, source_target_pairs={{0,496},{16,0},{32,16},{48,32},{64,48},{80,64},{96,80},{112,96},{1... | collective-permute-start | bytes 1572872 | tf_op jit(solution)/shard_map/ppermute | solution.py:30
  281.3 1.9 collective-permute-start.7
  283.2 4.1 %collective-permute-done.13 = f32[256,512]{1,0:T(8,128)} collective-permute-done((f32[256,512]{1,0:T(8,128)S(1)}, f32[256,512]{1,0:T(8,128)}, u32[]{:S(2)}, u32[]{:S(2)}) %collective-permute-start.13) | collective-permute-done | bytes 524320 | tf_op jit(solution)/shard_map/ppermute | solution.py:30
  287.4 6.0 %collective-permute-start.14 = (f32[256,512]{1,0:T(8,128)}, f32[256,512]{1,0:T(8,128)}, u32[]{:S(2)}, u32[]{:S(2)}) collective-permute-start(f32[256,512]{1,0:T(8,128)} %collective-permute-done.13), channel_id=1, source_target_pairs={{0,496},{16,0},{32,16},{48,32},{64,48},{80,64},{96,80},{112,96},{1... | collective-permute-start | bytes 1572872 | tf_op jit(solution)/shard_map/ppermute | solution.py:30
  293.6 1.9 collective-permute-start.8
  295.5 4.3 %collective-permute-done.14 = f32[256,512]{1,0:T(8,128)} collective-permute-done((f32[256,512]{1,0:T(8,128)}, f32[256,512]{1,0:T(8,128)}, u32[]{:S(2)}, u32[]{:S(2)}) %collective-permute-start.14) | collective-permute-done | bytes 524320 | tf_op jit(solution)/shard_map/ppermute | solution.py:30
  299.8 5.9 %collective-permute-start.15 = (f32[256,512]{1,0:T(8,128)}, f32[256,512]{1,0:T(8,128)}, u32[]{:S(2)}, u32[]{:S(2)}) collective-permute-start(f32[256,512]{1,0:T(8,128)} %collective-permute-done.14), channel_id=1, source_target_pairs={{0,496},{16,0},{32,16},{48,32},{64,48},{80,64},{96,80},{112,96},{1... | collective-permute-start | bytes 1572872 | tf_op jit(solution)/shard_map/ppermute | solution.py:30
  315.4 1.8 fusion.4
  325.4 1.7 convolution_add_fusion.1
  327.1 2.6 convolution_add_fusion
  (49 shorter events, 22.4 us)
Async XLA Ops:
  6.5 299.2 %all-gather.2.cloned.1.call-start = ((), (), s32[]{:S(2)}) async-start(), calls=%async_computation | async-start | bytes 8912896 | tf_op jit(solution)/shard_map/all_gather | solution.py:88
  9.4 76.7 %collective-permute-start = (f32[256,256]{1,0:T(8,128)S(1)}, f32[256,256]{1,0:T(8,128)S(1)}, u32[]{:S(2)}, u32[]{:S(2)}) collective-permute-start(f32[256,256]{1,0:T(8,128)S(1)} %get-tuple-element.5), channel_id=1, source_target_pairs={{0,0},{1,32},{2,64},{3,96},{4,128},{5,160},{6,192},{7,224},{8,256}... | collective-permute-start | bytes 786440 | tf_op jit(solution)/shard_map/ppermute | solution.py:15
  20.9 69.5 %collective-permute-start.1 = (f32[256,256]{1,0:T(8,128)S(1)}, f32[256,256]{1,0:T(8,128)S(1)}, u32[]{:S(2)}, u32[]{:S(2)}) collective-permute-start(f32[256,256]{1,0:T(8,128)S(1)} %get-tuple-element.6), channel_id=1, source_target_pairs={{0,16},{1,48},{2,80},{3,112},{4,144},{5,176},{6,208},{7,240},{8,27... | collective-permute-start | bytes 786440 | tf_op jit(solution)/shard_map/ppermute | solution.py:15
  92.3 125.5 %collective-permute-start.2 = (f32[256,512]{1,0:T(8,128)}, f32[256,512]{1,0:T(8,128)S(1)}, u32[]{:S(2)}, u32[]{:S(2)}) collective-permute-start(f32[256,512]{1,0:T(8,128)} %fusion.7), channel_id=1, source_target_pairs={{0,416},{1,385},{2,354},{3,323},{4,292},{5,261},{6,230},{7,199},{8... | collective-permute-start | bytes 1572872 | tf_op jit(solution)/shard_map/ppermute | solution.py:15
  217.8 10.5 %collective-permute-start.9 = (f32[256,512]{1,0:T(8,128)S(1)}, f32[256,512]{1,0:T(8,128)S(1)}, u32[]{:S(2)}, u32[]{:S(2)}) collective-permute-start(f32[256,512]{1,0:T(8,128)S(1)} %collective-permute-done.2), channel_id=1, source_target_pairs={{0,496},{16,0},{32,16},{48,32},{64,48},{80,64},{96,80},{112,96},{1... | collective-permute-start | bytes 1572872 | tf_op jit(solution)/shard_map/ppermute | solution.py:30
  219.8 16.8 %collective-permute-start.3 = (f32[256,512]{1,0:T(8,128)S(1)}, f32[256,512]{1,0:T(8,128)S(1)}, u32[]{:S(2)}, u32[]{:S(2)}) collective-permute-start(f32[256,512]{1,0:T(8,128)S(1)} %collective-permute-done.2), channel_id=1, source_target_pairs={{0,16},{16,32},{32,48},{48,64},{64,80},{80,96},{96,112},{112,128},... | collective-permute-start | bytes 1572872 | tf_op jit(solution)/shard_map/ppermute | solution.py:30
  228.3 52.9 %copy-start = (f32[256,512]{1,0:T(8,128)}, f32[256,512]{1,0:T(8,128)S(1)}, u32[]{:S(2)}) copy-start(f32[256,512]{1,0:T(8,128)S(1)} %collective-permute-done.9) | copy-start | bytes 1572868
  228.3 12.8 %collective-permute-start.10 = (f32[256,512]{1,0:T(8,128)S(1)}, f32[256,512]{1,0:T(8,128)S(1)}, u32[]{:S(2)}, u32[]{:S(2)}) collective-permute-start(f32[256,512]{1,0:T(8,128)S(1)} %collective-permute-done.9), channel_id=1, source_target_pairs={{0,496},{16,0},{32,16},{48,32},{64,48},{80,64},{96,80},{112,96},{1... | collective-permute-start | bytes 1572872 | tf_op jit(solution)/shard_map/ppermute | solution.py:30
  236.5 15.8 %collective-permute-start.4 = (f32[256,512]{1,0:T(8,128)S(1)}, f32[256,512]{1,0:T(8,128)S(1)}, u32[]{:S(2)}, u32[]{:S(2)}) collective-permute-start(f32[256,512]{1,0:T(8,128)S(1)} %collective-permute-done.3), channel_id=1, source_target_pairs={{0,16},{16,32},{32,48},{48,64},{64,80},{80,96},{96,112},{112,128},... | collective-permute-start | bytes 1572872 | tf_op jit(solution)/shard_map/ppermute | solution.py:30
  241.1 42.0 %copy-start.2 = (f32[256,512]{1,0:T(8,128)}, f32[256,512]{1,0:T(8,128)S(1)}, u32[]{:S(2)}) copy-start(f32[256,512]{1,0:T(8,128)S(1)} %collective-permute-done.10) | copy-start | bytes 1572868
  241.1 17.1 %collective-permute-start.11 = (f32[256,512]{1,0:T(8,128)S(1)}, f32[256,512]{1,0:T(8,128)S(1)}, u32[]{:S(2)}, u32[]{:S(2)}) collective-permute-start(f32[256,512]{1,0:T(8,128)S(1)} %collective-permute-done.10), channel_id=1, source_target_pairs={{0,496},{16,0},{32,16},{48,32},{64,48},{80,64},{96,80},{112,96},{1... | collective-permute-start | bytes 1572872 | tf_op jit(solution)/shard_map/ppermute | solution.py:30
  252.3 15.0 %collective-permute-start.5 = (f32[256,512]{1,0:T(8,128)S(1)}, f32[256,512]{1,0:T(8,128)S(1)}, u32[]{:S(2)}, u32[]{:S(2)}) collective-permute-start(f32[256,512]{1,0:T(8,128)S(1)} %collective-permute-done.4), channel_id=1, source_target_pairs={{0,16},{16,32},{32,48},{48,64},{64,80},{80,96},{96,112},{112,128},... | collective-permute-start | bytes 1572872 | tf_op jit(solution)/shard_map/ppermute | solution.py:30
  258.2 29.1 %copy-start.4 = (f32[256,512]{1,0:T(8,128)}, f32[256,512]{1,0:T(8,128)S(1)}, u32[]{:S(2)}) copy-start(f32[256,512]{1,0:T(8,128)S(1)} %collective-permute-done.11) | copy-start | bytes 1572868
  258.2 16.7 %collective-permute-start.12 = (f32[256,512]{1,0:T(8,128)S(1)}, f32[256,512]{1,0:T(8,128)S(1)}, u32[]{:S(2)}, u32[]{:S(2)}) collective-permute-start(f32[256,512]{1,0:T(8,128)S(1)} %collective-permute-done.11), channel_id=1, source_target_pairs={{0,496},{16,0},{32,16},{48,32},{64,48},{80,64},{96,80},{112,96},{1... | collective-permute-start | bytes 1572872 | tf_op jit(solution)/shard_map/ppermute | solution.py:30
  267.3 13.9 %collective-permute-start.6 = (f32[256,512]{1,0:T(8,128)S(1)}, f32[256,512]{1,0:T(8,128)S(1)}, u32[]{:S(2)}, u32[]{:S(2)}) collective-permute-start(f32[256,512]{1,0:T(8,128)S(1)} %collective-permute-done.5), channel_id=1, source_target_pairs={{0,16},{16,32},{32,48},{48,64},{64,80},{80,96},{96,112},{112,128},... | collective-permute-start | bytes 1572872 | tf_op jit(solution)/shard_map/ppermute | solution.py:30
  274.9 12.4 %copy-start.6 = (f32[256,512]{1,0:T(8,128)}, f32[256,512]{1,0:T(8,128)S(1)}, u32[]{:S(2)}) copy-start(f32[256,512]{1,0:T(8,128)S(1)} %collective-permute-done.12) | copy-start | bytes 1572868
  274.9 12.4 %collective-permute-start.13 = (f32[256,512]{1,0:T(8,128)S(1)}, f32[256,512]{1,0:T(8,128)}, u32[]{:S(2)}, u32[]{:S(2)}) collective-permute-start(f32[256,512]{1,0:T(8,128)S(1)} %collective-permute-done.12), channel_id=1, source_target_pairs={{0,496},{16,0},{32,16},{48,32},{64,48},{80,64},{96,80},{112,96},{1... | collective-permute-start | bytes 1572872 | tf_op jit(solution)/shard_map/ppermute | solution.py:30
  281.3 12.3 %collective-permute-start.7 = (f32[256,512]{1,0:T(8,128)S(1)}, f32[256,512]{1,0:T(8,128)S(1)}, u32[]{:S(2)}, u32[]{:S(2)}) collective-permute-start(f32[256,512]{1,0:T(8,128)S(1)} %collective-permute-done.6), channel_id=1, source_target_pairs={{0,16},{16,32},{32,48},{48,64},{64,80},{80,96},{96,112},{112,128},... | collective-permute-start | bytes 1572872 | tf_op jit(solution)/shard_map/ppermute | solution.py:30
  287.4 12.4 %collective-permute-start.14 = (f32[256,512]{1,0:T(8,128)}, f32[256,512]{1,0:T(8,128)}, u32[]{:S(2)}, u32[]{:S(2)}) collective-permute-start(f32[256,512]{1,0:T(8,128)} %collective-permute-done.13), channel_id=1, source_target_pairs={{0,496},{16,0},{32,16},{48,32},{64,48},{80,64},{96,80},{112,96},{1... | collective-permute-start | bytes 1572872 | tf_op jit(solution)/shard_map/ppermute | solution.py:30
  293.6 21.8 %collective-permute-start.8 = (f32[256,512]{1,0:T(8,128)S(1)}, f32[256,512]{1,0:T(8,128)}, u32[]{:S(2)}, u32[]{:S(2)}) collective-permute-start(f32[256,512]{1,0:T(8,128)S(1)} %collective-permute-done.7), channel_id=1, source_target_pairs={{0,16},{16,32},{32,48},{48,64},{64,80},{80,96},{96,112},{112,128},... | collective-permute-start | bytes 1572872 | tf_op jit(solution)/shard_map/ppermute | solution.py:30
  299.8 27.3 %collective-permute-start.15 = (f32[256,512]{1,0:T(8,128)}, f32[256,512]{1,0:T(8,128)}, u32[]{:S(2)}, u32[]{:S(2)}) collective-permute-start(f32[256,512]{1,0:T(8,128)} %collective-permute-done.14), channel_id=1, source_target_pairs={{0,496},{16,0},{32,16},{48,32},{64,48},{80,64},{96,80},{112,96},{1... | collective-permute-start | bytes 1572872 | tf_op jit(solution)/shard_map/ppermute | solution.py:30
  305.7 11.5 %copy-start.1 = (f32[256,512]{1,0:T(8,128)S(1)}, f32[256,512]{1,0:T(8,128)}, u32[]{:S(2)}) copy-start(f32[256,512]{1,0:T(8,128)} %copy-done) | copy-start | bytes 1572868
  305.8 13.1 %copy-start.3 = (f32[256,512]{1,0:T(8,128)S(1)}, f32[256,512]{1,0:T(8,128)}, u32[]{:S(2)}) copy-start(f32[256,512]{1,0:T(8,128)} %copy-done.2) | copy-start | bytes 1572868
  305.8 14.7 %copy-start.5 = (f32[256,512]{1,0:T(8,128)S(1)}, f32[256,512]{1,0:T(8,128)}, u32[]{:S(2)}) copy-start(f32[256,512]{1,0:T(8,128)} %copy-done.4) | copy-start | bytes 1572868
  307.5 14.6 %copy-start.7 = (f32[256,512]{1,0:T(8,128)S(1)}, f32[256,512]{1,0:T(8,128)}, u32[]{:S(2)}) copy-start(f32[256,512]{1,0:T(8,128)} %copy-done.6) | copy-start | bytes 1572868
Sparse Core Ops, SparseCore 0:
  92.5 138.7 all-gather.1

commit v12 on v11

--- a/solution.py
+++ b/solution.py
@@ -100,10 +100,14 @@
         before.insert(0, behind)
     pieces = before + [centre] + after
     total = None
-    for step in range(STEPS):
-        start = (row_id + 2 * col_id + step) % row_count
-        left = lax.dynamic_slice_in_dim(row_panel, start * group, group, axis=1)
-        term = jnp.dot(left, pieces[step], precision=lax.Precision.HIGHEST, preferred_element_type=jnp.float32)
+    for step in range(0, STEPS, 2):
+        lefts = []
+        for offset in range(2):
+            start = (row_id + 2 * col_id + step + offset) % row_count
+            lefts.append(lax.dynamic_slice_in_dim(row_panel, start * group, group, axis=1))
+        left = jnp.concatenate(lefts, axis=1)
+        right = jnp.concatenate(pieces[step : step + 2], axis=0)
+        term = jnp.dot(left, right, precision=lax.Precision.HIGHEST, preferred_element_type=jnp.float32)
         total = term if total is None else total + term
     return total
 

time: 338 us -> 328 us (0.970)
  matrix products: 23.7 us -> 12.5 us
    dot_general x14 -> x7, matrix products: 23.7 us -> 12.5 us  [body(): jnp.dot(left, right, precision=lax.Precision.HIGHEST, preferred_element_t...]
  transfers between devices with their start and end apart: 17 -> 17, of which waited for: 12 -> 12; matrix products, arithmetic and copies ran while one was open for 7% -> 4% of each run, Pallas kernels for 0% -> 0%
where the time goes in v12:
time: 328 us
  waiting for transfers between devices  227 us (69%)
  starting transfers between devices  64.7 us (20%)
  between operations  14 us (4%)
  matrix products  12.5 us (4%)
  local copies, waits for them, and re-layouts  4.6 us (1%)
  other arithmetic  4.43 us (1%)
    ppermute x3, waiting for transfers between devices, send(): return lax.ppermute(value, AXES, pairs)  189 us
    ppermute x13, starting transfers between devices, shift(): lax.ppermute(value, axis, [(i, (i - by) % length) for i in range(length)])  49.3 us
    ppermute x13, waiting for transfers between devices, shift(): lax.ppermute(value, axis, [(i, (i - by) % length) for i in range(length)])  38.1 us
    ppermute x3, starting transfers between devices, send(): return lax.ppermute(value, AXES, pairs)  15.3 us
    dot_general x7, matrix products, body(): jnp.dot(left, right, precision=lax.Precision.HIGHEST, preferred_element_t...  12.5 us
  transfers between devices with their start and end apart: 17, of which 12 were waited for; matrix products, arithmetic and copies ran while one was open for 4% of the time, Pallas kernels for 0%

profile of v12, /device:TPU:15, one launch (start us, length us, event | category | flops | bytes accessed | tf_op | source)
XLA Modules:
  0.0 327.6 jit_solution(3362115178952125946)
XLA Ops:
  9.4 11.5 %collective-permute-start = (f32[256,256]{1,0:T(8,128)S(1)}, f32[256,256]{1,0:T(8,128)S(1)}, u32[]{:S(2)}, u32[]{:S(2)}) collective-permute-start(f32[256,256]{1,0:T(8,128)S(1)} %get-tuple-element.19), channel_id=1, source_target_pairs={{0,0},{1,32},{2,64},{3,96},{4,128},{5,160},{6,192},{7,224},{8,256}... | collective-permute-start | bytes 786440 | tf_op jit(solution)/shard_map/ppermute | solution.py:15
  20.9 1.9 collective-permute-start.1
  24.7 61.4 %collective-permute-done = f32[256,256]{1,0:T(8,128)S(1)} collective-permute-done((f32[256,256]{1,0:T(8,128)S(1)}, f32[256,256]{1,0:T(8,128)S(1)}, u32[]{:S(2)}, u32[]{:S(2)}) %collective-permute-start) | collective-permute-done | bytes 262176 | tf_op jit(solution)/shard_map/ppermute | solution.py:15
  86.1 4.3 %collective-permute-done.1 = f32[256,256]{1,0:T(8,128)S(1)} collective-permute-done((f32[256,256]{1,0:T(8,128)S(1)}, f32[256,256]{1,0:T(8,128)S(1)}, u32[]{:S(2)}, u32[]{:S(2)}) %collective-permute-start.1) | collective-permute-done | bytes 262176 | tf_op jit(solution)/shard_map/ppermute | solution.py:15
  90.4 2.0 fusion.28
  92.3 1.9 collective-permute-start.2
  94.3 123.6 %collective-permute-done.2 = f32[256,512]{1,0:T(8,128)S(1)} collective-permute-done((f32[256,512]{1,0:T(8,128)}, f32[256,512]{1,0:T(8,128)S(1)}, u32[]{:S(2)}, u32[]{:S(2)}) %collective-permute-start.2) | collective-permute-done | bytes 524320 | tf_op jit(solution)/shard_map/ppermute | solution.py:15
  219.8 3.4 %collective-permute-start.3 = (f32[256,512]{1,0:T(8,128)S(1)}, f32[256,512]{1,0:T(8,128)S(1)}, u32[]{:S(2)}, u32[]{:S(2)}) collective-permute-start(f32[256,512]{1,0:T(8,128)S(1)} %collective-permute-done.2), channel_id=1, source_target_pairs={{0,16},{16,32},{32,48},{48,64},{64,80},{80,96},{96,112},{112,128},... | collective-permute-start | bytes 1572872 | tf_op jit(solution)/shard_map/ppermute | solution.py:30
  223.1 5.2 %collective-permute-done.9 = f32[256,512]{1,0:T(8,128)S(1)} collective-permute-done((f32[256,512]{1,0:T(8,128)S(1)}, f32[256,512]{1,0:T(8,128)S(1)}, u32[]{:S(2)}, u32[]{:S(2)}) %collective-permute-start.9) | collective-permute-done | bytes 524320 | tf_op jit(solution)/shard_map/ppermute | solution.py:30
  228.3 4.6 %collective-permute-start.10 = (f32[256,512]{1,0:T(8,128)S(1)}, f32[256,512]{1,0:T(8,128)S(1)}, u32[]{:S(2)}, u32[]{:S(2)}) collective-permute-start(f32[256,512]{1,0:T(8,128)S(1)} %collective-permute-done.9), channel_id=1, source_target_pairs={{0,496},{16,0},{32,16},{48,32},{64,48},{80,64},{96,80},{112,96},{1... | collective-permute-start | bytes 1572872 | tf_op jit(solution)/shard_map/ppermute | solution.py:30
  232.9 3.7 %collective-permute-done.3 = f32[256,512]{1,0:T(8,128)S(1)} collective-permute-done((f32[256,512]{1,0:T(8,128)S(1)}, f32[256,512]{1,0:T(8,128)S(1)}, u32[]{:S(2)}, u32[]{:S(2)}) %collective-permute-start.3) | collective-permute-done | bytes 524320 | tf_op jit(solution)/shard_map/ppermute | solution.py:30
  236.6 1.9 collective-permute-start.4
  238.5 2.6 collective-permute-done.10
  241.1 5.9 %collective-permute-start.11 = (f32[256,512]{1,0:T(8,128)S(1)}, f32[256,512]{1,0:T(8,128)S(1)}, u32[]{:S(2)}, u32[]{:S(2)}) collective-permute-start(f32[256,512]{1,0:T(8,128)S(1)} %collective-permute-done.10), channel_id=1, source_target_pairs={{0,496},{16,0},{32,16},{48,32},{64,48},{80,64},{96,80},{112,96},{1... | collective-permute-start | bytes 1572872 | tf_op jit(solution)/shard_map/ppermute | solution.py:30
  247.1 5.2 %collective-permute-done.4 = f32[256,512]{1,0:T(8,128)S(1)} collective-permute-done((f32[256,512]{1,0:T(8,128)S(1)}, f32[256,512]{1,0:T(8,128)S(1)}, u32[]{:S(2)}, u32[]{:S(2)}) %collective-permute-start.4) | collective-permute-done | bytes 524320 | tf_op jit(solution)/shard_map/ppermute | solution.py:30
  254.2 3.9 %collective-permute-done.11 = f32[256,512]{1,0:T(8,128)S(1)} collective-permute-done((f32[256,512]{1,0:T(8,128)S(1)}, f32[256,512]{1,0:T(8,128)S(1)}, u32[]{:S(2)}, u32[]{:S(2)}) %collective-permute-start.11) | collective-permute-done | bytes 524320 | tf_op jit(solution)/shard_map/ppermute | solution.py:30
  258.1 5.9 %collective-permute-start.12 = (f32[256,512]{1,0:T(8,128)S(1)}, f32[256,512]{1,0:T(8,128)S(1)}, u32[]{:S(2)}, u32[]{:S(2)}) collective-permute-start(f32[256,512]{1,0:T(8,128)S(1)} %collective-permute-done.11), channel_id=1, source_target_pairs={{0,496},{16,0},{32,16},{48,32},{64,48},{80,64},{96,80},{112,96},{1... | collective-permute-start | bytes 1572872 | tf_op jit(solution)/shard_map/ppermute | solution.py:30
  264.0 3.0 collective-permute-done.5
  267.0 1.9 collective-permute-start.6
  269.0 6.3 %collective-permute-done.12 = f32[256,512]{1,0:T(8,128)S(1)} collective-permute-done((f32[256,512]{1,0:T(8,128)S(1)}, f32[256,512]{1,0:T(8,128)S(1)}, u32[]{:S(2)}, u32[]{:S(2)}) %collective-permute-start.12) | collective-permute-done | bytes 524320 | tf_op jit(solution)/shard_map/ppermute | solution.py:30
  275.3 6.3 %collective-permute-start.13 = (f32[256,512]{1,0:T(8,128)S(1)}, f32[256,512]{1,0:T(8,128)S(1)}, u32[]{:S(2)}, u32[]{:S(2)}) collective-permute-start(f32[256,512]{1,0:T(8,128)S(1)} %collective-permute-done.12), channel_id=1, source_target_pairs={{0,496},{16,0},{32,16},{48,32},{64,48},{80,64},{96,80},{112,96},{1... | collective-permute-start | bytes 1572872 | tf_op jit(solution)/shard_map/ppermute | solution.py:30
  281.6 1.9 collective-permute-start.7
  283.6 4.1 %collective-permute-done.13 = f32[256,512]{1,0:T(8,128)S(1)} collective-permute-done((f32[256,512]{1,0:T(8,128)S(1)}, f32[256,512]{1,0:T(8,128)S(1)}, u32[]{:S(2)}, u32[]{:S(2)}) %collective-permute-start.13) | collective-permute-done | bytes 524320 | tf_op jit(solution)/shard_map/ppermute | solution.py:30
  287.7 5.9 %collective-permute-start.14 = (f32[256,512]{1,0:T(8,128)S(1)}, f32[256,512]{1,0:T(8,128)S(1)}, u32[]{:S(2)}, u32[]{:S(2)}) collective-permute-start(f32[256,512]{1,0:T(8,128)S(1)} %collective-permute-done.13), channel_id=1, source_target_pairs={{0,496},{16,0},{32,16},{48,32},{64,48},{80,64},{96,80},{112,96},{1... | collective-permute-start | bytes 1572872 | tf_op jit(solution)/shard_map/ppermute | solution.py:30
  293.9 1.9 collective-permute-start.8
  295.8 3.9 %collective-permute-done.14 = f32[256,512]{1,0:T(8,128)S(1)} collective-permute-done((f32[256,512]{1,0:T(8,128)S(1)}, f32[256,512]{1,0:T(8,128)S(1)}, u32[]{:S(2)}, u32[]{:S(2)}) %collective-permute-start.14) | collective-permute-done | bytes 524320 | tf_op jit(solution)/shard_map/ppermute | solution.py:30
  299.7 5.9 %collective-permute-start.15 = (f32[256,512]{1,0:T(8,128)S(1)}, f32[256,512]{1,0:T(8,128)}, u32[]{:S(2)}, u32[]{:S(2)}) collective-permute-start(f32[256,512]{1,0:T(8,128)S(1)} %collective-permute-done.14), channel_id=1, source_target_pairs={{0,496},{16,0},{32,16},{48,32},{64,48},{80,64},{96,80},{112,96},{1... | collective-permute-start | bytes 1572872 | tf_op jit(solution)/shard_map/ppermute | solution.py:30
  305.7 2.4 constant_dynamic-slice_fusion.1
  308.1 2.3 fusion.13
  311.5 2.1 fusion.5
  313.6 2.1 fusion.1
  317.8 2.9 convolution_add_fusion
  (43 shorter events, 11.8 us)
Async XLA Ops:
  6.5 299.2 %all-gather.2.cloned.1.call-start = ((), (), s32[]{:S(2)}) async-start(), calls=%async_computation | async-start | bytes 8912896 | tf_op jit(solution)/shard_map/all_gather | solution.py:88
  9.4 76.7 %collective-permute-start = (f32[256,256]{1,0:T(8,128)S(1)}, f32[256,256]{1,0:T(8,128)S(1)}, u32[]{:S(2)}, u32[]{:S(2)}) collective-permute-start(f32[256,256]{1,0:T(8,128)S(1)} %get-tuple-element.19), channel_id=1, source_target_pairs={{0,0},{1,32},{2,64},{3,96},{4,128},{5,160},{6,192},{7,224},{8,256}... | collective-permute-start | bytes 786440 | tf_op jit(solution)/shard_map/ppermute | solution.py:15
  20.9 69.5 %collective-permute-start.1 = (f32[256,256]{1,0:T(8,128)S(1)}, f32[256,256]{1,0:T(8,128)S(1)}, u32[]{:S(2)}, u32[]{:S(2)}) collective-permute-start(f32[256,256]{1,0:T(8,128)S(1)} %get-tuple-element.20), channel_id=1, source_target_pairs={{0,16},{1,48},{2,80},{3,112},{4,144},{5,176},{6,208},{7,240},{8,27... | collective-permute-start | bytes 786440 | tf_op jit(solution)/shard_map/ppermute | solution.py:15
  92.3 125.5 %collective-permute-start.2 = (f32[256,512]{1,0:T(8,128)}, f32[256,512]{1,0:T(8,128)S(1)}, u32[]{:S(2)}, u32[]{:S(2)}) collective-permute-start(f32[256,512]{1,0:T(8,128)} %fusion.28), channel_id=1, source_target_pairs={{0,416},{1,385},{2,354},{3,323},{4,292},{5,261},{6,230},{7,199},{8... | collective-permute-start | bytes 1572872 | tf_op jit(solution)/shard_map/ppermute | solution.py:15
  217.8 20.7 %copy-start = (f32[256,512]{1,0:T(8,128)}, f32[256,512]{1,0:T(8,128)S(1)}, u32[]{:S(2)}) copy-start(f32[256,512]{1,0:T(8,128)S(1)} %collective-permute-done.2) | copy-start | bytes 1572868
  217.8 10.5 %collective-permute-start.9 = (f32[256,512]{1,0:T(8,128)S(1)}, f32[256,512]{1,0:T(8,128)S(1)}, u32[]{:S(2)}, u32[]{:S(2)}) collective-permute-start(f32[256,512]{1,0:T(8,128)S(1)} %collective-permute-done.2), channel_id=1, source_target_pairs={{0,496},{16,0},{32,16},{48,32},{64,48},{80,64},{96,80},{112,96},{1... | collective-permute-start | bytes 1572872 | tf_op jit(solution)/shard_map/ppermute | solution.py:30
  219.8 16.9 %collective-permute-start.3 = (f32[256,512]{1,0:T(8,128)S(1)}, f32[256,512]{1,0:T(8,128)S(1)}, u32[]{:S(2)}, u32[]{:S(2)}) collective-permute-start(f32[256,512]{1,0:T(8,128)S(1)} %collective-permute-done.2), channel_id=1, source_target_pairs={{0,16},{16,32},{32,48},{48,64},{64,80},{80,96},{96,112},{112,128},... | collective-permute-start | bytes 1572872 | tf_op jit(solution)/shard_map/ppermute | solution.py:30
  228.3 25.8 %copy-start.1 = (f32[256,512]{1,0:T(8,128)}, f32[256,512]{1,0:T(8,128)S(1)}, u32[]{:S(2)}) copy-start(f32[256,512]{1,0:T(8,128)S(1)} %collective-permute-done.9) | copy-start | bytes 1572868
  228.3 12.8 %collective-permute-start.10 = (f32[256,512]{1,0:T(8,128)S(1)}, f32[256,512]{1,0:T(8,128)S(1)}, u32[]{:S(2)}, u32[]{:S(2)}) collective-permute-start(f32[256,512]{1,0:T(8,128)S(1)} %collective-permute-done.9), channel_id=1, source_target_pairs={{0,496},{16,0},{32,16},{48,32},{64,48},{80,64},{96,80},{112,96},{1... | collective-permute-start | bytes 1572872 | tf_op jit(solution)/shard_map/ppermute | solution.py:30
  236.6 32.3 %copy-start.2 = (f32[256,512]{1,0:T(8,128)}, f32[256,512]{1,0:T(8,128)S(1)}, u32[]{:S(2)}) copy-start(f32[256,512]{1,0:T(8,128)S(1)} %collective-permute-done.3) | copy-start | bytes 1572868
  236.6 15.6 %collective-permute-start.4 = (f32[256,512]{1,0:T(8,128)S(1)}, f32[256,512]{1,0:T(8,128)S(1)}, u32[]{:S(2)}, u32[]{:S(2)}) collective-permute-start(f32[256,512]{1,0:T(8,128)S(1)} %collective-permute-done.3), channel_id=1, source_target_pairs={{0,16},{16,32},{32,48},{48,64},{64,80},{80,96},{96,112},{112,128},... | collective-permute-start | bytes 1572872 | tf_op jit(solution)/shard_map/ppermute | solution.py:30
  241.1 16.9 %collective-permute-start.11 = (f32[256,512]{1,0:T(8,128)S(1)}, f32[256,512]{1,0:T(8,128)S(1)}, u32[]{:S(2)}, u32[]{:S(2)}) collective-permute-start(f32[256,512]{1,0:T(8,128)S(1)} %collective-permute-done.10), channel_id=1, source_target_pairs={{0,496},{16,0},{32,16},{48,32},{64,48},{80,64},{96,80},{112,96},{1... | collective-permute-start | bytes 1572872 | tf_op jit(solution)/shard_map/ppermute | solution.py:30
  252.2 31.3 %copy-start.4 = (f32[256,512]{1,0:T(8,128)}, f32[256,512]{1,0:T(8,128)S(1)}, u32[]{:S(2)}) copy-start(f32[256,512]{1,0:T(8,128)S(1)} %collective-permute-done.4) | copy-start | bytes 1572868
  252.2 14.8 %collective-permute-start.5 = (f32[256,512]{1,0:T(8,128)S(1)}, f32[256,512]{1,0:T(8,128)S(1)}, u32[]{:S(2)}, u32[]{:S(2)}) collective-permute-start(f32[256,512]{1,0:T(8,128)S(1)} %collective-permute-done.4), channel_id=1, source_target_pairs={{0,16},{16,32},{32,48},{48,64},{64,80},{80,96},{96,112},{112,128},... | collective-permute-start | bytes 1572872 | tf_op jit(solution)/shard_map/ppermute | solution.py:30
  258.1 17.2 %collective-permute-start.12 = (f32[256,512]{1,0:T(8,128)S(1)}, f32[256,512]{1,0:T(8,128)S(1)}, u32[]{:S(2)}, u32[]{:S(2)}) collective-permute-start(f32[256,512]{1,0:T(8,128)S(1)} %collective-permute-done.11), channel_id=1, source_target_pairs={{0,496},{16,0},{32,16},{48,32},{64,48},{80,64},{96,80},{112,96},{1... | collective-permute-start | bytes 1572872 | tf_op jit(solution)/shard_map/ppermute | solution.py:30
  267.0 14.6 %copy-start.6 = (f32[256,512]{1,0:T(8,128)}, f32[256,512]{1,0:T(8,128)S(1)}, u32[]{:S(2)}) copy-start(f32[256,512]{1,0:T(8,128)S(1)} %collective-permute-done.5) | copy-start | bytes 1572868
  267.0 14.6 %collective-permute-start.6 = (f32[256,512]{1,0:T(8,128)S(1)}, f32[256,512]{1,0:T(8,128)}, u32[]{:S(2)}, u32[]{:S(2)}) collective-permute-start(f32[256,512]{1,0:T(8,128)S(1)} %collective-permute-done.5), channel_id=1, source_target_pairs={{0,16},{16,32},{32,48},{48,64},{64,80},{80,96},{96,112},{112,128},... | collective-permute-start | bytes 1572872 | tf_op jit(solution)/shard_map/ppermute | solution.py:30
  275.3 12.4 %collective-permute-start.13 = (f32[256,512]{1,0:T(8,128)S(1)}, f32[256,512]{1,0:T(8,128)S(1)}, u32[]{:S(2)}, u32[]{:S(2)}) collective-permute-start(f32[256,512]{1,0:T(8,128)S(1)} %collective-permute-done.12), channel_id=1, source_target_pairs={{0,496},{16,0},{32,16},{48,32},{64,48},{80,64},{96,80},{112,96},{1... | collective-permute-start | bytes 1572872 | tf_op jit(solution)/shard_map/ppermute | solution.py:30
  281.6 12.2 %collective-permute-start.7 = (f32[256,512]{1,0:T(8,128)}, f32[256,512]{1,0:T(8,128)S(1)}, u32[]{:S(2)}, u32[]{:S(2)}) collective-permute-start(f32[256,512]{1,0:T(8,128)} %collective-permute-done.6), channel_id=1, source_target_pairs={{0,16},{16,32},{32,48},{48,64},{64,80},{80,96},{96,112},{112,128},... | collective-permute-start | bytes 1572872 | tf_op jit(solution)/shard_map/ppermute | solution.py:30
  287.7 12.0 %collective-permute-start.14 = (f32[256,512]{1,0:T(8,128)S(1)}, f32[256,512]{1,0:T(8,128)S(1)}, u32[]{:S(2)}, u32[]{:S(2)}) collective-permute-start(f32[256,512]{1,0:T(8,128)S(1)} %collective-permute-done.13), channel_id=1, source_target_pairs={{0,496},{16,0},{32,16},{48,32},{64,48},{80,64},{96,80},{112,96},{1... | collective-permute-start | bytes 1572872 | tf_op jit(solution)/shard_map/ppermute | solution.py:30
  293.9 19.7 %collective-permute-start.8 = (f32[256,512]{1,0:T(8,128)S(1)}, f32[256,512]{1,0:T(8,128)}, u32[]{:S(2)}, u32[]{:S(2)}) collective-permute-start(f32[256,512]{1,0:T(8,128)S(1)} %collective-permute-done.7), channel_id=1, source_target_pairs={{0,16},{16,32},{32,48},{48,64},{64,80},{80,96},{96,112},{112,128},... | collective-permute-start | bytes 1572872 | tf_op jit(solution)/shard_map/ppermute | solution.py:30
  299.7 18.1 %collective-permute-start.15 = (f32[256,512]{1,0:T(8,128)S(1)}, f32[256,512]{1,0:T(8,128)}, u32[]{:S(2)}, u32[]{:S(2)}) collective-permute-start(f32[256,512]{1,0:T(8,128)S(1)} %collective-permute-done.14), channel_id=1, source_target_pairs={{0,496},{16,0},{32,16},{48,32},{64,48},{80,64},{96,80},{112,96},{1... | collective-permute-start | bytes 1572872 | tf_op jit(solution)/shard_map/ppermute | solution.py:30
  305.7 4.7 %copy-start.3 = (f32[256,512]{1,0:T(8,128)S(1)}, f32[256,512]{1,0:T(8,128)}, u32[]{:S(2)}) copy-start(f32[256,512]{1,0:T(8,128)} %copy-done.2) | copy-start | bytes 1572868
  305.7 4.7 %copy-start.5 = (f32[256,512]{1,0:T(8,128)S(1)}, f32[256,512]{1,0:T(8,128)}, u32[]{:S(2)}) copy-start(f32[256,512]{1,0:T(8,128)} %copy-done.4) | copy-start | bytes 1572868
  305.7 5.7 %copy-start.7 = (f32[256,512]{1,0:T(8,128)S(1)}, f32[256,512]{1,0:T(8,128)}, u32[]{:S(2)}) copy-start(f32[256,512]{1,0:T(8,128)} %copy-done.6) | copy-start | bytes 1572868
Sparse Core Ops, SparseCore 0:
  92.5 138.7 all-gather.1

commit v13 on v12

--- a/solution.py
+++ b/solution.py
@@ -86,7 +86,7 @@
     density = (half_tri + mirrored) * live_rows[:, None] * live_cols[None, :]
     group = upper.shape[0]
     row_panel = lax.all_gather(density, "col", axis=1, tiled=True)
-    middle = STEPS // 2 - 1
+    middle = STEPS // 2
     centre = send(density, right_pairs(row_count, col_count, middle))
     ahead = centre
     behind = centre

time: 328 us -> 282 us (0.86)
  the two profiles are of different devices: /device:TPU:15 before, /device:TPU:38 now
where the time goes in v13:
time: 282 us; the launch traced here: 281 us
  waiting for transfers between devices  168 us (60%)
  starting transfers between devices  77.7 us (28%)
  between operations  14 us (5%)
  matrix products  12.5 us (4%)
  local copies, waits for them, and re-layouts  4.6 us (2%)
  other arithmetic  4.43 us (2%)
    ppermute x13, waiting for transfers between devices, shift(): lax.ppermute(value, axis, [(i, (i - by) % length) for i in range(length)])  99.3 us
    ppermute x3, waiting for transfers between devices, send(): return lax.ppermute(value, AXES, pairs)  68.6 us
    ppermute x13, starting transfers between devices, shift(): lax.ppermute(value, axis, [(i, (i - by) % length) for i in range(length)])  60.9 us
    ppermute x3, starting transfers between devices, send(): return lax.ppermute(value, AXES, pairs)  16.8 us
    dot_general x7, matrix products, body(): jnp.dot(left, right, precision=lax.Precision.HIGHEST, preferred_element_t...  12.5 us
  transfers between devices with their start and end apart: 17, of which 11 were waited for; matrix products, arithmetic and copies ran while one was open for 5% of the time, Pallas kernels for 0%

profile of v13, /device:TPU:38, one launch (start us, length us, event | category | flops | bytes accessed | tf_op | source)
XLA Modules:
  0.0 281.2 jit_solution(18093864656037670446)
XLA Ops:
  9.4 10.7 %collective-permute-start = (f32[256,256]{1,0:T(8,128)S(1)}, f32[256,256]{1,0:T(8,128)S(1)}, u32[]{:S(2)}, u32[]{:S(2)}) collective-permute-start(f32[256,256]{1,0:T(8,128)S(1)} %get-tuple-element.19), channel_id=1, source_target_pairs={{0,0},{1,32},{2,64},{3,96},{4,128},{5,160},{6,192},{7,224},{8,256}... | collective-permute-start | bytes 786440 | tf_op jit(solution)/shard_map/ppermute | solution.py:15
  20.1 4.2 %collective-permute-start.1 = (f32[256,256]{1,0:T(8,128)S(1)}, f32[256,256]{1,0:T(8,128)S(1)}, u32[]{:S(2)}, u32[]{:S(2)}) collective-permute-start(f32[256,256]{1,0:T(8,128)S(1)} %get-tuple-element.20), channel_id=1, source_target_pairs={{0,16},{1,48},{2,80},{3,112},{4,144},{5,176},{6,208},{7,240},{8,27... | collective-permute-start | bytes 786440 | tf_op jit(solution)/shard_map/ppermute | solution.py:15
  26.1 40.0 %collective-permute-done = f32[256,256]{1,0:T(8,128)S(1)} collective-permute-done((f32[256,256]{1,0:T(8,128)S(1)}, f32[256,256]{1,0:T(8,128)S(1)}, u32[]{:S(2)}, u32[]{:S(2)}) %collective-permute-start) | collective-permute-done | bytes 262176 | tf_op jit(solution)/shard_map/ppermute | solution.py:15
  66.1 9.4 %collective-permute-done.1 = f32[256,256]{1,0:T(8,128)S(1)} collective-permute-done((f32[256,256]{1,0:T(8,128)S(1)}, f32[256,256]{1,0:T(8,128)S(1)}, u32[]{:S(2)}, u32[]{:S(2)}) %collective-permute-start.1) | collective-permute-done | bytes 262176 | tf_op jit(solution)/shard_map/ppermute | solution.py:15
  75.5 2.0 fusion.28
  77.4 1.9 collective-permute-start.2
  79.4 19.3 %collective-permute-done.2 = f32[256,512]{1,0:T(8,128)S(1)} collective-permute-done((f32[256,512]{1,0:T(8,128)}, f32[256,512]{1,0:T(8,128)S(1)}, u32[]{:S(2)}, u32[]{:S(2)}) %collective-permute-start.2) | collective-permute-done | bytes 524320 | tf_op jit(solution)/shard_map/ppermute | solution.py:15
  98.7 1.9 collective-permute-start.3
  100.6 7.8 %collective-permute-start.10 = (f32[256,512]{1,0:T(8,128)S(1)}, f32[256,512]{1,0:T(8,128)S(1)}, u32[]{:S(2)}, u32[]{:S(2)}) collective-permute-start(f32[256,512]{1,0:T(8,128)S(1)} %collective-permute-done.2), channel_id=1, source_target_pairs={{0,496},{16,0},{32,16},{48,32},{64,48},{80,64},{96,80},{112,96},{1... | collective-permute-start | bytes 1572872 | tf_op jit(solution)/shard_map/ppermute | solution.py:30
  108.4 12.6 %collective-permute-done.3 = f32[256,512]{1,0:T(8,128)S(1)} collective-permute-done((f32[256,512]{1,0:T(8,128)S(1)}, f32[256,512]{1,0:T(8,128)S(1)}, u32[]{:S(2)}, u32[]{:S(2)}) %collective-permute-start.3) | collective-permute-done | bytes 524320 | tf_op jit(solution)/shard_map/ppermute | solution.py:30
  121.1 1.9 collective-permute-start.4
  123.0 7.8 %collective-permute-start.11 = (f32[256,512]{1,0:T(8,128)S(1)}, f32[256,512]{1,0:T(8,128)S(1)}, u32[]{:S(2)}, u32[]{:S(2)}) collective-permute-start(f32[256,512]{1,0:T(8,128)S(1)} %collective-permute-done.10), channel_id=1, source_target_pairs={{0,496},{16,0},{32,16},{48,32},{64,48},{80,64},{96,80},{112,96},{1... | collective-permute-start | bytes 1572872 | tf_op jit(solution)/shard_map/ppermute | solution.py:30
  130.9 6.5 %collective-permute-done.4 = f32[256,512]{1,0:T(8,128)S(1)} collective-permute-done((f32[256,512]{1,0:T(8,128)S(1)}, f32[256,512]{1,0:T(8,128)S(1)}, u32[]{:S(2)}, u32[]{:S(2)}) %collective-permute-start.4) | collective-permute-done | bytes 524320 | tf_op jit(solution)/shard_map/ppermute | solution.py:30
  137.4 1.9 collective-permute-start.5
  139.3 7.8 %collective-permute-start.12 = (f32[256,512]{1,0:T(8,128)S(1)}, f32[256,512]{1,0:T(8,128)S(1)}, u32[]{:S(2)}, u32[]{:S(2)}) collective-permute-start(f32[256,512]{1,0:T(8,128)S(1)} %collective-permute-done.11), channel_id=1, source_target_pairs={{0,496},{16,0},{32,16},{48,32},{64,48},{80,64},{96,80},{112,96},{1... | collective-permute-start | bytes 1572872 | tf_op jit(solution)/shard_map/ppermute | solution.py:30
  147.2 33.2 %collective-permute-done.5 = f32[256,512]{1,0:T(8,128)S(1)} collective-permute-done((f32[256,512]{1,0:T(8,128)S(1)}, f32[256,512]{1,0:T(8,128)S(1)}, u32[]{:S(2)}, u32[]{:S(2)}) %collective-permute-start.5) | collective-permute-done | bytes 524320 | tf_op jit(solution)/shard_map/ppermute | solution.py:30
  180.3 1.9 collective-permute-start.6
  182.3 2.3 collective-permute-done.12
  184.5 8.4 %collective-permute-start.13 = (f32[256,512]{1,0:T(8,128)S(1)}, f32[256,512]{1,0:T(8,128)S(1)}, u32[]{:S(2)}, u32[]{:S(2)}) collective-permute-start(f32[256,512]{1,0:T(8,128)S(1)} %collective-permute-done.12), channel_id=1, source_target_pairs={{0,496},{16,0},{32,16},{48,32},{64,48},{80,64},{96,80},{112,96},{1... | collective-permute-start | bytes 1572872 | tf_op jit(solution)/shard_map/ppermute | solution.py:30
  192.9 19.2 %collective-permute-done.6 = f32[256,512]{1,0:T(8,128)S(1)} collective-permute-done((f32[256,512]{1,0:T(8,128)S(1)}, f32[256,512]{1,0:T(8,128)S(1)}, u32[]{:S(2)}, u32[]{:S(2)}) %collective-permute-start.6) | collective-permute-done | bytes 524320 | tf_op jit(solution)/shard_map/ppermute | solution.py:30
  212.1 1.9 collective-permute-start.7
  214.1 7.8 %collective-permute-start.14 = (f32[256,512]{1,0:T(8,128)S(1)}, f32[256,512]{1,0:T(8,128)S(1)}, u32[]{:S(2)}, u32[]{:S(2)}) collective-permute-start(f32[256,512]{1,0:T(8,128)S(1)} %collective-permute-done.13), channel_id=1, source_target_pairs={{0,496},{16,0},{32,16},{48,32},{64,48},{80,64},{96,80},{112,96},{1... | collective-permute-start | bytes 1572872 | tf_op jit(solution)/shard_map/ppermute | solution.py:30
  221.9 9.4 %collective-permute-done.7 = f32[256,512]{1,0:T(8,128)} collective-permute-done((f32[256,512]{1,0:T(8,128)S(1)}, f32[256,512]{1,0:T(8,128)}, u32[]{:S(2)}, u32[]{:S(2)}) %collective-permute-start.7) | collective-permute-done | bytes 524320 | tf_op jit(solution)/shard_map/ppermute | solution.py:30
  233.5 7.8 %collective-permute-start.15 = (f32[256,512]{1,0:T(8,128)S(1)}, f32[256,512]{1,0:T(8,128)}, u32[]{:S(2)}, u32[]{:S(2)}) collective-permute-start(f32[256,512]{1,0:T(8,128)S(1)} %collective-permute-done.14), channel_id=1, source_target_pairs={{0,496},{16,0},{32,16},{48,32},{64,48},{80,64},{96,80},{112,96},{1... | collective-permute-start | bytes 1572872 | tf_op jit(solution)/shard_map/ppermute | solution.py:30
  241.3 10.8 %collective-permute-done.8 = f32[256,512]{1,0:T(8,128)S(1)} collective-permute-done((f32[256,512]{1,0:T(8,128)}, f32[256,512]{1,0:T(8,128)S(1)}, u32[]{:S(2)}, u32[]{:S(2)}) %collective-permute-start.8) | collective-permute-done | bytes 524320 | tf_op jit(solution)/shard_map/ppermute | solution.py:30
  252.1 1.9 collective-permute-start.9
  254.1 2.4 constant_dynamic-slice_fusion.1
  256.5 2.3 fusion.13
  259.8 2.1 fusion.5
  261.9 5.3 %collective-permute-done.9 = f32[256,512]{1,0:T(8,128)} collective-permute-done((f32[256,512]{1,0:T(8,128)S(1)}, f32[256,512]{1,0:T(8,128)}, u32[]{:S(2)}, u32[]{:S(2)}) %collective-permute-start.9) | collective-permute-done | bytes 524320 | tf_op jit(solution)/shard_map/ppermute | solution.py:30
  267.2 2.1 fusion.1
  271.5 2.9 %convolution_add_fusion = f32[256,512]{1,0:T(8,128)} fusion(f32[256,512]{1,0:T(8,128)S(1)} %convolution_add_fusion.1, f32[256,512]{1,0:T(8,128)} %collective-permute-done.15, f32[256,512]{1,0:T(8,128)S(1)} %collective-permute-done.14, f32[256,256]{1,0:T(8,128)S(1)} %get-tuple-element.6, f32[256,256]{1,0:T(8,128)S(1)} %get-tuple-element.5), kind=kOutput, calls=%fused_computation | convolution fusion | flops 805830656 | bytes 2621440 | tf_op jit(solution)/shard_map/dot_general | solution.py:110
  (43 shorter events, 9.8 us)
Async XLA Ops:
  6.5 247.5 %all-gather.2.cloned.1.call-start = ((), (), s32[]{:S(2)}) async-start(), calls=%async_computation | async-start | bytes 8912896 | tf_op jit(solution)/shard_map/all_gather | solution.py:88
  9.4 56.7 %collective-permute-start = (f32[256,256]{1,0:T(8,128)S(1)}, f32[256,256]{1,0:T(8,128)S(1)}, u32[]{:S(2)}, u32[]{:S(2)}) collective-permute-start(f32[256,256]{1,0:T(8,128)S(1)} %get-tuple-element.19), channel_id=1, source_target_pairs={{0,0},{1,32},{2,64},{3,96},{4,128},{5,160},{6,192},{7,224},{8,256}... | collective-permute-start | bytes 786440 | tf_op jit(solution)/shard_map/ppermute | solution.py:15
  20.1 55.3 %collective-permute-start.1 = (f32[256,256]{1,0:T(8,128)S(1)}, f32[256,256]{1,0:T(8,128)S(1)}, u32[]{:S(2)}, u32[]{:S(2)}) collective-permute-start(f32[256,256]{1,0:T(8,128)S(1)} %get-tuple-element.20), channel_id=1, source_target_pairs={{0,16},{1,48},{2,80},{3,112},{4,144},{5,176},{6,208},{7,240},{8,27... | collective-permute-start | bytes 786440 | tf_op jit(solution)/shard_map/ppermute | solution.py:15
  77.4 21.2 %collective-permute-start.2 = (f32[256,512]{1,0:T(8,128)}, f32[256,512]{1,0:T(8,128)S(1)}, u32[]{:S(2)}, u32[]{:S(2)}) collective-permute-start(f32[256,512]{1,0:T(8,128)} %fusion.28), channel_id=1, source_target_pairs={{0,400},{1,369},{2,338},{3,307},{4,276},{5,245},{6,214},{7,183},{8... | collective-permute-start | bytes 1572872 | tf_op jit(solution)/shard_map/ppermute | solution.py:15
  98.7 24.3 %copy-start = (f32[256,512]{1,0:T(8,128)}, f32[256,512]{1,0:T(8,128)S(1)}, u32[]{:S(2)}) copy-start(f32[256,512]{1,0:T(8,128)S(1)} %collective-permute-done.2) | copy-start | bytes 1572868
  98.7 22.4 %collective-permute-start.3 = (f32[256,512]{1,0:T(8,128)S(1)}, f32[256,512]{1,0:T(8,128)S(1)}, u32[]{:S(2)}, u32[]{:S(2)}) collective-permute-start(f32[256,512]{1,0:T(8,128)S(1)} %collective-permute-done.2), channel_id=1, source_target_pairs={{0,16},{16,32},{32,48},{48,64},{64,80},{80,96},{96,112},{112,128},... | collective-permute-start | bytes 1572872 | tf_op jit(solution)/shard_map/ppermute | solution.py:30
  100.6 22.4 %collective-permute-start.10 = (f32[256,512]{1,0:T(8,128)S(1)}, f32[256,512]{1,0:T(8,128)S(1)}, u32[]{:S(2)}, u32[]{:S(2)}) collective-permute-start(f32[256,512]{1,0:T(8,128)S(1)} %collective-permute-done.2), channel_id=1, source_target_pairs={{0,496},{16,0},{32,16},{48,32},{64,48},{80,64},{96,80},{112,96},{1... | collective-permute-start | bytes 1572872 | tf_op jit(solution)/shard_map/ppermute | solution.py:30
  121.1 18.2 %copy-start.1 = (f32[256,512]{1,0:T(8,128)}, f32[256,512]{1,0:T(8,128)S(1)}, u32[]{:S(2)}) copy-start(f32[256,512]{1,0:T(8,128)S(1)} %collective-permute-done.3) | copy-start | bytes 1572868
  121.1 16.3 %collective-permute-start.4 = (f32[256,512]{1,0:T(8,128)S(1)}, f32[256,512]{1,0:T(8,128)S(1)}, u32[]{:S(2)}, u32[]{:S(2)}) collective-permute-start(f32[256,512]{1,0:T(8,128)S(1)} %collective-permute-done.3), channel_id=1, source_target_pairs={{0,16},{16,32},{32,48},{48,64},{64,80},{80,96},{96,112},{112,128},... | collective-permute-start | bytes 1572872 | tf_op jit(solution)/shard_map/ppermute | solution.py:30
  123.0 16.3 %collective-permute-start.11 = (f32[256,512]{1,0:T(8,128)S(1)}, f32[256,512]{1,0:T(8,128)S(1)}, u32[]{:S(2)}, u32[]{:S(2)}) collective-permute-start(f32[256,512]{1,0:T(8,128)S(1)} %collective-permute-done.10), channel_id=1, source_target_pairs={{0,496},{16,0},{32,16},{48,32},{64,48},{80,64},{96,80},{112,96},{1... | collective-permute-start | bytes 1572872 | tf_op jit(solution)/shard_map/ppermute | solution.py:30
  137.4 44.9 %copy-start.2 = (f32[256,512]{1,0:T(8,128)}, f32[256,512]{1,0:T(8,128)S(1)}, u32[]{:S(2)}) copy-start(f32[256,512]{1,0:T(8,128)S(1)} %collective-permute-done.4) | copy-start | bytes 1572868
  137.4 43.0 %collective-permute-start.5 = (f32[256,512]{1,0:T(8,128)S(1)}, f32[256,512]{1,0:T(8,128)S(1)}, u32[]{:S(2)}, u32[]{:S(2)}) collective-permute-start(f32[256,512]{1,0:T(8,128)S(1)} %collective-permute-done.4), channel_id=1, source_target_pairs={{0,16},{16,32},{32,48},{48,64},{64,80},{80,96},{96,112},{112,128},... | collective-permute-start | bytes 1572872 | tf_op jit(solution)/shard_map/ppermute | solution.py:30
  139.3 45.2 %collective-permute-start.12 = (f32[256,512]{1,0:T(8,128)S(1)}, f32[256,512]{1,0:T(8,128)S(1)}, u32[]{:S(2)}, u32[]{:S(2)}) collective-permute-start(f32[256,512]{1,0:T(8,128)S(1)} %collective-permute-done.11), channel_id=1, source_target_pairs={{0,496},{16,0},{32,16},{48,32},{64,48},{80,64},{96,80},{112,96},{1... | collective-permute-start | bytes 1572872 | tf_op jit(solution)/shard_map/ppermute | solution.py:30
  180.3 33.7 %copy-start.4 = (f32[256,512]{1,0:T(8,128)}, f32[256,512]{1,0:T(8,128)S(1)}, u32[]{:S(2)}) copy-start(f32[256,512]{1,0:T(8,128)S(1)} %collective-permute-done.5) | copy-start | bytes 1572868
  180.3 31.8 %collective-permute-start.6 = (f32[256,512]{1,0:T(8,128)S(1)}, f32[256,512]{1,0:T(8,128)S(1)}, u32[]{:S(2)}, u32[]{:S(2)}) collective-permute-start(f32[256,512]{1,0:T(8,128)S(1)} %collective-permute-done.5), channel_id=1, source_target_pairs={{0,16},{16,32},{32,48},{48,64},{64,80},{80,96},{96,112},{112,128},... | collective-permute-start | bytes 1572872 | tf_op jit(solution)/shard_map/ppermute | solution.py:30
  184.5 29.5 %collective-permute-start.13 = (f32[256,512]{1,0:T(8,128)S(1)}, f32[256,512]{1,0:T(8,128)S(1)}, u32[]{:S(2)}, u32[]{:S(2)}) collective-permute-start(f32[256,512]{1,0:T(8,128)S(1)} %collective-permute-done.12), channel_id=1, source_target_pairs={{0,496},{16,0},{32,16},{48,32},{64,48},{80,64},{96,80},{112,96},{1... | collective-permute-start | bytes 1572872 | tf_op jit(solution)/shard_map/ppermute | solution.py:30
  212.1 9.8 %copy-start.6 = (f32[256,512]{1,0:T(8,128)}, f32[256,512]{1,0:T(8,128)S(1)}, u32[]{:S(2)}) copy-start(f32[256,512]{1,0:T(8,128)S(1)} %collective-permute-done.6) | copy-start | bytes 1572868
  212.1 19.2 %collective-permute-start.7 = (f32[256,512]{1,0:T(8,128)S(1)}, f32[256,512]{1,0:T(8,128)}, u32[]{:S(2)}, u32[]{:S(2)}) collective-permute-start(f32[256,512]{1,0:T(8,128)S(1)} %collective-permute-done.6), channel_id=1, source_target_pairs={{0,16},{16,32},{32,48},{48,64},{64,80},{80,96},{96,112},{112,128},... | collective-permute-start | bytes 1572872 | tf_op jit(solution)/shard_map/ppermute | solution.py:30
  214.1 19.4 %collective-permute-start.14 = (f32[256,512]{1,0:T(8,128)S(1)}, f32[256,512]{1,0:T(8,128)S(1)}, u32[]{:S(2)}, u32[]{:S(2)}) collective-permute-start(f32[256,512]{1,0:T(8,128)S(1)} %collective-permute-done.13), channel_id=1, source_target_pairs={{0,496},{16,0},{32,16},{48,32},{64,48},{80,64},{96,80},{112,96},{1... | collective-permute-start | bytes 1572872 | tf_op jit(solution)/shard_map/ppermute | solution.py:30
  231.3 20.8 %collective-permute-start.8 = (f32[256,512]{1,0:T(8,128)}, f32[256,512]{1,0:T(8,128)S(1)}, u32[]{:S(2)}, u32[]{:S(2)}) collective-permute-start(f32[256,512]{1,0:T(8,128)} %collective-permute-done.7), channel_id=1, source_target_pairs={{0,16},{16,32},{32,48},{48,64},{64,80},{80,96},{96,112},{112,128},... | collective-permute-start | bytes 1572872 | tf_op jit(solution)/shard_map/ppermute | solution.py:30
  233.5 38.0 %collective-permute-start.15 = (f32[256,512]{1,0:T(8,128)S(1)}, f32[256,512]{1,0:T(8,128)}, u32[]{:S(2)}, u32[]{:S(2)}) collective-permute-start(f32[256,512]{1,0:T(8,128)S(1)} %collective-permute-done.14), channel_id=1, source_target_pairs={{0,496},{16,0},{32,16},{48,32},{64,48},{80,64},{96,80},{112,96},{1... | collective-permute-start | bytes 1572872 | tf_op jit(solution)/shard_map/ppermute | solution.py:30
  252.1 15.1 %collective-permute-start.9 = (f32[256,512]{1,0:T(8,128)S(1)}, f32[256,512]{1,0:T(8,128)}, u32[]{:S(2)}, u32[]{:S(2)}) collective-permute-start(f32[256,512]{1,0:T(8,128)S(1)} %collective-permute-done.8), channel_id=1, source_target_pairs={{0,16},{16,32},{32,48},{48,64},{64,80},{80,96},{96,112},{112,128},... | collective-permute-start | bytes 1572872 | tf_op jit(solution)/shard_map/ppermute | solution.py:30
  254.1 4.7 %copy-start.3 = (f32[256,512]{1,0:T(8,128)S(1)}, f32[256,512]{1,0:T(8,128)}, u32[]{:S(2)}) copy-start(f32[256,512]{1,0:T(8,128)} %copy-done.2) | copy-start | bytes 1572868
  254.1 4.7 %copy-start.5 = (f32[256,512]{1,0:T(8,128)S(1)}, f32[256,512]{1,0:T(8,128)}, u32[]{:S(2)}) copy-start(f32[256,512]{1,0:T(8,128)} %copy-done.4) | copy-start | bytes 1572868
  254.1 5.7 %copy-start.7 = (f32[256,512]{1,0:T(8,128)S(1)}, f32[256,512]{1,0:T(8,128)}, u32[]{:S(2)}) copy-start(f32[256,512]{1,0:T(8,128)} %copy-done.6) | copy-start | bytes 1572868
Sparse Core Ops, SparseCore 0:
  77.6 137.1 all-gather.1

commit v14 on v13

--- a/solution.py
+++ b/solution.py
@@ -86,19 +86,22 @@
     density = (half_tri + mirrored) * live_rows[:, None] * live_cols[None, :]
     group = upper.shape[0]
     row_panel = lax.all_gather(density, "col", axis=1, tiled=True)
-    middle = STEPS // 2
-    centre = send(density, right_pairs(row_count, col_count, middle))
-    ahead = centre
-    behind = centre
-    after = []
-    before = []
-    for _ in range(STEPS - 1 - middle):
-        ahead = shift(ahead, "row", 1)
-        after.append(ahead)
-    for _ in range(middle):
-        behind = shift(behind, "row", -1)
-        before.insert(0, behind)
-    pieces = before + [centre] + after
+    split = STEPS // 2
+    spans = ((3, split - 1 - 3), (4, STEPS - split - 1 - 4))
+    centres = [send(density, right_pairs(row_count, col_count, split * k + back)) for k, (back, _) in enumerate(spans)]
+    lanes = [([], [centre], []) for centre in centres]
+    for direction, side in ((1, 2), (-1, 0)):
+        states = list(centres)
+        for step in range(max(spans[k][0 if direction < 0 else 1] for k in range(2))):
+            live = [k for k in range(2) if step < spans[k][0 if direction < 0 else 1]]
+            moved = shift(jnp.stack([states[k] for k in live]), "row", direction)
+            for slot, k in enumerate(live):
+                states[k] = moved[slot]
+                if direction > 0:
+                    lanes[k][side].append(moved[slot])
+                else:
+                    lanes[k][side].insert(0, moved[slot])
+    pieces = [p for lane in lanes for part in lane for p in part]
     total = None
     for step in range(0, STEPS, 2):
         lefts = []

time: 282 us -> 323 us (1.15)
  the two profiles are of different devices: /device:TPU:38 before, /device:TPU:57 now
where the time goes in v14:
time: 323 us; the launch traced here: 320 us
  starting transfers between devices  161 us (50%)
  waiting for transfers between devices  117 us (36%)
  between operations  13.9 us (4%)
  local copies, waits for them, and re-layouts  12.8 us (4%)
  matrix products  10.6 us (3%)
  other arithmetic  4.5 us (1%)
    ppermute x7, starting transfers between devices, shift(): lax.ppermute(value, axis, [(i, (i - by) % length) for i in range(length)])  119 us
    ppermute x7, waiting for transfers between devices, shift(): lax.ppermute(value, axis, [(i, (i - by) % length) for i in range(length)])  63.3 us
    ppermute x4, waiting for transfers between devices, send(): return lax.ppermute(value, AXES, pairs)  53.9 us
    ppermute x4, starting transfers between devices, send(): return lax.ppermute(value, AXES, pairs)  42 us
    dot_general x7, matrix products, body(): jnp.dot(left, right, precision=lax.Precision.HIGHEST, preferred_element_t...  10.6 us
  transfers between devices with their start and end apart: 12, of which 7 were waited for; matrix products, arithmetic and copies ran while one was open for 5% of the time, Pallas kernels for 0%

profile of v14, /device:TPU:57, one launch (start us, length us, event | category | flops | bytes accessed | tf_op | source)
XLA Modules:
  0.0 319.6 jit_solution(3716600216461301886)
XLA Ops:
  8.0 1.2 copy.8
  9.4 9.6 %collective-permute-start = (f32[256,256]{1,0:T(8,128)S(1)}, f32[256,256]{1,0:T(8,128)S(1)}, u32[]{:S(2)}, u32[]{:S(2)}) collective-permute-start(f32[256,256]{1,0:T(8,128)S(1)} %get-tuple-element.31), channel_id=1, source_target_pairs={{0,0},{1,32},{2,64},{3,96},{4,128},{5,160},{6,192},{7,224},{8,256}... | collective-permute-start | bytes 786440 | tf_op jit(solution)/shard_map/ppermute | solution.py:15
  19.0 3.7 %collective-permute-start.1 = (f32[256,256]{1,0:T(8,128)S(1)}, f32[256,256]{1,0:T(8,128)S(1)}, u32[]{:S(2)}, u32[]{:S(2)}) collective-permute-start(f32[256,256]{1,0:T(8,128)S(1)} %get-tuple-element.32), channel_id=1, source_target_pairs={{0,16},{1,48},{2,80},{3,112},{4,144},{5,176},{6,208},{7,240},{8,27... | collective-permute-start | bytes 786440 | tf_op jit(solution)/shard_map/ppermute | solution.py:15
  24.6 3.6 %collective-permute-done = f32[256,256]{1,0:T(8,128)S(1)} collective-permute-done((f32[256,256]{1,0:T(8,128)S(1)}, f32[256,256]{1,0:T(8,128)S(1)}, u32[]{:S(2)}, u32[]{:S(2)}) %collective-permute-start) | collective-permute-done | bytes 262176 | tf_op jit(solution)/shard_map/ppermute | solution.py:15
  28.2 8.9 %collective-permute-done.1 = f32[256,256]{1,0:T(8,128)S(1)} collective-permute-done((f32[256,256]{1,0:T(8,128)S(1)}, f32[256,256]{1,0:T(8,128)S(1)}, u32[]{:S(2)}, u32[]{:S(2)}) %collective-permute-start.1) | collective-permute-done | bytes 262176 | tf_op jit(solution)/shard_map/ppermute | solution.py:15
  37.0 2.0 fusion.24
  39.0 1.9 collective-permute-start.3
  40.9 26.7 %collective-permute-start.2 = (f32[256,512]{1,0:T(8,128)}, f32[256,512]{1,0:T(8,128)S(1)}, u32[]{:S(2)}, u32[]{:S(2)}) collective-permute-start(f32[256,512]{1,0:T(8,128)} %fusion.24), channel_id=1, source_target_pairs={{0,464},{1,433},{2,402},{3,371},{4,340},{5,309},{6,278},{7,247},{8... | collective-permute-start | bytes 1572872 | tf_op jit(solution)/shard_map/ppermute | solution.py:15
  67.7 41.4 %collective-permute-done.3 = f32[256,512]{1,0:T(8,128)S(1)} collective-permute-done((f32[256,512]{1,0:T(8,128)}, f32[256,512]{1,0:T(8,128)S(1)}, u32[]{:S(2)}, u32[]{:S(2)}) %collective-permute-start.3) | collective-permute-done | bytes 524320 | tf_op jit(solution)/shard_map/ppermute | solution.py:15
  110.0 15.2 %collective-permute-start.4 = (f32[2,256,512]{2,1,0:T(8,128)S(1)}, f32[2,256,512]{2,1,0:T(8,128)S(1)}, u32[]{:S(2)}, u32[]{:S(2)}) collective-permute-start(f32[2,256,512]{2,1,0:T(8,128)S(1)} %pad_maximum_fusion), channel_id=1, source_target_pairs={{0,16},{16,32},{32,48},{48,64},{64,80},{80,96},{96,112},{112,128},... | collective-permute-start | bytes 3145736 | tf_op jit(solution)/shard_map/ppermute | solution.py:30
  125.2 86.7 %collective-permute-start.7 = (f32[2,256,512]{2,1,0:T(8,128)S(1)}, f32[2,256,512]{2,1,0:T(8,128)S(1)}, u32[]{:S(2)}, u32[]{:S(2)}) collective-permute-start(f32[2,256,512]{2,1,0:T(8,128)S(1)} %pad_maximum_fusion), channel_id=1, source_target_pairs={{0,496},{16,0},{32,16},{48,32},{64,48},{80,64},{96,80},{112,96},{1... | collective-permute-start | bytes 3145736 | tf_op jit(solution)/shard_map/ppermute | solution.py:30
  211.9 23.2 %collective-permute-done.4 = f32[2,256,512]{2,1,0:T(8,128)S(1)} collective-permute-done((f32[2,256,512]{2,1,0:T(8,128)S(1)}, f32[2,256,512]{2,1,0:T(8,128)S(1)}, u32[]{:S(2)}, u32[]{:S(2)}) %collective-permute-start.4) | collective-permute-done | bytes 1048608 | tf_op jit(solution)/shard_map/ppermute | solution.py:30
  235.1 1.9 collective-permute-start.5
  237.0 5.5 %collective-permute-start.8 = (f32[2,256,512]{2,1,0:T(8,128)S(1)}, f32[2,256,512]{2,1,0:T(8,128)}, u32[]{:S(2)}, u32[]{:S(2)}) collective-permute-start(f32[2,256,512]{2,1,0:T(8,128)S(1)} %collective-permute-done.7), channel_id=1, source_target_pairs={{0,496},{16,0},{32,16},{48,32},{64,48},{80,64},{96,80},{112,96},{1... | collective-permute-start | bytes 3145736 | tf_op jit(solution)/shard_map/ppermute | solution.py:30
  242.7 20.4 %collective-permute-done.5 = f32[2,256,512]{2,1,0:T(8,128)} collective-permute-done((f32[2,256,512]{2,1,0:T(8,128)S(1)}, f32[2,256,512]{2,1,0:T(8,128)}, u32[]{:S(2)}, u32[]{:S(2)}) %collective-permute-start.5) | collective-permute-done | bytes 1048608 | tf_op jit(solution)/shard_map/ppermute | solution.py:30
  263.1 1.9 collective-permute-start.6
  265.9 1.1 slice_bitcast_fusion.2
  267.0 2.2 slice_bitcast_fusion
  269.2 5.5 %collective-permute-start.9 = (f32[1,256,512]{2,1,0:T(8,128)}, f32[1,256,512]{2,1,0:T(8,128)}, u32[]{:S(2)}, u32[]{:S(2)}) collective-permute-start(f32[1,256,512]{2,1,0:T(8,128)} %get-tuple-element.23), channel_id=1, source_target_pairs={{0,496},{16,0},{32,16},{48,32},{64,48},{80,64},{96,80},{112,96},{1... | collective-permute-start | bytes 1572872 | tf_op jit(solution)/shard_map/ppermute | solution.py:30
  274.7 2.3 slice_bitcast_fusion.3
  276.9 13.4 %collective-permute-done.6 = f32[2,256,512]{2,1,0:T(8,128)S(1)} collective-permute-done((f32[2,256,512]{2,1,0:T(8,128)}, f32[2,256,512]{2,1,0:T(8,128)S(1)}, u32[]{:S(2)}, u32[]{:S(2)}) %collective-permute-start.6) | collective-permute-done | bytes 1048608 | tf_op jit(solution)/shard_map/ppermute | solution.py:30
  290.3 1.0 slice_bitcast_fusion.8
  291.3 1.9 collective-permute-start.10
  293.3 2.4 constant_dynamic-slice_fusion.1
  295.7 2.3 fusion.3
  298.0 1.1 convolution_add_fusion.5
  299.1 1.1 convolution_add_fusion.4
  300.1 6.3 %collective-permute-done.10 = f32[1,256,512]{2,1,0:T(8,128)} collective-permute-done((f32[1,256,512]{2,1,0:T(8,128)}, f32[1,256,512]{2,1,0:T(8,128)}, u32[]{:S(2)}, u32[]{:S(2)}) %collective-permute-start.10) | collective-permute-done | bytes 524320 | tf_op jit(solution)/shard_map/ppermute | solution.py:30
  306.5 2.3 convolution_add_fusion.3
  308.7 1.1 convolution_add_fusion.2
  309.8 1.1 convolution_add_fusion.1
  310.9 1.9 convolution_add_fusion
  (33 shorter events, 5.2 us)
Async XLA Ops:
  6.5 286.7 %all-gather.2.cloned.1.call-start = ((), (), s32[]{:S(2)}) async-start(), calls=%async_computation | async-start | bytes 8912896 | tf_op jit(solution)/shard_map/all_gather | solution.py:88
  9.4 18.8 %collective-permute-start = (f32[256,256]{1,0:T(8,128)S(1)}, f32[256,256]{1,0:T(8,128)S(1)}, u32[]{:S(2)}, u32[]{:S(2)}) collective-permute-start(f32[256,256]{1,0:T(8,128)S(1)} %get-tuple-element.31), channel_id=1, source_target_pairs={{0,0},{1,32},{2,64},{3,96},{4,128},{5,160},{6,192},{7,224},{8,256}... | collective-permute-start | bytes 786440 | tf_op jit(solution)/shard_map/ppermute | solution.py:15
  19.0 18.0 %collective-permute-start.1 = (f32[256,256]{1,0:T(8,128)S(1)}, f32[256,256]{1,0:T(8,128)S(1)}, u32[]{:S(2)}, u32[]{:S(2)}) collective-permute-start(f32[256,256]{1,0:T(8,128)S(1)} %get-tuple-element.32), channel_id=1, source_target_pairs={{0,16},{1,48},{2,80},{3,112},{4,144},{5,176},{6,208},{7,240},{8,27... | collective-permute-start | bytes 786440 | tf_op jit(solution)/shard_map/ppermute | solution.py:15
  39.0 70.1 %collective-permute-start.3 = (f32[256,512]{1,0:T(8,128)}, f32[256,512]{1,0:T(8,128)S(1)}, u32[]{:S(2)}, u32[]{:S(2)}) collective-permute-start(f32[256,512]{1,0:T(8,128)} %fusion.24), channel_id=1, source_target_pairs={{0,336},{1,305},{2,274},{3,243},{4,212},{5,181},{6,150},{7,119},{8... | collective-permute-start | bytes 1572872 | tf_op jit(solution)/shard_map/ppermute | solution.py:15
  40.9 68.2 %collective-permute-start.2 = (f32[256,512]{1,0:T(8,128)}, f32[256,512]{1,0:T(8,128)S(1)}, u32[]{:S(2)}, u32[]{:S(2)}) collective-permute-start(f32[256,512]{1,0:T(8,128)} %fusion.24), channel_id=1, source_target_pairs={{0,464},{1,433},{2,402},{3,371},{4,340},{5,309},{6,278},{7,247},{8... | collective-permute-start | bytes 1572872 | tf_op jit(solution)/shard_map/ppermute | solution.py:15
  109.1 0.8 copy-start.4
  110.0 125.1 %collective-permute-start.4 = (f32[2,256,512]{2,1,0:T(8,128)S(1)}, f32[2,256,512]{2,1,0:T(8,128)S(1)}, u32[]{:S(2)}, u32[]{:S(2)}) collective-permute-start(f32[2,256,512]{2,1,0:T(8,128)S(1)} %pad_maximum_fusion), channel_id=1, source_target_pairs={{0,16},{16,32},{32,48},{48,64},{64,80},{80,96},{96,112},{112,128},... | collective-permute-start | bytes 3145736 | tf_op jit(solution)/shard_map/ppermute | solution.py:30
  125.2 111.8 %collective-permute-start.7 = (f32[2,256,512]{2,1,0:T(8,128)S(1)}, f32[2,256,512]{2,1,0:T(8,128)S(1)}, u32[]{:S(2)}, u32[]{:S(2)}) collective-permute-start(f32[2,256,512]{2,1,0:T(8,128)S(1)} %pad_maximum_fusion), channel_id=1, source_target_pairs={{0,496},{16,0},{32,16},{48,32},{64,48},{80,64},{96,80},{112,96},{1... | collective-permute-start | bytes 3145736 | tf_op jit(solution)/shard_map/ppermute | solution.py:30
  235.1 28.0 %collective-permute-start.5 = (f32[2,256,512]{2,1,0:T(8,128)S(1)}, f32[2,256,512]{2,1,0:T(8,128)}, u32[]{:S(2)}, u32[]{:S(2)}) collective-permute-start(f32[2,256,512]{2,1,0:T(8,128)S(1)} %collective-permute-done.4), channel_id=1, source_target_pairs={{0,16},{16,32},{32,48},{48,64},{64,80},{80,96},{96,112},{112,128},... | collective-permute-start | bytes 3145736 | tf_op jit(solution)/shard_map/ppermute | solution.py:30
  237.0 30.0 %collective-permute-start.8 = (f32[2,256,512]{2,1,0:T(8,128)S(1)}, f32[2,256,512]{2,1,0:T(8,128)}, u32[]{:S(2)}, u32[]{:S(2)}) collective-permute-start(f32[2,256,512]{2,1,0:T(8,128)S(1)} %collective-permute-done.7), channel_id=1, source_target_pairs={{0,496},{16,0},{32,16},{48,32},{64,48},{80,64},{96,80},{112,96},{1... | collective-permute-start | bytes 3145736 | tf_op jit(solution)/shard_map/ppermute | solution.py:30
  263.1 27.2 %collective-permute-start.6 = (f32[2,256,512]{2,1,0:T(8,128)}, f32[2,256,512]{2,1,0:T(8,128)S(1)}, u32[]{:S(2)}, u32[]{:S(2)}) collective-permute-start(f32[2,256,512]{2,1,0:T(8,128)} %collective-permute-done.5), channel_id=1, source_target_pairs={{0,16},{16,32},{32,48},{48,64},{64,80},{80,96},{96,112},{112,128},... | collective-permute-start | bytes 3145736 | tf_op jit(solution)/shard_map/ppermute | solution.py:30
  269.2 30.9 %collective-permute-start.9 = (f32[1,256,512]{2,1,0:T(8,128)}, f32[1,256,512]{2,1,0:T(8,128)}, u32[]{:S(2)}, u32[]{:S(2)}) collective-permute-start(f32[1,256,512]{2,1,0:T(8,128)} %get-tuple-element.23), channel_id=1, source_target_pairs={{0,496},{16,0},{32,16},{48,32},{64,48},{80,64},{96,80},{112,96},{1... | collective-permute-start | bytes 1572872 | tf_op jit(solution)/shard_map/ppermute | solution.py:30
  291.3 15.2 %collective-permute-start.10 = (f32[1,256,512]{2,1,0:T(8,128)}, f32[1,256,512]{2,1,0:T(8,128)}, u32[]{:S(2)}, u32[]{:S(2)}) collective-permute-start(f32[1,256,512]{2,1,0:T(8,128)} %get-tuple-element.27), channel_id=1, source_target_pairs={{0,16},{16,32},{32,48},{48,64},{64,80},{80,96},{96,112},{112,128},... | collective-permute-start | bytes 1572872 | tf_op jit(solution)/shard_map/ppermute | solution.py:30
  293.3 4.7 %copy-start.3 = (f32[256,512]{1,0:T(8,128)S(1)}, f32[256,512]{1,0:T(8,128)}, u32[]{:S(2)}) copy-start(f32[256,512]{1,0:T(8,128)} %get-tuple-element.30) | copy-start | bytes 1572868
  293.3 5.8 %copy-start.1 = (f32[256,512]{1,0:T(8,128)S(1)}, f32[256,512]{1,0:T(8,128)}, u32[]{:S(2)}) copy-start(f32[256,512]{1,0:T(8,128)} %get-tuple-element.20) | copy-start | bytes 1572868
  293.3 15.5 %copy-start.2 = (f32[256,512]{1,0:T(8,128)S(1)}, f32[256,512]{1,0:T(8,128)}, u32[]{:S(2)}) copy-start(f32[256,512]{1,0:T(8,128)} %get-tuple-element.29) | copy-start | bytes 1572868
  293.3 16.5 %copy-start = (f32[256,512]{1,0:T(8,128)S(1)}, f32[256,512]{1,0:T(8,128)}, u32[]{:S(2)}) copy-start(f32[256,512]{1,0:T(8,128)} %get-tuple-element.24) | copy-start | bytes 1572868
Sparse Core Ops, SparseCore 0:
  39.1 185.1 all-gather.1

commit v15 on v13

--- a/solution.py
+++ b/solution.py
@@ -88,16 +88,19 @@
     row_panel = lax.all_gather(density, "col", axis=1, tiled=True)
     middle = STEPS // 2
     centre = send(density, right_pairs(row_count, col_count, middle))
-    ahead = centre
-    behind = centre
-    after = []
-    before = []
-    for _ in range(STEPS - 1 - middle):
-        ahead = shift(ahead, "row", 1)
-        after.append(ahead)
-    for _ in range(middle):
-        behind = shift(behind, "row", -1)
-        before.insert(0, behind)
+    first_ahead = shift(centre, "row", 1)
+    first_behind = shift(centre, "row", -1)
+    ahead = jnp.stack([centre, first_ahead])
+    behind = jnp.stack([first_behind, centre])
+    after = [first_ahead]
+    before = [first_behind]
+    for _ in range(2):
+        ahead = shift(ahead, "row", 2)
+        after += [ahead[0], ahead[1]]
+    for _ in range(3):
+        behind = shift(behind, "row", -2)
+        before = [behind[0], behind[1]] + before
+    after.append(shift(ahead[0], "row", 2))
     pieces = before + [centre] + after
     total = None
     for step in range(0, STEPS, 2):

time: 282 us -> 327 us (1.16)
  the two profiles are of different devices: /device:TPU:38 before, /device:TPU:68 now
where the time goes in v15:
time: 327 us; the launch traced here: 326 us
  waiting for transfers between devices  158 us (48%)
  starting transfers between devices  126 us (39%)
  between operations  13.9 us (4%)
  local copies, waits for them, and re-layouts  13.6 us (4%)
  matrix products  10.5 us (3%)
  other arithmetic  4.66 us (1%)
    ppermute x8, waiting for transfers between devices, shift(): lax.ppermute(value, axis, [(i, (i - by) % length) for i in range(length)])  133 us
    ppermute x8, starting transfers between devices, shift(): lax.ppermute(value, axis, [(i, (i - by) % length) for i in range(length)])  111 us
    ppermute x3, waiting for transfers between devices, send(): return lax.ppermute(value, AXES, pairs)  24.9 us
    ppermute x3, starting transfers between devices, send(): return lax.ppermute(value, AXES, pairs)  15.3 us
    dot_general x7, matrix products, body(): jnp.dot(left, right, precision=lax.Precision.HIGHEST, preferred_element_t...  10.5 us
  transfers between devices with their start and end apart: 12, of which 8 were waited for; matrix products, arithmetic and copies ran while one was open for 6% of the time, Pallas kernels for 0%

profile of v15, /device:TPU:68, one launch (start us, length us, event | category | flops | bytes accessed | tf_op | source)
XLA Modules:
  0.0 326.1 jit_solution(1809091438102820003)
XLA Ops:
  8.0 1.2 copy.8
  9.4 3.4 %collective-permute-start = (f32[256,256]{1,0:T(8,128)S(1)}, f32[256,256]{1,0:T(8,128)S(1)}, u32[]{:S(2)}, u32[]{:S(2)}) collective-permute-start(f32[256,256]{1,0:T(8,128)S(1)} %get-tuple-element.31), channel_id=1, source_target_pairs={{0,0},{1,32},{2,64},{3,96},{4,128},{5,160},{6,192},{7,224},{8,256}... | collective-permute-start | bytes 786440 | tf_op jit(solution)/shard_map/ppermute | solution.py:15
  12.8 3.9 %collective-permute-start.1 = (f32[256,256]{1,0:T(8,128)S(1)}, f32[256,256]{1,0:T(8,128)S(1)}, u32[]{:S(2)}, u32[]{:S(2)}) collective-permute-start(f32[256,256]{1,0:T(8,128)S(1)} %get-tuple-element.32), channel_id=1, source_target_pairs={{0,16},{1,48},{2,80},{3,112},{4,144},{5,176},{6,208},{7,240},{8,27... | collective-permute-start | bytes 786440 | tf_op jit(solution)/shard_map/ppermute | solution.py:15
  18.6 2.4 collective-permute-done
  21.0 14.2 %collective-permute-done.1 = f32[256,256]{1,0:T(8,128)S(1)} collective-permute-done((f32[256,256]{1,0:T(8,128)S(1)}, f32[256,256]{1,0:T(8,128)S(1)}, u32[]{:S(2)}, u32[]{:S(2)}) %collective-permute-start.1) | collective-permute-done | bytes 262176 | tf_op jit(solution)/shard_map/ppermute | solution.py:15
  35.2 2.0 fusion.28
  37.2 8.0 %collective-permute-start.2 = (f32[256,512]{1,0:T(8,128)}, f32[256,512]{1,0:T(8,128)S(1)}, u32[]{:S(2)}, u32[]{:S(2)}) collective-permute-start(f32[256,512]{1,0:T(8,128)} %fusion.28), channel_id=1, source_target_pairs={{0,400},{1,369},{2,338},{3,307},{4,276},{5,245},{6,214},{7,183},{8... | collective-permute-start | bytes 1572872 | tf_op jit(solution)/shard_map/ppermute | solution.py:15
  45.2 8.2 %collective-permute-done.2 = f32[256,512]{1,0:T(8,128)S(1)} collective-permute-done((f32[256,512]{1,0:T(8,128)}, f32[256,512]{1,0:T(8,128)S(1)}, u32[]{:S(2)}, u32[]{:S(2)}) %collective-permute-start.2) | collective-permute-done | bytes 524320 | tf_op jit(solution)/shard_map/ppermute | solution.py:15
  53.4 48.0 %collective-permute-start.7 = (f32[256,512]{1,0:T(8,128)S(1)}, f32[256,512]{1,0:T(8,128)S(1)}, u32[]{:S(2)}, u32[]{:S(2)}) collective-permute-start(f32[256,512]{1,0:T(8,128)S(1)} %collective-permute-done.2), channel_id=1, source_target_pairs={{0,496},{16,0},{32,16},{48,32},{64,48},{80,64},{96,80},{112,96},{1... | collective-permute-start | bytes 1572872 | tf_op jit(solution)/shard_map/ppermute | solution.py:30
  101.5 1.9 collective-permute-start.3
  103.4 4.7 %collective-permute-done.7 = f32[256,512]{1,0:T(8,128)S(1)} collective-permute-done((f32[256,512]{1,0:T(8,128)S(1)}, f32[256,512]{1,0:T(8,128)S(1)}, u32[]{:S(2)}, u32[]{:S(2)}) %collective-permute-start.7) | collective-permute-done | bytes 524320 | tf_op jit(solution)/shard_map/ppermute | solution.py:30
  108.1 7.6 %collective-permute-done.3 = f32[256,512]{1,0:T(8,128)S(1)} collective-permute-done((f32[256,512]{1,0:T(8,128)S(1)}, f32[256,512]{1,0:T(8,128)S(1)}, u32[]{:S(2)}, u32[]{:S(2)}) %collective-permute-start.3) | collective-permute-done | bytes 524320 | tf_op jit(solution)/shard_map/ppermute | solution.py:30
  116.0 1.9 collective-permute-start.4
  117.9 22.5 %collective-permute-start.8 = (f32[2,256,512]{2,1,0:T(8,128)S(1)}, f32[2,256,512]{2,1,0:T(8,128)}, u32[]{:S(2)}, u32[]{:S(2)}) collective-permute-start(f32[2,256,512]{2,1,0:T(8,128)S(1)} %get-tuple-element.30), channel_id=1, source_target_pairs={{0,480},{16,496},{32,0},{48,16},{64,32},{80,48},{96,64},{112,80},{... | collective-permute-start | bytes 3145736 | tf_op jit(solution)/shard_map/ppermute | solution.py:30
  140.5 64.8 %collective-permute-done.4 = f32[2,256,512]{2,1,0:T(8,128)S(1)} collective-permute-done((f32[2,256,512]{2,1,0:T(8,128)S(1)}, f32[2,256,512]{2,1,0:T(8,128)S(1)}, u32[]{:S(2)}, u32[]{:S(2)}) %collective-permute-start.4) | collective-permute-done | bytes 1048608 | tf_op jit(solution)/shard_map/ppermute | solution.py:30
  205.2 1.9 collective-permute-start.5
  207.2 14.0 %collective-permute-start.9 = (f32[2,256,512]{2,1,0:T(8,128)}, f32[2,256,512]{2,1,0:T(8,128)}, u32[]{:S(2)}, u32[]{:S(2)}) collective-permute-start(f32[2,256,512]{2,1,0:T(8,128)} %collective-permute-done.8), channel_id=1, source_target_pairs={{0,480},{16,496},{32,0},{48,16},{64,32},{80,48},{96,64},{112,80},{... | collective-permute-start | bytes 3145736 | tf_op jit(solution)/shard_map/ppermute | solution.py:30
  221.3 35.3 %collective-permute-done.5 = f32[2,256,512]{2,1,0:T(8,128)} collective-permute-done((f32[2,256,512]{2,1,0:T(8,128)S(1)}, f32[2,256,512]{2,1,0:T(8,128)}, u32[]{:S(2)}, u32[]{:S(2)}) %collective-permute-start.5) | collective-permute-done | bytes 1048608 | tf_op jit(solution)/shard_map/ppermute | solution.py:30
  256.7 1.9 collective-permute-start.6
  258.6 1.3 slice_bitcast_fusion.5
  259.8 2.3 slice_bitcast_fusion.3
  262.1 2.1 slice_bitcast_fusion
  264.2 18.4 %collective-permute-start.10 = (f32[256,512]{1,0:T(8,128)}, f32[256,512]{1,0:T(8,128)}, u32[]{:S(2)}, u32[]{:S(2)}) collective-permute-start(f32[256,512]{1,0:T(8,128)} %get-tuple-element.20), channel_id=1, source_target_pairs={{0,480},{16,496},{32,0},{48,16},{64,32},{80,48},{96,64},{112,80},{... | collective-permute-start | bytes 1572872 | tf_op jit(solution)/shard_map/ppermute | solution.py:30
  282.6 2.2 slice_bitcast_fusion.7
  284.9 20.2 %collective-permute-done.6 = f32[2,256,512]{2,1,0:T(8,128)S(1)} collective-permute-done((f32[2,256,512]{2,1,0:T(8,128)}, f32[2,256,512]{2,1,0:T(8,128)S(1)}, u32[]{:S(2)}, u32[]{:S(2)}) %collective-permute-start.6) | collective-permute-done | bytes 1048608 | tf_op jit(solution)/shard_map/ppermute | solution.py:30
  305.1 1.1 slice_bitcast_fusion.9
  306.3 2.4 constant_dynamic-slice_fusion.1
  308.7 2.3 fusion.19
  311.0 1.1 fusion.5
  312.1 1.1 convolution_add_fusion.3
  315.3 1.1 fusion.1
  316.4 2.9 convolution_add_fusion
  (35 shorter events, 5.8 us)
Async XLA Ops:
  6.5 299.7 %all-gather.2.cloned.1.call-start = ((), (), s32[]{:S(2)}) async-start(), calls=%async_computation | async-start | bytes 8912896 | tf_op jit(solution)/shard_map/all_gather | solution.py:88
  9.4 11.6 %collective-permute-start = (f32[256,256]{1,0:T(8,128)S(1)}, f32[256,256]{1,0:T(8,128)S(1)}, u32[]{:S(2)}, u32[]{:S(2)}) collective-permute-start(f32[256,256]{1,0:T(8,128)S(1)} %get-tuple-element.31), channel_id=1, source_target_pairs={{0,0},{1,32},{2,64},{3,96},{4,128},{5,160},{6,192},{7,224},{8,256}... | collective-permute-start | bytes 786440 | tf_op jit(solution)/shard_map/ppermute | solution.py:15
  12.8 22.4 %collective-permute-start.1 = (f32[256,256]{1,0:T(8,128)S(1)}, f32[256,256]{1,0:T(8,128)S(1)}, u32[]{:S(2)}, u32[]{:S(2)}) collective-permute-start(f32[256,256]{1,0:T(8,128)S(1)} %get-tuple-element.32), channel_id=1, source_target_pairs={{0,16},{1,48},{2,80},{3,112},{4,144},{5,176},{6,208},{7,240},{8,27... | collective-permute-start | bytes 786440 | tf_op jit(solution)/shard_map/ppermute | solution.py:15
  37.2 16.2 %collective-permute-start.2 = (f32[256,512]{1,0:T(8,128)}, f32[256,512]{1,0:T(8,128)S(1)}, u32[]{:S(2)}, u32[]{:S(2)}) collective-permute-start(f32[256,512]{1,0:T(8,128)} %fusion.28), channel_id=1, source_target_pairs={{0,400},{1,369},{2,338},{3,307},{4,276},{5,245},{6,214},{7,183},{8... | collective-permute-start | bytes 1572872 | tf_op jit(solution)/shard_map/ppermute | solution.py:15
  53.4 54.7 %collective-permute-start.7 = (f32[256,512]{1,0:T(8,128)S(1)}, f32[256,512]{1,0:T(8,128)S(1)}, u32[]{:S(2)}, u32[]{:S(2)}) collective-permute-start(f32[256,512]{1,0:T(8,128)S(1)} %collective-permute-done.2), channel_id=1, source_target_pairs={{0,496},{16,0},{32,16},{48,32},{64,48},{80,64},{96,80},{112,96},{1... | collective-permute-start | bytes 1572872 | tf_op jit(solution)/shard_map/ppermute | solution.py:30
  101.5 14.3 %collective-permute-start.3 = (f32[256,512]{1,0:T(8,128)S(1)}, f32[256,512]{1,0:T(8,128)S(1)}, u32[]{:S(2)}, u32[]{:S(2)}) collective-permute-start(f32[256,512]{1,0:T(8,128)S(1)} %collective-permute-done.2), channel_id=1, source_target_pairs={{0,16},{16,32},{32,48},{48,64},{64,80},{80,96},{96,112},{112,128},... | collective-permute-start | bytes 1572872 | tf_op jit(solution)/shard_map/ppermute | solution.py:30
  116.0 89.2 %collective-permute-start.4 = (f32[2,256,512]{2,1,0:T(8,128)S(1)}, f32[2,256,512]{2,1,0:T(8,128)S(1)}, u32[]{:S(2)}, u32[]{:S(2)}) collective-permute-start(f32[2,256,512]{2,1,0:T(8,128)S(1)} %get-tuple-element.29), channel_id=1, source_target_pairs={{0,32},{16,48},{32,64},{48,80},{64,96},{80,112},{96,128},{112,144}... | collective-permute-start | bytes 3145736 | tf_op jit(solution)/shard_map/ppermute | solution.py:30
  117.9 89.2 %collective-permute-start.8 = (f32[2,256,512]{2,1,0:T(8,128)S(1)}, f32[2,256,512]{2,1,0:T(8,128)}, u32[]{:S(2)}, u32[]{:S(2)}) collective-permute-start(f32[2,256,512]{2,1,0:T(8,128)S(1)} %get-tuple-element.30), channel_id=1, source_target_pairs={{0,480},{16,496},{32,0},{48,16},{64,32},{80,48},{96,64},{112,80},{... | collective-permute-start | bytes 3145736 | tf_op jit(solution)/shard_map/ppermute | solution.py:30
  205.2 51.4 %copy-start.5 = (f32[2,256,512]{2,1,0:T(8,128)}, f32[2,256,512]{2,1,0:T(8,128)S(1)}, u32[]{:S(2)}) copy-start(f32[2,256,512]{2,1,0:T(8,128)S(1)} %collective-permute-done.4) | copy-start | bytes 3145732
  205.2 51.4 %collective-permute-start.5 = (f32[2,256,512]{2,1,0:T(8,128)S(1)}, f32[2,256,512]{2,1,0:T(8,128)}, u32[]{:S(2)}, u32[]{:S(2)}) collective-permute-start(f32[2,256,512]{2,1,0:T(8,128)S(1)} %collective-permute-done.4), channel_id=1, source_target_pairs={{0,32},{16,48},{32,64},{48,80},{64,96},{80,112},{96,128},{112,144}... | collective-permute-start | bytes 3145736 | tf_op jit(solution)/shard_map/ppermute | solution.py:30
  207.2 55.0 %collective-permute-start.9 = (f32[2,256,512]{2,1,0:T(8,128)}, f32[2,256,512]{2,1,0:T(8,128)}, u32[]{:S(2)}, u32[]{:S(2)}) collective-permute-start(f32[2,256,512]{2,1,0:T(8,128)} %collective-permute-done.8), channel_id=1, source_target_pairs={{0,480},{16,496},{32,0},{48,16},{64,32},{80,48},{96,64},{112,80},{... | collective-permute-start | bytes 3145736 | tf_op jit(solution)/shard_map/ppermute | solution.py:30
  256.7 48.4 %collective-permute-start.6 = (f32[2,256,512]{2,1,0:T(8,128)}, f32[2,256,512]{2,1,0:T(8,128)S(1)}, u32[]{:S(2)}, u32[]{:S(2)}) collective-permute-start(f32[2,256,512]{2,1,0:T(8,128)} %collective-permute-done.5), channel_id=1, source_target_pairs={{0,32},{16,48},{32,64},{48,80},{64,96},{80,112},{96,128},{112,144}... | collective-permute-start | bytes 3145736 | tf_op jit(solution)/shard_map/ppermute | solution.py:30
  264.2 52.2 %collective-permute-start.10 = (f32[256,512]{1,0:T(8,128)}, f32[256,512]{1,0:T(8,128)}, u32[]{:S(2)}, u32[]{:S(2)}) collective-permute-start(f32[256,512]{1,0:T(8,128)} %get-tuple-element.20), channel_id=1, source_target_pairs={{0,480},{16,496},{32,0},{48,16},{64,32},{80,48},{96,64},{112,80},{... | collective-permute-start | bytes 1572872 | tf_op jit(solution)/shard_map/ppermute | solution.py:30
  306.2 4.7 %copy-start.3 = (f32[256,512]{1,0:T(8,128)S(1)}, f32[256,512]{1,0:T(8,128)}, u32[]{:S(2)}) copy-start(f32[256,512]{1,0:T(8,128)} %get-tuple-element.25) | copy-start | bytes 1572868
  306.2 4.7 %copy-start.4 = (f32[256,512]{1,0:T(8,128)S(1)}, f32[256,512]{1,0:T(8,128)}, u32[]{:S(2)}) copy-start(f32[256,512]{1,0:T(8,128)} %get-tuple-element.26) | copy-start | bytes 1572868
  306.2 5.8 %copy-start = (f32[256,512]{1,0:T(8,128)S(1)}, f32[256,512]{1,0:T(8,128)}, u32[]{:S(2)}) copy-start(f32[256,512]{1,0:T(8,128)} %get-tuple-element.23) | copy-start | bytes 1572868
  306.2 5.8 %copy-start.1 = (f32[256,512]{1,0:T(8,128)S(1)}, f32[256,512]{1,0:T(8,128)}, u32[]{:S(2)}) copy-start(f32[256,512]{1,0:T(8,128)} %get-tuple-element.24) | copy-start | bytes 1572868
  306.3 6.9 %copy-start.2 = (f32[256,512]{1,0:T(8,128)S(1)}, f32[256,512]{1,0:T(8,128)}, u32[]{:S(2)}) copy-start(f32[256,512]{1,0:T(8,128)} %get-tuple-element.27) | copy-start | bytes 1572868
Sparse Core Ops, SparseCore 0:
  37.3 176.7 all-gather.1

commit v16 on v13

--- a/solution.py
+++ b/solution.py
@@ -99,13 +99,11 @@
         behind = shift(behind, "row", -1)
         before.insert(0, behind)
     pieces = before + [centre] + after
+    wrapped = jnp.concatenate([row_panel, row_panel[:, :group]], axis=1)
     total = None
     for step in range(0, STEPS, 2):
-        lefts = []
-        for offset in range(2):
-            start = (row_id + 2 * col_id + step + offset) % row_count
-            lefts.append(lax.dynamic_slice_in_dim(row_panel, start * group, group, axis=1))
-        left = jnp.concatenate(lefts, axis=1)
+        start = (row_id + 2 * col_id + step) % row_count
+        left = lax.dynamic_slice_in_dim(wrapped, start * group, 2 * group, axis=1)
         right = jnp.concatenate(pieces[step : step + 2], axis=0)
         term = jnp.dot(left, right, precision=lax.Precision.HIGHEST, preferred_element_type=jnp.float32)
         total = term if total is None else total + term

time: 282 us -> 287 us (1.018)
  the two profiles are of different devices: /device:TPU:38 before, /device:TPU:4 now
where the time goes in v16:
time: 287 us; the launch traced here: 286 us
  waiting for transfers between devices  163 us (57%)
  starting transfers between devices  87.6 us (31%)
  between operations  13.9 us (5%)
  matrix products  13.3 us (5%)
  other arithmetic  4.43 us (2%)
  local copies, waits for them, and re-layouts  3.45 us (1%)
    ppermute x13, waiting for transfers between devices, shift(): lax.ppermute(value, axis, [(i, (i - by) % length) for i in range(length)])  100 us
    ppermute x13, starting transfers between devices, shift(): lax.ppermute(value, axis, [(i, (i - by) % length) for i in range(length)])  67.2 us
    ppermute x3, waiting for transfers between devices, send(): return lax.ppermute(value, AXES, pairs)  62.8 us
    ppermute x3, starting transfers between devices, send(): return lax.ppermute(value, AXES, pairs)  20.4 us
    dot_general x7, matrix products, body(): jnp.dot(left, right, precision=lax.Precision.HIGHEST, preferred_element_t...  13.3 us
  transfers between devices with their start and end apart: 17, of which 11 were waited for; matrix products, arithmetic and copies ran while one was open for 5% of the time, Pallas kernels for 0%

profile of v16, /device:TPU:4, one launch (start us, length us, event | category | flops | bytes accessed | tf_op | source)
XLA Modules:
  0.0 286.0 jit_solution(7141641494994585049)
XLA Ops:
  9.4 5.2 %collective-permute-start.1 = (f32[256,256]{1,0:T(8,128)S(1)}, f32[256,256]{1,0:T(8,128)S(1)}, u32[]{:S(2)}, u32[]{:S(2)}) collective-permute-start(f32[256,256]{1,0:T(8,128)S(1)} %get-tuple-element.6), channel_id=1, source_target_pairs={{0,16},{1,48},{2,80},{3,112},{4,144},{5,176},{6,208},{7,240},{8,27... | collective-permute-start | bytes 786440 | tf_op jit(solution)/shard_map/ppermute | solution.py:15
  14.7 4.8 %collective-permute-start = (f32[256,256]{1,0:T(8,128)S(1)}, f32[256,256]{1,0:T(8,128)S(1)}, u32[]{:S(2)}, u32[]{:S(2)}) collective-permute-start(f32[256,256]{1,0:T(8,128)S(1)} %get-tuple-element.5), channel_id=1, source_target_pairs={{0,0},{1,32},{2,64},{3,96},{4,128},{5,160},{6,192},{7,224},{8,256}... | collective-permute-start | bytes 786440 | tf_op jit(solution)/shard_map/ppermute | solution.py:15
  21.4 1.9 collective-permute-done.1
  23.3 6.6 %collective-permute-done = f32[256,256]{1,0:T(8,128)S(1)} collective-permute-done((f32[256,256]{1,0:T(8,128)S(1)}, f32[256,256]{1,0:T(8,128)S(1)}, u32[]{:S(2)}, u32[]{:S(2)}) %collective-permute-start) | collective-permute-done | bytes 262176 | tf_op jit(solution)/shard_map/ppermute | solution.py:15
  29.9 2.0 fusion.42
  31.8 10.3 %collective-permute-start.2 = (f32[256,512]{1,0:T(8,128)}, f32[256,512]{1,0:T(8,128)S(1)}, u32[]{:S(2)}, u32[]{:S(2)}) collective-permute-start(f32[256,512]{1,0:T(8,128)} %fusion.42), channel_id=1, source_target_pairs={{0,400},{1,369},{2,338},{3,307},{4,276},{5,245},{6,214},{7,183},{8... | collective-permute-start | bytes 1572872 | tf_op jit(solution)/shard_map/ppermute | solution.py:15
  42.2 54.3 %collective-permute-done.2 = f32[256,512]{1,0:T(8,128)S(1)} collective-permute-done((f32[256,512]{1,0:T(8,128)}, f32[256,512]{1,0:T(8,128)S(1)}, u32[]{:S(2)}, u32[]{:S(2)}) %collective-permute-start.2) | collective-permute-done | bytes 524320 | tf_op jit(solution)/shard_map/ppermute | solution.py:15
  96.5 1.9 collective-permute-start.3
  98.4 20.0 %collective-permute-done.3 = f32[256,512]{1,0:T(8,128)S(1)} collective-permute-done((f32[256,512]{1,0:T(8,128)S(1)}, f32[256,512]{1,0:T(8,128)S(1)}, u32[]{:S(2)}, u32[]{:S(2)}) %collective-permute-start.3) | collective-permute-done | bytes 524320 | tf_op jit(solution)/shard_map/ppermute | solution.py:30
  118.5 1.9 collective-permute-start.4
  120.4 13.5 %collective-permute-start.10 = (f32[256,512]{1,0:T(8,128)S(1)}, f32[256,512]{1,0:T(8,128)S(1)}, u32[]{:S(2)}, u32[]{:S(2)}) collective-permute-start(f32[256,512]{1,0:T(8,128)S(1)} %collective-permute-done.2), channel_id=1, source_target_pairs={{0,496},{16,0},{32,16},{48,32},{64,48},{80,64},{96,80},{112,96},{1... | collective-permute-start | bytes 1572872 | tf_op jit(solution)/shard_map/ppermute | solution.py:30
  133.8 9.8 %collective-permute-done.4 = f32[256,512]{1,0:T(8,128)S(1)} collective-permute-done((f32[256,512]{1,0:T(8,128)S(1)}, f32[256,512]{1,0:T(8,128)S(1)}, u32[]{:S(2)}, u32[]{:S(2)}) %collective-permute-start.4) | collective-permute-done | bytes 524320 | tf_op jit(solution)/shard_map/ppermute | solution.py:30
  143.7 1.9 collective-permute-start.5
  145.6 4.4 %collective-permute-done.10 = f32[256,512]{1,0:T(8,128)S(1)} collective-permute-done((f32[256,512]{1,0:T(8,128)S(1)}, f32[256,512]{1,0:T(8,128)S(1)}, u32[]{:S(2)}, u32[]{:S(2)}) %collective-permute-start.10) | collective-permute-done | bytes 524320 | tf_op jit(solution)/shard_map/ppermute | solution.py:30
  150.0 8.4 %collective-permute-start.11 = (f32[256,512]{1,0:T(8,128)S(1)}, f32[256,512]{1,0:T(8,128)S(1)}, u32[]{:S(2)}, u32[]{:S(2)}) collective-permute-start(f32[256,512]{1,0:T(8,128)S(1)} %collective-permute-done.10), channel_id=1, source_target_pairs={{0,496},{16,0},{32,16},{48,32},{64,48},{80,64},{96,80},{112,96},{1... | collective-permute-start | bytes 1572872 | tf_op jit(solution)/shard_map/ppermute | solution.py:30
  158.4 33.6 %collective-permute-done.5 = f32[256,512]{1,0:T(8,128)S(1)} collective-permute-done((f32[256,512]{1,0:T(8,128)S(1)}, f32[256,512]{1,0:T(8,128)S(1)}, u32[]{:S(2)}, u32[]{:S(2)}) %collective-permute-start.5) | collective-permute-done | bytes 524320 | tf_op jit(solution)/shard_map/ppermute | solution.py:30
  192.0 1.9 collective-permute-start.6
  193.9 2.4 collective-permute-done.11
  196.3 8.4 %collective-permute-start.12 = (f32[256,512]{1,0:T(8,128)S(1)}, f32[256,512]{1,0:T(8,128)S(1)}, u32[]{:S(2)}, u32[]{:S(2)}) collective-permute-start(f32[256,512]{1,0:T(8,128)S(1)} %collective-permute-done.11), channel_id=1, source_target_pairs={{0,496},{16,0},{32,16},{48,32},{64,48},{80,64},{96,80},{112,96},{1... | collective-permute-start | bytes 1572872 | tf_op jit(solution)/shard_map/ppermute | solution.py:30
  204.7 12.9 %collective-permute-done.6 = f32[256,512]{1,0:T(8,128)S(1)} collective-permute-done((f32[256,512]{1,0:T(8,128)S(1)}, f32[256,512]{1,0:T(8,128)S(1)}, u32[]{:S(2)}, u32[]{:S(2)}) %collective-permute-start.6) | collective-permute-done | bytes 524320 | tf_op jit(solution)/shard_map/ppermute | solution.py:30
  217.6 1.9 collective-permute-start.7
  219.5 7.8 %collective-permute-start.13 = (f32[256,512]{1,0:T(8,128)S(1)}, f32[256,512]{1,0:T(8,128)}, u32[]{:S(2)}, u32[]{:S(2)}) collective-permute-start(f32[256,512]{1,0:T(8,128)S(1)} %collective-permute-done.12), channel_id=1, source_target_pairs={{0,496},{16,0},{32,16},{48,32},{64,48},{80,64},{96,80},{112,96},{1... | collective-permute-start | bytes 1572872 | tf_op jit(solution)/shard_map/ppermute | solution.py:30
  227.4 9.0 %collective-permute-done.7 = f32[256,512]{1,0:T(8,128)S(1)} collective-permute-done((f32[256,512]{1,0:T(8,128)S(1)}, f32[256,512]{1,0:T(8,128)S(1)}, u32[]{:S(2)}, u32[]{:S(2)}) %collective-permute-start.7) | collective-permute-done | bytes 524320 | tf_op jit(solution)/shard_map/ppermute | solution.py:30
  236.4 1.9 collective-permute-start.8
  238.3 7.9 %collective-permute-start.14 = (f32[256,512]{1,0:T(8,128)}, f32[256,512]{1,0:T(8,128)}, u32[]{:S(2)}, u32[]{:S(2)}) collective-permute-start(f32[256,512]{1,0:T(8,128)} %collective-permute-done.13), channel_id=1, source_target_pairs={{0,496},{16,0},{32,16},{48,32},{64,48},{80,64},{96,80},{112,96},{1... | collective-permute-start | bytes 1572872 | tf_op jit(solution)/shard_map/ppermute | solution.py:30
  246.2 8.4 %collective-permute-done.8 = f32[256,512]{1,0:T(8,128)} collective-permute-done((f32[256,512]{1,0:T(8,128)S(1)}, f32[256,512]{1,0:T(8,128)}, u32[]{:S(2)}, u32[]{:S(2)}) %collective-permute-start.8) | collective-permute-done | bytes 524320 | tf_op jit(solution)/shard_map/ppermute | solution.py:30
  254.5 1.9 collective-permute-start.9
  256.6 7.8 %collective-permute-start.15 = (f32[256,512]{1,0:T(8,128)}, f32[256,512]{1,0:T(8,128)}, u32[]{:S(2)}, u32[]{:S(2)}) collective-permute-start(f32[256,512]{1,0:T(8,128)} %collective-permute-done.14), channel_id=1, source_target_pairs={{0,496},{16,0},{32,16},{48,32},{64,48},{80,64},{96,80},{112,96},{1... | collective-permute-start | bytes 1572872 | tf_op jit(solution)/shard_map/ppermute | solution.py:30
  265.6 2.4 fusion.13
  270.3 2.4 fusion.1
  273.9 2.1 convolution_add_fusion.1
  276.0 3.1 %convolution_add_fusion = f32[256,512]{1,0:T(8,128)} fusion(f32[256,512]{1,0:T(8,128)S(1)} %convolution_add_fusion.1, f32[256,512]{1,0:T(8,128)} %collective-permute-done.15, f32[256,512]{1,0:T(8,128)} %collective-permute-done.14, s32[]{:T(128)S(6)} %select_n.121, f32[256,8192]{1,0:T(8,128)S(1)} %copy-done, f32[256,256]{1,0:T(8,128)S(1)} %slice.16), kind=kOutput, calls=%fused_computation.14 | convolution fusion | flops 805830656 | bytes 10747908 | tf_op jit(solution)/shard_map/dot_general | solution.py:108
  (41 shorter events, 9.3 us)
Async XLA Ops:
  6.5 257.9 %all-gather.2.cloned.1.call-start = ((), (), s32[]{:S(2)}) async-start(), calls=%async_computation | async-start | bytes 8912896 | tf_op jit(solution)/shard_map/all_gather | solution.py:88
  9.4 13.9 %collective-permute-start.1 = (f32[256,256]{1,0:T(8,128)S(1)}, f32[256,256]{1,0:T(8,128)S(1)}, u32[]{:S(2)}, u32[]{:S(2)}) collective-permute-start(f32[256,256]{1,0:T(8,128)S(1)} %get-tuple-element.6), channel_id=1, source_target_pairs={{0,16},{1,48},{2,80},{3,112},{4,144},{5,176},{6,208},{7,240},{8,27... | collective-permute-start | bytes 786440 | tf_op jit(solution)/shard_map/ppermute | solution.py:15
  14.7 15.2 %collective-permute-start = (f32[256,256]{1,0:T(8,128)S(1)}, f32[256,256]{1,0:T(8,128)S(1)}, u32[]{:S(2)}, u32[]{:S(2)}) collective-permute-start(f32[256,256]{1,0:T(8,128)S(1)} %get-tuple-element.5), channel_id=1, source_target_pairs={{0,0},{1,32},{2,64},{3,96},{4,128},{5,160},{6,192},{7,224},{8,256}... | collective-permute-start | bytes 786440 | tf_op jit(solution)/shard_map/ppermute | solution.py:15
  31.8 64.7 %collective-permute-start.2 = (f32[256,512]{1,0:T(8,128)}, f32[256,512]{1,0:T(8,128)S(1)}, u32[]{:S(2)}, u32[]{:S(2)}) collective-permute-start(f32[256,512]{1,0:T(8,128)} %fusion.42), channel_id=1, source_target_pairs={{0,400},{1,369},{2,338},{3,307},{4,276},{5,245},{6,214},{7,183},{8... | collective-permute-start | bytes 1572872 | tf_op jit(solution)/shard_map/ppermute | solution.py:15
  96.5 21.9 %collective-permute-start.3 = (f32[256,512]{1,0:T(8,128)S(1)}, f32[256,512]{1,0:T(8,128)S(1)}, u32[]{:S(2)}, u32[]{:S(2)}) collective-permute-start(f32[256,512]{1,0:T(8,128)S(1)} %collective-permute-done.2), channel_id=1, source_target_pairs={{0,16},{16,32},{32,48},{48,64},{64,80},{80,96},{96,112},{112,128},... | collective-permute-start | bytes 1572872 | tf_op jit(solution)/shard_map/ppermute | solution.py:30
  118.5 25.2 %collective-permute-start.4 = (f32[256,512]{1,0:T(8,128)S(1)}, f32[256,512]{1,0:T(8,128)S(1)}, u32[]{:S(2)}, u32[]{:S(2)}) collective-permute-start(f32[256,512]{1,0:T(8,128)S(1)} %collective-permute-done.3), channel_id=1, source_target_pairs={{0,16},{16,32},{32,48},{48,64},{64,80},{80,96},{96,112},{112,128},... | collective-permute-start | bytes 1572872 | tf_op jit(solution)/shard_map/ppermute | solution.py:30
  120.4 29.6 %collective-permute-start.10 = (f32[256,512]{1,0:T(8,128)S(1)}, f32[256,512]{1,0:T(8,128)S(1)}, u32[]{:S(2)}, u32[]{:S(2)}) collective-permute-start(f32[256,512]{1,0:T(8,128)S(1)} %collective-permute-done.2), channel_id=1, source_target_pairs={{0,496},{16,0},{32,16},{48,32},{64,48},{80,64},{96,80},{112,96},{1... | collective-permute-start | bytes 1572872 | tf_op jit(solution)/shard_map/ppermute | solution.py:30
  143.7 48.3 %collective-permute-start.5 = (f32[256,512]{1,0:T(8,128)S(1)}, f32[256,512]{1,0:T(8,128)S(1)}, u32[]{:S(2)}, u32[]{:S(2)}) collective-permute-start(f32[256,512]{1,0:T(8,128)S(1)} %collective-permute-done.4), channel_id=1, source_target_pairs={{0,16},{16,32},{32,48},{48,64},{64,80},{80,96},{96,112},{112,128},... | collective-permute-start | bytes 1572872 | tf_op jit(solution)/shard_map/ppermute | solution.py:30
  150.0 104.6 %copy-start.1 = (f32[256,512]{1,0:T(8,128)}, f32[256,512]{1,0:T(8,128)S(1)}, u32[]{:S(2)}) copy-start(f32[256,512]{1,0:T(8,128)S(1)} %collective-permute-done.10) | copy-start | bytes 1572868
  150.0 46.3 %collective-permute-start.11 = (f32[256,512]{1,0:T(8,128)S(1)}, f32[256,512]{1,0:T(8,128)S(1)}, u32[]{:S(2)}, u32[]{:S(2)}) collective-permute-start(f32[256,512]{1,0:T(8,128)S(1)} %collective-permute-done.10), channel_id=1, source_target_pairs={{0,496},{16,0},{32,16},{48,32},{64,48},{80,64},{96,80},{112,96},{1... | collective-permute-start | bytes 1572872 | tf_op jit(solution)/shard_map/ppermute | solution.py:30
  192.0 25.6 %collective-permute-start.6 = (f32[256,512]{1,0:T(8,128)S(1)}, f32[256,512]{1,0:T(8,128)S(1)}, u32[]{:S(2)}, u32[]{:S(2)}) collective-permute-start(f32[256,512]{1,0:T(8,128)S(1)} %collective-permute-done.5), channel_id=1, source_target_pairs={{0,16},{16,32},{32,48},{48,64},{64,80},{80,96},{96,112},{112,128},... | collective-permute-start | bytes 1572872 | tf_op jit(solution)/shard_map/ppermute | solution.py:30
  196.3 58.3 %copy-start.3 = (f32[256,512]{1,0:T(8,128)}, f32[256,512]{1,0:T(8,128)S(1)}, u32[]{:S(2)}) copy-start(f32[256,512]{1,0:T(8,128)S(1)} %collective-permute-done.11) | copy-start | bytes 1572868
  196.3 23.2 %collective-permute-start.12 = (f32[256,512]{1,0:T(8,128)S(1)}, f32[256,512]{1,0:T(8,128)S(1)}, u32[]{:S(2)}, u32[]{:S(2)}) collective-permute-start(f32[256,512]{1,0:T(8,128)S(1)} %collective-permute-done.11), channel_id=1, source_target_pairs={{0,496},{16,0},{32,16},{48,32},{64,48},{80,64},{96,80},{112,96},{1... | collective-permute-start | bytes 1572872 | tf_op jit(solution)/shard_map/ppermute | solution.py:30
  217.6 18.8 %collective-permute-start.7 = (f32[256,512]{1,0:T(8,128)S(1)}, f32[256,512]{1,0:T(8,128)S(1)}, u32[]{:S(2)}, u32[]{:S(2)}) collective-permute-start(f32[256,512]{1,0:T(8,128)S(1)} %collective-permute-done.6), channel_id=1, source_target_pairs={{0,16},{16,32},{32,48},{48,64},{64,80},{80,96},{96,112},{112,128},... | collective-permute-start | bytes 1572872 | tf_op jit(solution)/shard_map/ppermute | solution.py:30
  219.5 35.0 %copy-start.5 = (f32[256,512]{1,0:T(8,128)}, f32[256,512]{1,0:T(8,128)S(1)}, u32[]{:S(2)}) copy-start(f32[256,512]{1,0:T(8,128)S(1)} %collective-permute-done.12) | copy-start | bytes 1572868
  219.5 18.7 %collective-permute-start.13 = (f32[256,512]{1,0:T(8,128)S(1)}, f32[256,512]{1,0:T(8,128)}, u32[]{:S(2)}, u32[]{:S(2)}) collective-permute-start(f32[256,512]{1,0:T(8,128)S(1)} %collective-permute-done.12), channel_id=1, source_target_pairs={{0,496},{16,0},{32,16},{48,32},{64,48},{80,64},{96,80},{112,96},{1... | collective-permute-start | bytes 1572872 | tf_op jit(solution)/shard_map/ppermute | solution.py:30
  236.4 18.2 %collective-permute-start.8 = (f32[256,512]{1,0:T(8,128)S(1)}, f32[256,512]{1,0:T(8,128)}, u32[]{:S(2)}, u32[]{:S(2)}) collective-permute-start(f32[256,512]{1,0:T(8,128)S(1)} %collective-permute-done.7), channel_id=1, source_target_pairs={{0,16},{16,32},{32,48},{48,64},{64,80},{80,96},{96,112},{112,128},... | collective-permute-start | bytes 1572872 | tf_op jit(solution)/shard_map/ppermute | solution.py:30
  238.3 18.3 %collective-permute-start.14 = (f32[256,512]{1,0:T(8,128)}, f32[256,512]{1,0:T(8,128)}, u32[]{:S(2)}, u32[]{:S(2)}) collective-permute-start(f32[256,512]{1,0:T(8,128)} %collective-permute-done.13), channel_id=1, source_target_pairs={{0,496},{16,0},{32,16},{48,32},{64,48},{80,64},{96,80},{112,96},{1... | collective-permute-start | bytes 1572872 | tf_op jit(solution)/shard_map/ppermute | solution.py:30
  254.5 15.8 %collective-permute-start.9 = (f32[256,512]{1,0:T(8,128)}, f32[256,512]{1,0:T(8,128)}, u32[]{:S(2)}, u32[]{:S(2)}) collective-permute-start(f32[256,512]{1,0:T(8,128)} %collective-permute-done.8), channel_id=1, source_target_pairs={{0,16},{16,32},{32,48},{48,64},{64,80},{80,96},{96,112},{112,128},... | collective-permute-start | bytes 1572872 | tf_op jit(solution)/shard_map/ppermute | solution.py:30
  256.6 19.4 %collective-permute-start.15 = (f32[256,512]{1,0:T(8,128)}, f32[256,512]{1,0:T(8,128)}, u32[]{:S(2)}, u32[]{:S(2)}) collective-permute-start(f32[256,512]{1,0:T(8,128)} %collective-permute-done.14), channel_id=1, source_target_pairs={{0,496},{16,0},{32,16},{48,32},{64,48},{80,64},{96,80},{112,96},{1... | collective-permute-start | bytes 1572872 | tf_op jit(solution)/shard_map/ppermute | solution.py:30
  264.5 3.6 %copy-start = (f32[256,8192]{1,0:T(8,128)S(1)}, f32[256,8192]{1,0:T(8,128)}, u32[]{:S(2)}) copy-start(f32[256,8192]{1,0:T(8,128)} %all-gather.2.cloned.1.call-done) | copy-start | bytes 25165828
  270.3 2.5 copy-start.2
  270.3 2.5 copy-start.4
  270.3 3.6 %copy-start.6 = (f32[256,512]{1,0:T(8,128)S(1)}, f32[256,512]{1,0:T(8,128)}, u32[]{:S(2)}) copy-start(f32[256,512]{1,0:T(8,128)} %copy-done.5) | copy-start | bytes 1572868
Sparse Core Ops, SparseCore 0:
  32.0 187.7 all-gather.1

commit v17 on v13

--- a/solution.py
+++ b/solution.py
@@ -100,13 +100,14 @@
         before.insert(0, behind)
     pieces = before + [centre] + after
     total = None
-    for step in range(0, STEPS, 2):
+    for first in range(middle, STEPS):
+        pair = (first, STEPS - 1 - first)
         lefts = []
-        for offset in range(2):
-            start = (row_id + 2 * col_id + step + offset) % row_count
+        for step in pair:
+            start = (row_id + 2 * col_id + step) % row_count
             lefts.append(lax.dynamic_slice_in_dim(row_panel, start * group, group, axis=1))
         left = jnp.concatenate(lefts, axis=1)
-        right = jnp.concatenate(pieces[step : step + 2], axis=0)
+        right = jnp.concatenate([pieces[step] for step in pair], axis=0)
         term = jnp.dot(left, right, precision=lax.Precision.HIGHEST, preferred_element_type=jnp.float32)
         total = term if total is None else total + term
     return total

time: 282 us -> 278 us (0.986)
  waiting for transfers between devices: 168 us -> 163 us
    ppermute x13, waiting for transfers between devices: 99.3 us -> 94.7 us  [shift(): lax.ppermute(value, axis, [(i, (i - by) % length) for i in range(length)])]
where the time goes in v17:
time: 278 us; the launch traced here: 277 us
  waiting for transfers between devices  163 us (59%)
  starting transfers between devices  77.7 us (28%)
  between operations  13.9 us (5%)
  matrix products  13 us (5%)
  local copies, waits for them, and re-layouts  4.48 us (2%)
  other arithmetic  4.43 us (2%)
    ppermute x13, waiting for transfers between devices, shift(): lax.ppermute(value, axis, [(i, (i - by) % length) for i in range(length)])  94.7 us
    ppermute x3, waiting for transfers between devices, send(): return lax.ppermute(value, AXES, pairs)  68.6 us
    ppermute x13, starting transfers between devices, shift(): lax.ppermute(value, axis, [(i, (i - by) % length) for i in range(length)])  60.9 us
    ppermute x3, starting transfers between devices, send(): return lax.ppermute(value, AXES, pairs)  16.8 us
    dot_general x7, matrix products, body(): jnp.dot(left, right, precision=lax.Precision.HIGHEST, preferred_element_t...  13 us
  transfers between devices with their start and end apart: 17, of which 11 were waited for; matrix products, arithmetic and copies ran while one was open for 5% of the time, Pallas kernels for 0%

profile of v17, /device:TPU:38, one launch (start us, length us, event | category | flops | bytes accessed | tf_op | source)
XLA Modules:
  0.0 276.9 jit_solution(6291870268220341889)
XLA Ops:
  9.4 10.7 %collective-permute-start = (f32[256,256]{1,0:T(8,128)S(1)}, f32[256,256]{1,0:T(8,128)S(1)}, u32[]{:S(2)}, u32[]{:S(2)}) collective-permute-start(f32[256,256]{1,0:T(8,128)S(1)} %get-tuple-element.19), channel_id=1, source_target_pairs={{0,0},{1,32},{2,64},{3,96},{4,128},{5,160},{6,192},{7,224},{8,256}... | collective-permute-start | bytes 786440 | tf_op jit(solution)/shard_map/ppermute | solution.py:15
  20.1 4.2 %collective-permute-start.1 = (f32[256,256]{1,0:T(8,128)S(1)}, f32[256,256]{1,0:T(8,128)S(1)}, u32[]{:S(2)}, u32[]{:S(2)}) collective-permute-start(f32[256,256]{1,0:T(8,128)S(1)} %get-tuple-element.20), channel_id=1, source_target_pairs={{0,16},{1,48},{2,80},{3,112},{4,144},{5,176},{6,208},{7,240},{8,27... | collective-permute-start | bytes 786440 | tf_op jit(solution)/shard_map/ppermute | solution.py:15
  26.1 40.0 %collective-permute-done = f32[256,256]{1,0:T(8,128)S(1)} collective-permute-done((f32[256,256]{1,0:T(8,128)S(1)}, f32[256,256]{1,0:T(8,128)S(1)}, u32[]{:S(2)}, u32[]{:S(2)}) %collective-permute-start) | collective-permute-done | bytes 262176 | tf_op jit(solution)/shard_map/ppermute | solution.py:15
  66.1 9.4 %collective-permute-done.1 = f32[256,256]{1,0:T(8,128)S(1)} collective-permute-done((f32[256,256]{1,0:T(8,128)S(1)}, f32[256,256]{1,0:T(8,128)S(1)}, u32[]{:S(2)}, u32[]{:S(2)}) %collective-permute-start.1) | collective-permute-done | bytes 262176 | tf_op jit(solution)/shard_map/ppermute | solution.py:15
  75.5 2.0 fusion.24
  77.4 1.9 collective-permute-start.2
  79.4 19.3 %collective-permute-done.2 = f32[256,512]{1,0:T(8,128)S(1)} collective-permute-done((f32[256,512]{1,0:T(8,128)}, f32[256,512]{1,0:T(8,128)S(1)}, u32[]{:S(2)}, u32[]{:S(2)}) %collective-permute-start.2) | collective-permute-done | bytes 524320 | tf_op jit(solution)/shard_map/ppermute | solution.py:15
  98.7 1.9 collective-permute-start.3
  100.6 7.8 %collective-permute-start.4 = (f32[256,512]{1,0:T(8,128)S(1)}, f32[256,512]{1,0:T(8,128)S(1)}, u32[]{:S(2)}, u32[]{:S(2)}) collective-permute-start(f32[256,512]{1,0:T(8,128)S(1)} %collective-permute-done.2), channel_id=1, source_target_pairs={{0,496},{16,0},{32,16},{48,32},{64,48},{80,64},{96,80},{112,96},{1... | collective-permute-start | bytes 1572872 | tf_op jit(solution)/shard_map/ppermute | solution.py:30
  108.4 12.6 %collective-permute-done.3 = f32[256,512]{1,0:T(8,128)S(1)} collective-permute-done((f32[256,512]{1,0:T(8,128)S(1)}, f32[256,512]{1,0:T(8,128)S(1)}, u32[]{:S(2)}, u32[]{:S(2)}) %collective-permute-start.3) | collective-permute-done | bytes 524320 | tf_op jit(solution)/shard_map/ppermute | solution.py:30
  121.1 1.9 collective-permute-start.5
  123.0 7.8 %collective-permute-start.6 = (f32[256,512]{1,0:T(8,128)S(1)}, f32[256,512]{1,0:T(8,128)S(1)}, u32[]{:S(2)}, u32[]{:S(2)}) collective-permute-start(f32[256,512]{1,0:T(8,128)S(1)} %collective-permute-done.4), channel_id=1, source_target_pairs={{0,496},{16,0},{32,16},{48,32},{64,48},{80,64},{96,80},{112,96},{1... | collective-permute-start | bytes 1572872 | tf_op jit(solution)/shard_map/ppermute | solution.py:30
  130.9 6.5 %collective-permute-done.5 = f32[256,512]{1,0:T(8,128)S(1)} collective-permute-done((f32[256,512]{1,0:T(8,128)S(1)}, f32[256,512]{1,0:T(8,128)S(1)}, u32[]{:S(2)}, u32[]{:S(2)}) %collective-permute-start.5) | collective-permute-done | bytes 524320 | tf_op jit(solution)/shard_map/ppermute | solution.py:30
  137.4 1.9 collective-permute-start.7
  139.3 7.8 %collective-permute-start.8 = (f32[256,512]{1,0:T(8,128)S(1)}, f32[256,512]{1,0:T(8,128)S(1)}, u32[]{:S(2)}, u32[]{:S(2)}) collective-permute-start(f32[256,512]{1,0:T(8,128)S(1)} %collective-permute-done.6), channel_id=1, source_target_pairs={{0,496},{16,0},{32,16},{48,32},{64,48},{80,64},{96,80},{112,96},{1... | collective-permute-start | bytes 1572872 | tf_op jit(solution)/shard_map/ppermute | solution.py:30
  147.2 33.2 %collective-permute-done.7 = f32[256,512]{1,0:T(8,128)S(1)} collective-permute-done((f32[256,512]{1,0:T(8,128)S(1)}, f32[256,512]{1,0:T(8,128)S(1)}, u32[]{:S(2)}, u32[]{:S(2)}) %collective-permute-start.7) | collective-permute-done | bytes 524320 | tf_op jit(solution)/shard_map/ppermute | solution.py:30
  180.3 1.9 collective-permute-start.9
  182.3 2.3 collective-permute-done.8
  184.6 8.4 %collective-permute-start.10 = (f32[256,512]{1,0:T(8,128)S(1)}, f32[256,512]{1,0:T(8,128)}, u32[]{:S(2)}, u32[]{:S(2)}) collective-permute-start(f32[256,512]{1,0:T(8,128)S(1)} %collective-permute-done.8), channel_id=1, source_target_pairs={{0,496},{16,0},{32,16},{48,32},{64,48},{80,64},{96,80},{112,96},{1... | collective-permute-start | bytes 1572872 | tf_op jit(solution)/shard_map/ppermute | solution.py:30
  193.0 19.2 %collective-permute-done.9 = f32[256,512]{1,0:T(8,128)S(1)} collective-permute-done((f32[256,512]{1,0:T(8,128)S(1)}, f32[256,512]{1,0:T(8,128)S(1)}, u32[]{:S(2)}, u32[]{:S(2)}) %collective-permute-start.9) | collective-permute-done | bytes 524320 | tf_op jit(solution)/shard_map/ppermute | solution.py:30
  212.1 1.9 collective-permute-start.11
  214.0 7.8 %collective-permute-start.12 = (f32[256,512]{1,0:T(8,128)}, f32[256,512]{1,0:T(8,128)}, u32[]{:S(2)}, u32[]{:S(2)}) collective-permute-start(f32[256,512]{1,0:T(8,128)} %collective-permute-done.10), channel_id=1, source_target_pairs={{0,496},{16,0},{32,16},{48,32},{64,48},{80,64},{96,80},{112,96},{1... | collective-permute-start | bytes 1572872 | tf_op jit(solution)/shard_map/ppermute | solution.py:30
  221.9 9.3 %collective-permute-done.11 = f32[256,512]{1,0:T(8,128)} collective-permute-done((f32[256,512]{1,0:T(8,128)S(1)}, f32[256,512]{1,0:T(8,128)}, u32[]{:S(2)}, u32[]{:S(2)}) %collective-permute-start.11) | collective-permute-done | bytes 524320 | tf_op jit(solution)/shard_map/ppermute | solution.py:30
  231.2 1.9 collective-permute-start.13
  233.3 7.8 %collective-permute-start.14 = (f32[256,512]{1,0:T(8,128)}, f32[256,512]{1,0:T(8,128)}, u32[]{:S(2)}, u32[]{:S(2)}) collective-permute-start(f32[256,512]{1,0:T(8,128)} %collective-permute-done.12), channel_id=1, source_target_pairs={{0,496},{16,0},{32,16},{48,32},{64,48},{80,64},{96,80},{112,96},{1... | collective-permute-start | bytes 1572872 | tf_op jit(solution)/shard_map/ppermute | solution.py:30
  241.2 10.5 %collective-permute-done.13 = f32[256,512]{1,0:T(8,128)} collective-permute-done((f32[256,512]{1,0:T(8,128)}, f32[256,512]{1,0:T(8,128)}, u32[]{:S(2)}, u32[]{:S(2)}) %collective-permute-start.13) | collective-permute-done | bytes 524320 | tf_op jit(solution)/shard_map/ppermute | solution.py:30
  251.7 1.9 collective-permute-start.15
  253.7 2.3 constant_dynamic-slice_fusion.1
  255.9 2.3 fusion
  261.4 2.3 convolution_add_fusion.2
  263.7 2.3 convolution_add_fusion.1
  267.0 3.1 %convolution_add_fusion = f32[256,512]{1,0:T(8,128)} fusion(f32[256,512]{1,0:T(8,128)S(1)} %convolution_add_fusion.1, f32[256,512]{1,0:T(8,128)} %collective-permute-done.15, f32[256,512]{1,0:T(8,128)} %collective-permute-done.14, f32[256,256]{1,0:T(8,128)S(1)} %get-tuple-element.6, f32[256,256]{1,0:T(8,128)S(1)} %get-tuple-element.5), kind=kOutput, calls=%fused_computation | convolution fusion | flops 805830656 | bytes 2621440 | tf_op jit(solution)/shard_map/dot_general | solution.py:111
  (31 shorter events, 9.0 us)
Async XLA Ops:
  6.5 247.1 %all-gather.2.cloned.1.call-start = ((), (), s32[]{:S(2)}) async-start(), calls=%async_computation | async-start | bytes 8912896 | tf_op jit(solution)/shard_map/all_gather | solution.py:88
  9.4 56.7 %collective-permute-start = (f32[256,256]{1,0:T(8,128)S(1)}, f32[256,256]{1,0:T(8,128)S(1)}, u32[]{:S(2)}, u32[]{:S(2)}) collective-permute-start(f32[256,256]{1,0:T(8,128)S(1)} %get-tuple-element.19), channel_id=1, source_target_pairs={{0,0},{1,32},{2,64},{3,96},{4,128},{5,160},{6,192},{7,224},{8,256}... | collective-permute-start | bytes 786440 | tf_op jit(solution)/shard_map/ppermute | solution.py:15
  20.1 55.3 %collective-permute-start.1 = (f32[256,256]{1,0:T(8,128)S(1)}, f32[256,256]{1,0:T(8,128)S(1)}, u32[]{:S(2)}, u32[]{:S(2)}) collective-permute-start(f32[256,256]{1,0:T(8,128)S(1)} %get-tuple-element.20), channel_id=1, source_target_pairs={{0,16},{1,48},{2,80},{3,112},{4,144},{5,176},{6,208},{7,240},{8,27... | collective-permute-start | bytes 786440 | tf_op jit(solution)/shard_map/ppermute | solution.py:15
  77.4 21.2 %collective-permute-start.2 = (f32[256,512]{1,0:T(8,128)}, f32[256,512]{1,0:T(8,128)S(1)}, u32[]{:S(2)}, u32[]{:S(2)}) collective-permute-start(f32[256,512]{1,0:T(8,128)} %fusion.24), channel_id=1, source_target_pairs={{0,400},{1,369},{2,338},{3,307},{4,276},{5,245},{6,214},{7,183},{8... | collective-permute-start | bytes 1572872 | tf_op jit(solution)/shard_map/ppermute | solution.py:15
  98.7 24.3 %copy-start = (f32[256,512]{1,0:T(8,128)}, f32[256,512]{1,0:T(8,128)S(1)}, u32[]{:S(2)}) copy-start(f32[256,512]{1,0:T(8,128)S(1)} %collective-permute-done.2) | copy-start | bytes 1572868
  98.7 22.4 %collective-permute-start.3 = (f32[256,512]{1,0:T(8,128)S(1)}, f32[256,512]{1,0:T(8,128)S(1)}, u32[]{:S(2)}, u32[]{:S(2)}) collective-permute-start(f32[256,512]{1,0:T(8,128)S(1)} %collective-permute-done.2), channel_id=1, source_target_pairs={{0,16},{16,32},{32,48},{48,64},{64,80},{80,96},{96,112},{112,128},... | collective-permute-start | bytes 1572872 | tf_op jit(solution)/shard_map/ppermute | solution.py:30
  100.6 22.4 %collective-permute-start.4 = (f32[256,512]{1,0:T(8,128)S(1)}, f32[256,512]{1,0:T(8,128)S(1)}, u32[]{:S(2)}, u32[]{:S(2)}) collective-permute-start(f32[256,512]{1,0:T(8,128)S(1)} %collective-permute-done.2), channel_id=1, source_target_pairs={{0,496},{16,0},{32,16},{48,32},{64,48},{80,64},{96,80},{112,96},{1... | collective-permute-start | bytes 1572872 | tf_op jit(solution)/shard_map/ppermute | solution.py:30
  121.1 18.2 %copy-start.1 = (f32[256,512]{1,0:T(8,128)}, f32[256,512]{1,0:T(8,128)S(1)}, u32[]{:S(2)}) copy-start(f32[256,512]{1,0:T(8,128)S(1)} %collective-permute-done.3) | copy-start | bytes 1572868
  121.1 16.3 %collective-permute-start.5 = (f32[256,512]{1,0:T(8,128)S(1)}, f32[256,512]{1,0:T(8,128)S(1)}, u32[]{:S(2)}, u32[]{:S(2)}) collective-permute-start(f32[256,512]{1,0:T(8,128)S(1)} %collective-permute-done.3), channel_id=1, source_target_pairs={{0,16},{16,32},{32,48},{48,64},{64,80},{80,96},{96,112},{112,128},... | collective-permute-start | bytes 1572872 | tf_op jit(solution)/shard_map/ppermute | solution.py:30
  123.0 16.3 %collective-permute-start.6 = (f32[256,512]{1,0:T(8,128)S(1)}, f32[256,512]{1,0:T(8,128)S(1)}, u32[]{:S(2)}, u32[]{:S(2)}) collective-permute-start(f32[256,512]{1,0:T(8,128)S(1)} %collective-permute-done.4), channel_id=1, source_target_pairs={{0,496},{16,0},{32,16},{48,32},{64,48},{80,64},{96,80},{112,96},{1... | collective-permute-start | bytes 1572872 | tf_op jit(solution)/shard_map/ppermute | solution.py:30
  137.4 42.9 %collective-permute-start.7 = (f32[256,512]{1,0:T(8,128)S(1)}, f32[256,512]{1,0:T(8,128)S(1)}, u32[]{:S(2)}, u32[]{:S(2)}) collective-permute-start(f32[256,512]{1,0:T(8,128)S(1)} %collective-permute-done.5), channel_id=1, source_target_pairs={{0,16},{16,32},{32,48},{48,64},{64,80},{80,96},{96,112},{112,128},... | collective-permute-start | bytes 1572872 | tf_op jit(solution)/shard_map/ppermute | solution.py:30
  139.3 45.2 %collective-permute-start.8 = (f32[256,512]{1,0:T(8,128)S(1)}, f32[256,512]{1,0:T(8,128)S(1)}, u32[]{:S(2)}, u32[]{:S(2)}) collective-permute-start(f32[256,512]{1,0:T(8,128)S(1)} %collective-permute-done.6), channel_id=1, source_target_pairs={{0,496},{16,0},{32,16},{48,32},{64,48},{80,64},{96,80},{112,96},{1... | collective-permute-start | bytes 1572872 | tf_op jit(solution)/shard_map/ppermute | solution.py:30
  180.3 31.8 %collective-permute-start.9 = (f32[256,512]{1,0:T(8,128)S(1)}, f32[256,512]{1,0:T(8,128)S(1)}, u32[]{:S(2)}, u32[]{:S(2)}) collective-permute-start(f32[256,512]{1,0:T(8,128)S(1)} %collective-permute-done.7), channel_id=1, source_target_pairs={{0,16},{16,32},{32,48},{48,64},{64,80},{80,96},{96,112},{112,128},... | collective-permute-start | bytes 1572872 | tf_op jit(solution)/shard_map/ppermute | solution.py:30
  184.6 29.5 %collective-permute-start.10 = (f32[256,512]{1,0:T(8,128)S(1)}, f32[256,512]{1,0:T(8,128)}, u32[]{:S(2)}, u32[]{:S(2)}) collective-permute-start(f32[256,512]{1,0:T(8,128)S(1)} %collective-permute-done.8), channel_id=1, source_target_pairs={{0,496},{16,0},{32,16},{48,32},{64,48},{80,64},{96,80},{112,96},{1... | collective-permute-start | bytes 1572872 | tf_op jit(solution)/shard_map/ppermute | solution.py:30
  212.1 19.1 %collective-permute-start.11 = (f32[256,512]{1,0:T(8,128)S(1)}, f32[256,512]{1,0:T(8,128)}, u32[]{:S(2)}, u32[]{:S(2)}) collective-permute-start(f32[256,512]{1,0:T(8,128)S(1)} %collective-permute-done.9), channel_id=1, source_target_pairs={{0,16},{16,32},{32,48},{48,64},{64,80},{80,96},{96,112},{112,128},... | collective-permute-start | bytes 1572872 | tf_op jit(solution)/shard_map/ppermute | solution.py:30
  214.0 19.3 %collective-permute-start.12 = (f32[256,512]{1,0:T(8,128)}, f32[256,512]{1,0:T(8,128)}, u32[]{:S(2)}, u32[]{:S(2)}) collective-permute-start(f32[256,512]{1,0:T(8,128)} %collective-permute-done.10), channel_id=1, source_target_pairs={{0,496},{16,0},{32,16},{48,32},{64,48},{80,64},{96,80},{112,96},{1... | collective-permute-start | bytes 1572872 | tf_op jit(solution)/shard_map/ppermute | solution.py:30
  231.2 20.5 %collective-permute-start.13 = (f32[256,512]{1,0:T(8,128)}, f32[256,512]{1,0:T(8,128)}, u32[]{:S(2)}, u32[]{:S(2)}) collective-permute-start(f32[256,512]{1,0:T(8,128)} %collective-permute-done.11), channel_id=1, source_target_pairs={{0,16},{16,32},{32,48},{48,64},{64,80},{80,96},{96,112},{112,128},... | collective-permute-start | bytes 1572872 | tf_op jit(solution)/shard_map/ppermute | solution.py:30
  233.3 32.6 %collective-permute-start.14 = (f32[256,512]{1,0:T(8,128)}, f32[256,512]{1,0:T(8,128)}, u32[]{:S(2)}, u32[]{:S(2)}) collective-permute-start(f32[256,512]{1,0:T(8,128)} %collective-permute-done.12), channel_id=1, source_target_pairs={{0,496},{16,0},{32,16},{48,32},{64,48},{80,64},{96,80},{112,96},{1... | collective-permute-start | bytes 1572872 | tf_op jit(solution)/shard_map/ppermute | solution.py:30
  251.7 15.3 %collective-permute-start.15 = (f32[256,512]{1,0:T(8,128)}, f32[256,512]{1,0:T(8,128)}, u32[]{:S(2)}, u32[]{:S(2)}) collective-permute-start(f32[256,512]{1,0:T(8,128)} %collective-permute-done.13), channel_id=1, source_target_pairs={{0,16},{16,32},{32,48},{48,64},{64,80},{80,96},{96,112},{112,128},... | collective-permute-start | bytes 1572872 | tf_op jit(solution)/shard_map/ppermute | solution.py:30
Sparse Core Ops, SparseCore 0:
  77.6 137.1 all-gather.1
